TPU v7x, 32 devices: a whole 2x2x4 slice. The times are simulated.
32 devices in a mesh: dp: 4 (over y, x), expert: 8 (over z, core).
Axes of the slice: x: 2, y: 2, z: 4, core: 2. Of those that a mesh axis runs over, the one named last changes fastest.
Arguments:
- tokens: bfloat16 [4096, 4096], P(('dp', 'expert')), may hold values from -6 to 6
- expert_ids: int32 [4096, 2], P(('dp', 'expert')), may hold values from 0 to 7, all different within a row; in each aligned block of 128 rows (0 to 127, 128 to 255, ...) at most 64 rows name the same one
- combine: float32 [4096, 2], P(('dp', 'expert')), may hold values from 0.2 to 1
- weight_gate: bfloat16 [8, 768, 4096], P('expert'), may hold values from -0.09375 to 0.09375
- weight_up: bfloat16 [8, 768, 4096], P('expert'), may hold values from -0.09375 to 0.09375
- weight_down: bfloat16 [8, 768, 4096], P('expert'), may hold values from -0.21875 to 0.21875
- grad_out: bfloat16 [4096, 4096], P(('dp', 'expert')), may hold values from -6 to 6
Outputs:
- mixed: bfloat16 [4096, 4096], P(('dp', 'expert'))
- grad_tokens: bfloat16 [4096, 4096], P(('dp', 'expert'))
- grad_combine: float32 [4096, 2], P(('dp', 'expert'))
- grad_gate: bfloat16 [8, 768, 4096], P('expert', 'dp')
- grad_up: bfloat16 [8, 768, 4096], P('expert', 'dp')
- grad_down: bfloat16 [8, 768, 4096], P('expert', 'dp')
Inputs may be any that keep to these rules, and one draw needn't show every extreme that they name: `expert_ids`: each row names 2 different experts. In the rows of one device no expert is named more than 64 times, a bound that some block reaches.
All inputs are finite; a program needn't handle non-finite values.
Results may differ from a plain program's by a relative error of at most 0.012.
Values may be sent and summed in bfloat16 or wider, within the bound.
No kernel may reach another device: no remote copies, remote signals or barrier semaphores. Data moves between devices by JAX's collectives and lax.ppermute only.
A program may use at most 192 MiB of HBM per device.

v0:
```python
import jax
import jax.numpy as jnp
from jax import lax
from jax.sharding import PartitionSpec as P


def slot_table(expert_ids, experts, capacity):
    tok_count, top_count = expert_ids.shape
    pair_total = tok_count * top_count
    flat_ids = expert_ids.reshape(pair_total)
    onehot = (flat_ids[:, None] == jnp.arange(experts, dtype=jnp.int32)[None, :]).astype(jnp.int32)
    earlier = jnp.cumsum(onehot, axis=0) - onehot
    position = jnp.sum(earlier * onehot, axis=1)
    target = flat_ids * capacity + position
    table = jnp.full((experts * capacity,), pair_total, jnp.int32)
    table = table.at[target].set(jnp.arange(pair_total, dtype=jnp.int32))
    return (target, table)


def per_device(tokens, expert_ids, combine, weight_gate, weight_up, weight_down, grad_out):
    tok_count, top_count = expert_ids.shape
    model_width = tokens.shape[1]
    experts = lax.axis_size("expert")
    copies = lax.axis_size("dp")
    capacity = 2 * tok_count * top_count // experts
    pair_total = tok_count * top_count
    target, table = slot_table(expert_ids, experts, capacity)
    valid = table < pair_total
    pair_safe = jnp.minimum(table, pair_total - 1)
    token_row = pair_safe // top_count
    weight_pair = jnp.where(
        valid, combine.reshape(pair_total)[pair_safe], jnp.zeros((), jnp.float32)
    )
    send_rows = jnp.where(valid[:, None], tokens[token_row], jnp.zeros((), tokens.dtype))
    send_grads = (weight_pair[:, None] * grad_out[token_row].astype(jnp.float32)).astype(
        jnp.bfloat16
    )
    send_rows = send_rows.reshape(experts, capacity, model_width)
    send_grads = send_grads.reshape(experts, capacity, model_width)
    recv_rows, recv_grads = (
        lax.all_to_all(send_rows, "expert", split_axis=0, concat_axis=0, tiled=True),
        lax.all_to_all(send_grads, "expert", split_axis=0, concat_axis=0, tiled=True),
    )
    in_rows = recv_rows.reshape(experts * capacity, model_width)
    out_grads = recv_grads.reshape(experts * capacity, model_width)
    w_gate = weight_gate[0]
    w_up = weight_up[0]
    w_down = weight_down[0]
    gate_pre = jnp.dot(in_rows, w_gate.T, preferred_element_type=jnp.float32)
    up_pre = jnp.dot(in_rows, w_up.T, preferred_element_type=jnp.float32)
    sigmoid_gate = jax.nn.sigmoid(gate_pre)
    activated = (gate_pre * sigmoid_gate * up_pre).astype(jnp.bfloat16)
    expert_out = jnp.dot(activated, w_down, preferred_element_type=jnp.float32).astype(jnp.bfloat16)
    expert_out = expert_out.reshape(experts, capacity, model_width)
    scale = (tok_count * top_count * copies) ** (-0.5)
    grad_act = jnp.dot(out_grads, w_down.T, preferred_element_type=jnp.float32)
    grad_gate_pre = (
        grad_act * up_pre * sigmoid_gate * (1.0 + gate_pre * (1.0 - sigmoid_gate))
    ).astype(jnp.bfloat16)
    grad_up_pre = (grad_act * gate_pre * sigmoid_gate).astype(jnp.bfloat16)
    row_grads = (
        jnp.dot(grad_gate_pre, w_gate, preferred_element_type=jnp.float32)
        + jnp.dot(grad_up_pre, w_up, preferred_element_type=jnp.float32)
    ).astype(jnp.bfloat16)
    row_grads = row_grads.reshape(experts, capacity, model_width)
    gate_term = scale * jnp.einsum(
        "rf,rd->fd", grad_gate_pre, in_rows, preferred_element_type=jnp.float32
    )
    up_term = scale * jnp.einsum(
        "rf,rd->fd", grad_up_pre, in_rows, preferred_element_type=jnp.float32
    )
    all_share = lax.psum_scatter(
        jnp.concatenate(
            [
                jnp.concatenate([gate_term, up_term], axis=1),
                scale
                * jnp.einsum("rf,rd->fd", activated, out_grads, preferred_element_type=jnp.float32),
            ],
            axis=1,
        ).astype(jnp.bfloat16),
        "dp",
        scatter_dimension=0,
        tiled=True,
    ).astype(jnp.float32)
    gate_share = all_share[:, :model_width]
    up_share = all_share[:, model_width : 2 * model_width]
    down_share = all_share[:, 2 * model_width :]
    back_out, back_grads = (
        lax.all_to_all(expert_out, "expert", split_axis=0, concat_axis=0, tiled=True),
        lax.all_to_all(row_grads, "expert", split_axis=0, concat_axis=0, tiled=True),
    )
    picked_out = back_out.reshape(experts * capacity, model_width)[target].astype(jnp.float32)
    picked_out = picked_out.reshape(tok_count, top_count, model_width)
    picked_grads = back_grads.reshape(experts * capacity, model_width)[target].astype(jnp.float32)
    picked_grads = picked_grads.reshape(tok_count, top_count, model_width)
    mixed = jnp.sum(combine[:, :, None] * picked_out, axis=1).astype(jnp.bfloat16)
    grad_tokens = jnp.sum(picked_grads, axis=1).astype(jnp.bfloat16)
    grad_combine = jnp.sum(grad_out.astype(jnp.float32)[:, None, :] * picked_out, axis=2)
    grad_gate = gate_share.astype(jnp.bfloat16)[None]
    grad_up = up_share.astype(jnp.bfloat16)[None]
    grad_down = down_share.astype(jnp.bfloat16)[None]
    return (mixed, grad_tokens, grad_combine, grad_gate, grad_up, grad_down)


def solution(mesh):
    in_specs = (
        P(("dp", "expert"), None),
        P(("dp", "expert"), None),
        P(("dp", "expert"), None),
        P("expert", None, None),
        P("expert", None, None),
        P("expert", None, None),
        P(("dp", "expert"), None),
    )
    out_specs = (
        P(("dp", "expert"), None),
        P(("dp", "expert"), None),
        P(("dp", "expert"), None),
        P("expert", "dp", None),
        P("expert", "dp", None),
        P("expert", "dp", None),
    )
    return jax.shard_map(
        per_device, mesh=mesh, in_specs=in_specs, out_specs=out_specs, check_vma=False
    )
```

profile of v0, /device:TPU:0, one launch (start us, length us, event | category | flops | bytes accessed | tf_op | source)
XLA Modules:
  0.0 535.6 jit_solution(16978454798665837195)
XLA Ops:
  10.3 1.4 scatter_custom_fusion
  12.7 3.5 gather_fusion.2
  16.3 4.3 gather_fusion.3
  20.6 5.6 %fusion = bf16[8,64,4096]{2,1,0:T(8,128)(2,1)} fusion(bf16[8,64,4096]{2,1,0:T(8,128)(2,1)} %bitcast.59, f32[8,64]{1,0:T(8,128)S(1)} %mul.91), kind=kLoop, calls=%fused_computation.11 | loop fusion | flops 6291456 | bytes 8390656 | tf_op jit(solution)/shard_map/convert_element_type | solution.py:35
  26.2 6.3 %all-to-all-start.2 = ((bf16[8,64,4096]{2,1,0:T(8,128)(2,1)}), bf16[8,64,4096]{2,1,0:T(8,128)(2,1)}, u32[]{:S(2)}, u32[]{:S(2)}) async-start(bf16[8,64,4096]{2,1,0:T(8,128)(2,1)} %fusion), calls=%async_computation.2 | async-start | bytes 8388608 | tf_op jit(solution)/shard_map/all_to_all | solution.py:42
  32.6 4.4 gather_fusion
  37.0 4.5 broadcast_select_fusion
  41.5 85.1 %all-to-all-done.2 = bf16[8,64,4096]{2,1,0:T(8,128)(2,1)} async-done(((bf16[8,64,4096]{2,1,0:T(8,128)(2,1)}), bf16[8,64,4096]{2,1,0:T(8,128)(2,1)}, u32[]{:S(2)}, u32[]{:S(2)}) %all-to-all-start.2) | async-done | bytes 4194336 | tf_op jit(solution)/shard_map/all_to_all | solution.py:42
  126.7 4.5 all-to-all-start
  131.3 8.7 %fusion.1 = f32[512,768]{1,0:T(8,128)} fusion(bf16[512,4096]{1,0:T(8,128)(2,1)} %bitcast.12, bf16[1,768,4096]{2,1,0:T(8,128)(2,1)} %param.12), kind=kOutput, calls=%fused_computation.13 | convolution fusion | flops 3221225472 | bytes 12058624 | tf_op jit(solution)/shard_map/dot_general | solution.py:56
  139.9 85.3 %all-to-all-done = bf16[8,64,4096]{2,1,0:T(8,128)(2,1)} async-done(((bf16[8,64,4096]{2,1,0:T(8,128)(2,1)}), bf16[8,64,4096]{2,1,0:T(8,128)(2,1)}, u32[]{:S(2)}, u32[]{:S(2)}) %all-to-all-start) | async-done | bytes 4194336 | tf_op jit(solution)/shard_map/all_to_all | solution.py:41
  225.2 7.5 %fusion.7 = f32[512,768]{1,0:T(8,128)S(1)} fusion(bf16[512,4096]{1,0:T(8,128)(2,1)} %bitcast.5, bf16[1,768,4096]{2,1,0:T(8,128)(2,1)} %param.11), kind=kOutput, calls=%fused_computation.19 | convolution fusion | flops 3221225472 | bytes 12058624 | tf_op jit(solution)/shard_map/dot_general | solution.py:50
  232.7 8.1 %multiply_convert_fusion.4 = (bf16[512,768]{1,0:T(8,128)(2,1)S(1)}, bf16[512,768]{1,0:T(8,128)(2,1)S(1)}, bf16[512,768]{1,0:T(8,128)(2,1)S(1)}) fusion(f32[512,768]{1,0:T(8,128)S(1)} %copy-done.5, f32[512,768]{1,0:T(8,128)S(1)} %fusion.7, bf16[512,4096]{1,0:T(8,128)(2,1)} %bitcast.5, bf16[1,768,4096]{2,1,0:T(8,128)(2,1)} %param.10), kind=kOutput, calls=%fused_computation.33 | convolution fusion | flops 3227516928 | bytes 15990784 | tf_op jit(solution)/shard_map/dot_general | solution.py:49
  240.8 6.2 %multiply_convert_fusion = bf16[768,4096]{1,0:T(8,128)(2,1)S(1)} fusion(bf16[512,768]{1,0:T(8,128)(2,1)S(1)} %get-tuple-element.20, bf16[512,4096]{1,0:T(8,128)(2,1)} %bitcast.12), kind=kOutput, calls=%fused_computation.7 | convolution fusion | flops 3227516928 | bytes 11272192 | tf_op jit(solution)/shard_map/rf,rd->fd/dot_general | solution.py:77
  247.1 5.9 %multiply_convert_fusion.1 = bf16[768,4096]{1,0:T(8,128)(2,1)S(1)} fusion(bf16[512,768]{1,0:T(8,128)(2,1)S(1)} %get-tuple-element.21, bf16[512,4096]{1,0:T(8,128)(2,1)} %bitcast.5), kind=kOutput, calls=%fused_computation.8 | convolution fusion | flops 3227516928 | bytes 11272192 | tf_op jit(solution)/shard_map/rf,rd->fd/dot_general | solution.py:69
  253.0 5.9 %multiply_convert_fusion.2 = bf16[768,4096]{1,0:T(8,128)(2,1)S(1)} fusion(bf16[512,768]{1,0:T(8,128)(2,1)S(1)} %get-tuple-element.19, bf16[512,4096]{1,0:T(8,128)(2,1)} %bitcast.5), kind=kOutput, calls=%fused_computation.9 | convolution fusion | flops 3227516928 | bytes 11272192 | tf_op jit(solution)/shard_map/rf,rd->fd/dot_general | solution.py:66
  258.9 27.9 %pad_maximum_fusion = bf16[768,12288]{1,0:T(8,128)(2,1)} fusion(bf16[768,4096]{1,0:T(8,128)(2,1)S(1)} %multiply_convert_fusion, bf16[768,4096]{1,0:T(8,128)(2,1)S(1)} %multiply_convert_fusion.1, bf16[768,4096]{1,0:T(8,128)(2,1)S(1)} %multiply_convert_fusion.2), kind=kLoop, calls=%fused_computation.6 | loop fusion | flops 56623104 | bytes 37748736 | tf_op jit(solution)/shard_map/concatenate | solution.py:73
  286.9 8.5 %fusion.13 = bf16[512,4096]{1,0:T(8,128)(2,1)} fusion(bf16[512,768]{1,0:T(8,128)(2,1)} %copy-done.4, bf16[1,768,4096]{2,1,0:T(8,128)(2,1)} %param.12), kind=kOutput, calls=%fused_computation.25 | convolution fusion | flops 3223322624 | bytes 11272192 | tf_op jit(solution)/shard_map/dot_general | solution.py:53
  295.4 4.6 all-to-all-start.1
  300.0 5.5 %fusion.5 = f32[512,4096]{1,0:T(8,128)S(1)} fusion(bf16[512,768]{1,0:T(8,128)(2,1)S(1)} %get-tuple-element.21, bf16[1,768,4096]{2,1,0:T(8,128)(2,1)} %param.11), kind=kOutput, calls=%fused_computation.17 | convolution fusion | flops 3221225472 | bytes 15466496 | tf_op jit(solution)/shard_map/dot_general | solution.py:63
  305.5 7.9 %add_convert_fusion = bf16[512,4096]{1,0:T(8,128)(2,1)} fusion(f32[512,4096]{1,0:T(8,128)S(1)} %fusion.5, bf16[512,768]{1,0:T(8,128)(2,1)S(1)} %get-tuple-element.19, bf16[1,768,4096]{2,1,0:T(8,128)(2,1)} %param.10), kind=kOutput, calls=%fused_computation.12 | convolution fusion | flops 3225419776 | bytes 19660800 | tf_op jit(solution)/shard_map/dot_general | solution.py:62
  313.4 80.5 %all-to-all-done.1 = bf16[8,64,4096]{2,1,0:T(8,128)(2,1)} async-done(((bf16[8,64,4096]{2,1,0:T(8,128)(2,1)}), bf16[8,64,4096]{2,1,0:T(8,128)(2,1)}, u32[]{:S(2)}, u32[]{:S(2)}) %all-to-all-start.1) | async-done | bytes 4194336 | tf_op jit(solution)/shard_map/all_to_all | solution.py:89
  394.0 4.6 all-to-all-start.3
  398.5 1.6 convert_element_type.71
  400.1 6.6 %gather_fusion.1 = bf16[256,4096]{1,0:T(8,128)(2,1)S(1)} fusion(bf16[512,4096]{1,0:T(8,128)(2,1)} %bitcast.10, s32[1024]{0:T(1024)S(1)} %pad_clamp_fusion.1), kind=kCustom, calls=%fused_computation.1 | custom fusion | bytes 4195328 | tf_op jit(solution)/shard_map/gather | solution.py:92
  406.7 4.1 reshape.123
  410.8 81.7 %all-to-all-done.3 = bf16[8,64,4096]{2,1,0:T(8,128)(2,1)} async-done(((bf16[8,64,4096]{2,1,0:T(8,128)(2,1)}), bf16[8,64,4096]{2,1,0:T(8,128)(2,1)}, u32[]{:S(2)}, u32[]{:S(2)}) %all-to-all-start.3) | async-done | bytes 4194336 | tf_op jit(solution)/shard_map/all_to_all | solution.py:90
  492.6 7.9 %gather_fusion.4 = bf16[256,4096]{1,0:T(8,128)(2,1)} fusion(bf16[512,4096]{1,0:T(8,128)(2,1)} %bitcast.14, s32[1024]{0:T(1024)S(1)} %pad_clamp_fusion.1), kind=kCustom, calls=%fused_computation.4 | custom fusion | bytes 4195328 | tf_op jit(solution)/shard_map/gather | solution.py:94
  500.5 4.6 gather.25
  505.1 10.3 %multiply_reduce_fusion = (f32[128,2]{1,0:T(8,128)S(1)}, bf16[128,4096]{1,0:T(8,128)(2,1)}) fusion(f32[128,2,4096]{2,1,0:T(2,128)} %reshape.123, f32[128,4096]{1,0:T(8,128)S(1)} %copy-done.3, f32[128,2]{1,0:T(8,128)S(1)} %copy.19), kind=kLoop, calls=%fused_computation.26 | loop fusion | flops 3669760 | bytes 7342080 | tf_op jit(solution)/shard_map/reduce_sum | solution.py:98
  516.0 7.8 %reduce_sum.44 = bf16[128,4096]{1,0:T(8,128)(2,1)} reduce(bf16[128,2,4096]{2,1,0:T(2,128)(2,1)} %gather.25, bf16[]{:T(256)} %constant.36.clone.1), dimensions={1}, to_apply=%region_5.6 | reduce | flops 524288 | bytes 3145730 | tf_op jit(solution)/shard_map/reduce_sum | solution.py:97
  523.8 4.7 slice_bitcast_fusion
  (38 shorter events, 4.9 us)
Async XLA Ops:
  7.2 25.4 %copy-start = (bf16[128,4096]{1,0:T(8,128)(2,1)S(1)}, bf16[128,4096]{1,0:T(8,128)(2,1)}, u32[]{:S(2)}) copy-start(bf16[128,4096]{1,0:T(8,128)(2,1)} %param.7) | copy-start | bytes 3145732
  7.2 9.1 %copy-start.2 = (bf16[128,4096]{1,0:T(8,128)(2,1)S(1)}, bf16[128,4096]{1,0:T(8,128)(2,1)}, u32[]{:S(2)}) copy-start(bf16[128,4096]{1,0:T(8,128)(2,1)} %param.13) | copy-start | bytes 3145732
  26.2 100.4 %all-to-all-start.2 = ((bf16[8,64,4096]{2,1,0:T(8,128)(2,1)}), bf16[8,64,4096]{2,1,0:T(8,128)(2,1)}, u32[]{:S(2)}, u32[]{:S(2)}) async-start(bf16[8,64,4096]{2,1,0:T(8,128)(2,1)} %fusion), calls=%async_computation.2 | async-start | bytes 8388608 | tf_op jit(solution)/shard_map/all_to_all | solution.py:42
  126.7 98.6 %all-to-all-start = ((bf16[8,64,4096]{2,1,0:T(8,128)(2,1)}), bf16[8,64,4096]{2,1,0:T(8,128)(2,1)}, u32[]{:S(2)}, u32[]{:S(2)}) async-start(bf16[8,64,4096]{2,1,0:T(8,128)(2,1)} %broadcast_select_fusion), calls=%async_computation | async-start | bytes 8388608 | tf_op jit(solution)/shard_map/all_to_all | solution.py:41
  131.2 392.6 %reduce-scatter.2.cloned.1.call-start = ((), (), s32[]{:S(2)}) async-start(), calls=%async_computation.5 | async-start | bytes 23592960 | tf_op jit(solution)/shard_map/reduce_scatter | solution.py:72
  225.2 7.5 %copy-start.5 = (f32[512,768]{1,0:T(8,128)S(1)}, f32[512,768]{1,0:T(8,128)}, u32[]{:S(2)}) copy-start(f32[512,768]{1,0:T(8,128)} %fusion.1) | copy-start | bytes 4718596
  240.8 6.2 %copy-start.4 = (bf16[512,768]{1,0:T(8,128)(2,1)}, bf16[512,768]{1,0:T(8,128)(2,1)S(1)}, u32[]{:S(2)}) copy-start(bf16[512,768]{1,0:T(8,128)(2,1)S(1)} %get-tuple-element.20) | copy-start | bytes 2359300
  295.4 98.6 %all-to-all-start.1 = ((bf16[8,64,4096]{2,1,0:T(8,128)(2,1)}), bf16[8,64,4096]{2,1,0:T(8,128)(2,1)}, u32[]{:S(2)}, u32[]{:S(2)}) async-start(bf16[8,64,4096]{2,1,0:T(8,128)(2,1)} %bitcast.61), calls=%async_computation.1 | async-start | bytes 8388608 | tf_op jit(solution)/shard_map/all_to_all | solution.py:89
  394.0 98.6 %all-to-all-start.3 = ((bf16[8,64,4096]{2,1,0:T(8,128)(2,1)}), bf16[8,64,4096]{2,1,0:T(8,128)(2,1)}, u32[]{:S(2)}, u32[]{:S(2)}) async-start(bf16[8,64,4096]{2,1,0:T(8,128)(2,1)} %bitcast.60), calls=%async_computation.3 | async-start | bytes 8388608 | tf_op jit(solution)/shard_map/all_to_all | solution.py:90
  500.5 4.6 copy-start.3
  516.0 12.4 %copy-start.1 = (bf16[128,4096]{1,0:T(8,128)(2,1)S(1)}, bf16[128,4096]{1,0:T(8,128)(2,1)}, u32[]{:S(2)}) copy-start(bf16[128,4096]{1,0:T(8,128)(2,1)} %param.7) | copy-start | bytes 3145732
Sparse Core Ops, SparseCore 0:
  287.0 169.7 reduce-scatter.1
where the time goes:
time: 538 us; the launch traced here: 536 us
  waiting for transfers between devices  333 us (62%)
  matrix products  64.3 us (12%)
  other arithmetic  59.2 us (11%)
  local copies, waits for them, and re-layouts  44.8 us (8%)
  starting transfers between devices  20.1 us (4%)
  between operations  14.5 us (3%)
    all_to_all x1, waiting for transfers between devices, per_device(): lax.all_to_all(send_rows, 'expert', split_axis=0, concat_axis=0, tiled=True)  85.3 us
    all_to_all x1, waiting for transfers between devices, per_device(): lax.all_to_all(send_grads, 'expert', split_axis=0, concat_axis=0, tiled=T...  85.1 us
    all_to_all x1, waiting for transfers between devices, per_device(): lax.all_to_all(row_grads, 'expert', split_axis=0, concat_axis=0, tiled=True)  81.7 us
    all_to_all x1, waiting for transfers between devices, per_device(): lax.all_to_all(expert_out, 'expert', split_axis=0, concat_axis=0, tiled=T...  80.5 us
    concatenate x1, other arithmetic, per_device(): jnp.concatenate([jnp.concatenate([gate_term, up_term], axis=1), scale * j...  27.9 us
    gather x2, local copies, waits for them, and re-layouts, per_device(): back_grads.reshape(experts * capacity, model_width)[target]  12.5 us
  transfers between devices with their start and end apart: 5, of which 4 were waited for; matrix products, arithmetic and copies ran while one was open for 16% of the time, Pallas kernels for 0%

commit v1 on v0

v1 whole, which is shorter than its diff:
```python
import jax
import jax.numpy as jnp
from jax import lax
from jax.sharding import PartitionSpec as P


def slot_targets(expert_ids, experts, capacity):
    tok_count, top_count = expert_ids.shape
    pair_total = tok_count * top_count
    flat_ids = expert_ids.reshape(pair_total)
    onehot = (flat_ids[:, None] == jnp.arange(experts, dtype=jnp.int32)[None, :]).astype(jnp.int32)
    earlier = jnp.cumsum(onehot, axis=0) - onehot
    position = jnp.sum(earlier * onehot, axis=1)
    return (flat_ids * capacity + position).reshape(tok_count, top_count)


def per_device(tokens, expert_ids, combine, weight_gate, weight_up, weight_down, grad_out):
    tok_count, top_count = expert_ids.shape
    model_width = tokens.shape[1]
    experts = lax.axis_size("expert")
    copies = lax.axis_size("dp")
    capacity = 2 * tok_count * top_count // experts
    slots = experts * capacity
    target = slot_targets(expert_ids, experts, capacity)
    slot_iota = jnp.arange(slots, dtype=jnp.int32)
    hit = target.T[:, :, None] == slot_iota[None, None, :]
    send_onehot = jnp.any(hit, axis=0).T.astype(jnp.bfloat16)
    weight_pair = jnp.sum(
        jnp.where(hit, combine.T[:, :, None], jnp.zeros((), jnp.float32)), axis=(0, 1)
    )
    with jax.named_scope("dispatch_rows"):
        send_rows = jnp.dot(send_onehot, tokens, preferred_element_type=jnp.float32).astype(
            jnp.bfloat16
        )
        send_go = jnp.dot(send_onehot, grad_out, preferred_element_type=jnp.float32)
        send_grads = (weight_pair[:, None] * send_go).astype(jnp.bfloat16)
    send_rows = send_rows.reshape(experts, capacity, model_width)
    send_grads = send_grads.reshape(experts, capacity, model_width)
    recv_rows = lax.all_to_all(send_rows, "expert", split_axis=0, concat_axis=0, tiled=True)
    recv_grads = lax.all_to_all(send_grads, "expert", split_axis=0, concat_axis=0, tiled=True)
    in_rows = recv_rows.reshape(slots, model_width)
    out_grads = recv_grads.reshape(slots, model_width)
    w_gate = weight_gate[0]
    w_up = weight_up[0]
    w_down = weight_down[0]
    gate_pre = jnp.dot(in_rows, w_gate.T, preferred_element_type=jnp.float32)
    up_pre = jnp.dot(in_rows, w_up.T, preferred_element_type=jnp.float32)
    sigmoid_gate = jax.nn.sigmoid(gate_pre)
    activated = (gate_pre * sigmoid_gate * up_pre).astype(jnp.bfloat16)
    expert_out = jnp.dot(activated, w_down, preferred_element_type=jnp.float32).astype(jnp.bfloat16)
    back_out = lax.all_to_all(
        expert_out.reshape(experts, capacity, model_width),
        "expert",
        split_axis=0,
        concat_axis=0,
        tiled=True,
    )
    scale = (tok_count * top_count * copies) ** (-0.5)
    grad_act = jnp.dot(out_grads, w_down.T, preferred_element_type=jnp.float32)
    grad_gate_pre = (
        grad_act * up_pre * sigmoid_gate * (1.0 + gate_pre * (1.0 - sigmoid_gate))
    ).astype(jnp.bfloat16)
    grad_up_pre = (grad_act * gate_pre * sigmoid_gate).astype(jnp.bfloat16)
    row_grads = (
        jnp.dot(grad_gate_pre, w_gate, preferred_element_type=jnp.float32)
        + jnp.dot(grad_up_pre, w_up, preferred_element_type=jnp.float32)
    ).astype(jnp.bfloat16)
    back_grads = lax.all_to_all(
        row_grads.reshape(experts, capacity, model_width),
        "expert",
        split_axis=0,
        concat_axis=0,
        tiled=True,
    )
    with jax.named_scope("weight_grads"):
        down_term = (
            scale * jnp.einsum("rf,rd->fd", activated, out_grads, preferred_element_type=jnp.float32)
        ).astype(jnp.bfloat16)
        gate_term = (
            scale * jnp.einsum("rf,rd->fd", grad_gate_pre, in_rows, preferred_element_type=jnp.float32)
        ).astype(jnp.bfloat16)
        up_term = (
            scale * jnp.einsum("rf,rd->fd", grad_up_pre, in_rows, preferred_element_type=jnp.float32)
        ).astype(jnp.bfloat16)
    down_share = lax.psum_scatter(down_term, "dp", scatter_dimension=0, tiled=True)
    gate_share = lax.psum_scatter(gate_term, "dp", scatter_dimension=0, tiled=True)
    up_share = lax.psum_scatter(up_term, "dp", scatter_dimension=0, tiled=True)
    pick_onehot = hit.reshape(top_count * tok_count, slots).astype(jnp.bfloat16)
    with jax.named_scope("combine_rows"):
        picked_out = jnp.dot(
            pick_onehot, back_out.reshape(slots, model_width), preferred_element_type=jnp.float32
        ).reshape(top_count, tok_count, model_width)
        grad_f32 = grad_out.astype(jnp.float32)
        mixed = combine[:, 0:1] * picked_out[0]
        for k in range(1, top_count):
            mixed = mixed + combine[:, k : k + 1] * picked_out[k]
        mixed = mixed.astype(jnp.bfloat16)
        grad_combine = jnp.stack(
            [jnp.sum(grad_f32 * picked_out[k], axis=1) for k in range(top_count)], axis=1
        )
        picked_grads = jnp.dot(
            pick_onehot, back_grads.reshape(slots, model_width), preferred_element_type=jnp.float32
        ).reshape(top_count, tok_count, model_width)
        grad_tokens = picked_grads[0]
        for k in range(1, top_count):
            grad_tokens = grad_tokens + picked_grads[k]
        grad_tokens = grad_tokens.astype(jnp.bfloat16)
    return (mixed, grad_tokens, grad_combine, gate_share[None], up_share[None], down_share[None])


def solution(mesh):
    in_specs = (
        P(("dp", "expert"), None),
        P(("dp", "expert"), None),
        P(("dp", "expert"), None),
        P("expert", None, None),
        P("expert", None, None),
        P("expert", None, None),
        P(("dp", "expert"), None),
    )
    out_specs = (
        P(("dp", "expert"), None),
        P(("dp", "expert"), None),
        P(("dp", "expert"), None),
        P("expert", "dp", None),
        P("expert", "dp", None),
        P("expert", "dp", None),
    )
    return jax.shard_map(
        per_device, mesh=mesh, in_specs=in_specs, out_specs=out_specs, check_vma=False
    )
```

time: 538 us -> 463 us (0.86)
  other arithmetic: 59.2 us -> 6.15 us
  local copies, waits for them, and re-layouts: 44.8 us -> 1.6 us
  matrix products: 64.3 us -> 83.5 us
    gather x6 -> x0, local copies, waits for them, and re-layouts: 31.4 us -> none  [the longest x2 12.5 us: per_device(): back_grads.reshape(experts * capacity, model_width)[target]]
    concatenate x1 -> x0, other arithmetic: 27.9 us -> none  [per_device(): jnp.concatenate([jnp.concatenate([gate_term, up_term], axis=1), scale * j...]
    reduce_sum x3, other arithmetic: 18.2 us -> 2.95 us  [the longest x1 2.03 us: per_device(): jnp.sum(grad_f32 * picked_out[k], axis=1)]
    dot_general x0 -> x4, matrix products: none -> 15 us  [the longest x1 4.45 us: per_device(): send_go = jnp.dot(send_onehot, grad_out, preferred_element_type=jnp.float32)]
    convert_element_type x3 -> x2, other arithmetic: 7.18 us -> 1.19 us  [the longest x1 1.19 us: per_device(): grad_tokens = grad_tokens.astype(jnp.bfloat16)]
    all_to_all x1, waiting for transfers between devices: 85.1 us -> 90.7 us  [per_device(): lax.all_to_all(send_grads, 'expert', split_axis=0, concat_axis=0, tiled=T...]
  transfers between devices with their start and end apart: 5 -> 7, of which waited for: 4 -> 4; matrix products, arithmetic and copies ran while one was open for 16% -> 13% of each run, Pallas kernels for 0% -> 0%
where the time goes in v1:
time: 463 us; the launch traced here: 462 us
  waiting for transfers between devices  336 us (73%)
  matrix products  83.5 us (18%)
  starting transfers between devices  20.8 us (4%)
  between operations  13.9 us (3%)
  other arithmetic  6.15 us (1%)
    all_to_all x1, waiting for transfers between devices, per_device(): lax.all_to_all(send_grads, 'expert', split_axis=0, concat_axis=0, tiled=T...  90.7 us
    all_to_all x1, waiting for transfers between devices, per_device(): lax.all_to_all(row_grads.reshape(experts, capacity, model_width), 'expert...  87.8 us
    all_to_all x1, waiting for transfers between devices, per_device(): lax.all_to_all(send_rows, 'expert', split_axis=0, concat_axis=0, tiled=True)  85.1 us
    all_to_all x1, waiting for transfers between devices, per_device(): lax.all_to_all(expert_out.reshape(experts, capacity, model_width), 'exper...  72.5 us
  transfers between devices with their start and end apart: 7, of which 4 were waited for; matrix products, arithmetic and copies ran while one was open for 13% of the time, Pallas kernels for 0%

profile of v1, /device:TPU:0, one launch (start us, length us, event | category | flops | bytes accessed | tf_op | source)
XLA Modules:
  0.0 462.1 jit_solution(15140624412198575515)
XLA Ops:
  7.2 0.9 copy.30
  8.3 0.6 reduce-window.6
  8.9 0.2 slice_reduce_fusion
  9.3 0.1 reduce_sum.39
  9.5 0.7 fusion.28
  10.3 0.8 select_reduce_fusion
  11.2 4.5 multiply_convert_fusion.3
  15.6 6.3 %all-to-all-start.2 = ((bf16[8,64,4096]{2,1,0:T(8,128)(2,1)}), bf16[8,64,4096]{2,1,0:T(8,128)(2,1)}, u32[]{:S(2)}, u32[]{:S(2)}) async-start(bf16[8,64,4096]{2,1,0:T(8,128)(2,1)} %bitcast.71), calls=%async_computation.2 | async-start | bytes 8388608 | tf_op jit(solution)/shard_map/all_to_all | solution.py:40
  21.9 3.4 convolution_convert_fusion
  25.3 90.7 %all-to-all-done.2 = bf16[8,64,4096]{2,1,0:T(8,128)(2,1)} async-done(((bf16[8,64,4096]{2,1,0:T(8,128)(2,1)}), bf16[8,64,4096]{2,1,0:T(8,128)(2,1)}, u32[]{:S(2)}, u32[]{:S(2)}) %all-to-all-start.2) | async-done | bytes 4194336 | tf_op jit(solution)/shard_map/all_to_all | solution.py:40
  116.0 4.5 all-to-all-start
  120.6 0.2 reduce-scatter.8.cloned.1.call-start
  120.8 8.6 %fusion = f32[512,768]{1,0:T(8,128)} fusion(bf16[512,4096]{1,0:T(8,128)(2,1)} %bitcast.15, bf16[1,768,4096]{2,1,0:T(8,128)(2,1)} %param.12), kind=kOutput, calls=%fused_computation.5 | convolution fusion | flops 3221225472 | bytes 12058624 | tf_op jit(solution)/shard_map/dot_general | solution.py:59
  129.5 85.1 %all-to-all-done = bf16[8,64,4096]{2,1,0:T(8,128)(2,1)} async-done(((bf16[8,64,4096]{2,1,0:T(8,128)(2,1)}), bf16[8,64,4096]{2,1,0:T(8,128)(2,1)}, u32[]{:S(2)}, u32[]{:S(2)}) %all-to-all-start) | async-done | bytes 4194336 | tf_op jit(solution)/shard_map/all_to_all | solution.py:39
  214.6 7.2 %fusion.6 = f32[512,768]{1,0:T(8,128)S(1)} fusion(bf16[512,4096]{1,0:T(8,128)(2,1)} %bitcast.6, bf16[1,768,4096]{2,1,0:T(8,128)(2,1)} %param.11), kind=kOutput, calls=%fused_computation.11 | convolution fusion | flops 3221225472 | bytes 12058624 | tf_op jit(solution)/shard_map/dot_general | solution.py:47
  221.8 8.1 %multiply_convert_fusion.5 = (bf16[512,768]{1,0:T(8,128)(2,1)S(1)}, bf16[512,768]{1,0:T(8,128)(2,1)S(1)}, bf16[512,768]{1,0:T(8,128)(2,1)S(1)}) fusion(f32[512,768]{1,0:T(8,128)S(1)} %copy-done.4, f32[512,768]{1,0:T(8,128)S(1)} %fusion.6, bf16[512,4096]{1,0:T(8,128)(2,1)} %bitcast.6, bf16[1,768,4096]{2,1,0:T(8,128)(2,1)} %param.10), kind=kOutput, calls=%fused_computation.27 | convolution fusion | flops 3227516928 | bytes 15990784 | tf_op jit(solution)/shard_map/dot_general | solution.py:46
  230.0 7.6 %multiply_convert_fusion = bf16[768,4096]{1,0:T(8,128)(2,1)} fusion(bf16[512,768]{1,0:T(8,128)(2,1)S(1)} %get-tuple-element.10, bf16[512,4096]{1,0:T(8,128)(2,1)} %bitcast.15), kind=kOutput, calls=%fused_computation | convolution fusion | flops 3227516928 | bytes 11272192 | tf_op jit(solution)/shard_map/weight_grads/rf,rd->fd/dot_general | solution.py:77
  237.6 0.3 reduce-scatter.4.cloned.1.call-start
  237.9 7.6 %multiply_convert_fusion.2 = bf16[768,4096]{1,0:T(8,128)(2,1)} fusion(bf16[512,768]{1,0:T(8,128)(2,1)S(1)} %get-tuple-element.9, bf16[512,4096]{1,0:T(8,128)(2,1)} %bitcast.6), kind=kOutput, calls=%fused_computation.2 | convolution fusion | flops 3227516928 | bytes 11272192 | tf_op jit(solution)/shard_map/weight_grads/rf,rd->fd/dot_general | solution.py:80
  245.5 7.9 %fusion.12 = bf16[512,4096]{1,0:T(8,128)(2,1)} fusion(bf16[512,768]{1,0:T(8,128)(2,1)S(1)} %get-tuple-element.10, bf16[1,768,4096]{2,1,0:T(8,128)(2,1)} %param.12), kind=kOutput, calls=%fused_computation.18 | convolution fusion | flops 3223322624 | bytes 11272192 | tf_op jit(solution)/shard_map/dot_general | solution.py:50
  253.3 4.7 %all-to-all-start.1 = ((bf16[8,64,4096]{2,1,0:T(8,128)(2,1)}), bf16[8,64,4096]{2,1,0:T(8,128)(2,1)}, u32[]{:S(2)}, u32[]{:S(2)}) async-start(bf16[8,64,4096]{2,1,0:T(8,128)(2,1)} %bitcast.73), calls=%async_computation.1 | async-start | bytes 8388608 | tf_op jit(solution)/shard_map/all_to_all | solution.py:51
  258.1 7.9 %multiply_convert_fusion.1 = bf16[768,4096]{1,0:T(8,128)(2,1)} fusion(bf16[512,768]{1,0:T(8,128)(2,1)S(1)} %get-tuple-element.11, bf16[512,4096]{1,0:T(8,128)(2,1)} %bitcast.6), kind=kOutput, calls=%fused_computation.1 | convolution fusion | flops 3227516928 | bytes 11272192 | tf_op jit(solution)/shard_map/weight_grads/rf,rd->fd/dot_general | solution.py:83
  266.0 5.5 %fusion.4 = f32[512,4096]{1,0:T(8,128)S(1)} fusion(bf16[512,768]{1,0:T(8,128)(2,1)S(1)} %get-tuple-element.11, bf16[1,768,4096]{2,1,0:T(8,128)(2,1)} %param.11), kind=kOutput, calls=%fused_computation.9 | convolution fusion | flops 3221225472 | bytes 15466496 | tf_op jit(solution)/shard_map/dot_general | solution.py:66
  271.5 8.0 %add_convert_fusion = bf16[512,4096]{1,0:T(8,128)(2,1)} fusion(f32[512,4096]{1,0:T(8,128)S(1)} %fusion.4, bf16[512,768]{1,0:T(8,128)(2,1)S(1)} %get-tuple-element.9, bf16[1,768,4096]{2,1,0:T(8,128)(2,1)} %param.10), kind=kOutput, calls=%fused_computation.3 | convolution fusion | flops 3225419776 | bytes 19660800 | tf_op jit(solution)/shard_map/dot_general | solution.py:65
  279.5 72.5 %all-to-all-done.1 = bf16[8,64,4096]{2,1,0:T(8,128)(2,1)} async-done(((bf16[8,64,4096]{2,1,0:T(8,128)(2,1)}), bf16[8,64,4096]{2,1,0:T(8,128)(2,1)}, u32[]{:S(2)}, u32[]{:S(2)}) %all-to-all-start.1) | async-done | bytes 4194336 | tf_op jit(solution)/shard_map/all_to_all | solution.py:51
  352.0 4.7 %all-to-all-start.3 = ((bf16[8,64,4096]{2,1,0:T(8,128)(2,1)}), bf16[8,64,4096]{2,1,0:T(8,128)(2,1)}, u32[]{:S(2)}, u32[]{:S(2)}) async-start(bf16[8,64,4096]{2,1,0:T(8,128)(2,1)} %bitcast.72), calls=%async_computation.3 | async-start | bytes 8388608 | tf_op jit(solution)/shard_map/all_to_all | solution.py:68
  356.8 3.6 fusion.22
  360.4 2.0 fusion.17
  362.4 0.6 pad_maximum_fusion
  363.0 87.8 %all-to-all-done.3 = bf16[8,64,4096]{2,1,0:T(8,128)(2,1)} async-done(((bf16[8,64,4096]{2,1,0:T(8,128)(2,1)}), bf16[8,64,4096]{2,1,0:T(8,128)(2,1)}, u32[]{:S(2)}, u32[]{:S(2)}) %all-to-all-start.3) | async-done | bytes 4194336 | tf_op jit(solution)/shard_map/all_to_all | solution.py:68
  450.8 3.6 fusion.21
  454.4 1.2 fusion.19
  (26 shorter events, 0.7 us)
Async XLA Ops:
  7.2 14.8 %copy-start = (bf16[128,4096]{1,0:T(8,128)(2,1)S(1)}, bf16[128,4096]{1,0:T(8,128)(2,1)}, u32[]{:S(2)}) copy-start(bf16[128,4096]{1,0:T(8,128)(2,1)} %param.7) | copy-start | bytes 3145732
  15.6 100.4 %all-to-all-start.2 = ((bf16[8,64,4096]{2,1,0:T(8,128)(2,1)}), bf16[8,64,4096]{2,1,0:T(8,128)(2,1)}, u32[]{:S(2)}, u32[]{:S(2)}) async-start(bf16[8,64,4096]{2,1,0:T(8,128)(2,1)} %bitcast.71), calls=%async_computation.2 | async-start | bytes 8388608 | tf_op jit(solution)/shard_map/all_to_all | solution.py:40
  116.0 98.6 %all-to-all-start = ((bf16[8,64,4096]{2,1,0:T(8,128)(2,1)}), bf16[8,64,4096]{2,1,0:T(8,128)(2,1)}, u32[]{:S(2)}, u32[]{:S(2)}) async-start(bf16[8,64,4096]{2,1,0:T(8,128)(2,1)} %bitcast.70), calls=%async_computation | async-start | bytes 8388608 | tf_op jit(solution)/shard_map/all_to_all | solution.py:39
  120.6 334.9 %reduce-scatter.8.cloned.1.call-start = ((), (), s32[]{:S(2)}) async-start(), calls=%async_computation.9 | async-start | bytes 7864320 | tf_op jit(solution)/shard_map/reduce_scatter | solution.py:85
  214.6 7.2 %copy-start.4 = (f32[512,768]{1,0:T(8,128)S(1)}, f32[512,768]{1,0:T(8,128)}, u32[]{:S(2)}) copy-start(f32[512,768]{1,0:T(8,128)} %fusion) | copy-start | bytes 4718596
  237.6 217.9 %reduce-scatter.4.cloned.1.call-start = ((), (), s32[]{:S(2)}) async-start(), calls=%async_computation.7 | async-start | bytes 7864320 | tf_op jit(solution)/shard_map/reduce_scatter | solution.py:86
  253.3 98.7 %all-to-all-start.1 = ((bf16[8,64,4096]{2,1,0:T(8,128)(2,1)}), bf16[8,64,4096]{2,1,0:T(8,128)(2,1)}, u32[]{:S(2)}, u32[]{:S(2)}) async-start(bf16[8,64,4096]{2,1,0:T(8,128)(2,1)} %bitcast.73), calls=%async_computation.1 | async-start | bytes 8388608 | tf_op jit(solution)/shard_map/all_to_all | solution.py:51
  258.0 197.5 %reduce-scatter.6.cloned.1.call-start = ((), (), s32[]{:S(2)}) async-start(), calls=%async_computation.8 | async-start | bytes 7864320 | tf_op jit(solution)/shard_map/reduce_scatter | solution.py:87
  352.0 4.8 %copy-start.3 = (f32[128,2]{0,1:T(2,128)S(1)}, f32[128,2]{0,1:T(2,128)}, u32[]{:S(2)}) copy-start(f32[128,2]{0,1:T(2,128)} %param.9) | copy-start | bytes 3076
  352.0 98.8 %all-to-all-start.3 = ((bf16[8,64,4096]{2,1,0:T(8,128)(2,1)}), bf16[8,64,4096]{2,1,0:T(8,128)(2,1)}, u32[]{:S(2)}, u32[]{:S(2)}) async-start(bf16[8,64,4096]{2,1,0:T(8,128)(2,1)} %bitcast.72), calls=%async_computation.3 | async-start | bytes 8388608 | tf_op jit(solution)/shard_map/all_to_all | solution.py:68
  356.8 3.6 copy-start.2
  450.8 4.8 %copy-start.1 = (bf16[128,4096]{1,0:T(8,128)(2,1)S(1)}, bf16[128,4096]{1,0:T(8,128)(2,1)}, u32[]{:S(2)}) copy-start(bf16[128,4096]{1,0:T(8,128)(2,1)} %param.7) | copy-start | bytes 3145732
Sparse Core Ops, SparseCore 0:
  237.7 69.0 reduce-scatter.7
  310.4 70.1 reduce-scatter.3
  384.2 70.1 reduce-scatter.5

commit v2 on v1

--- a/solution.py
+++ b/solution.py
@@ -37,17 +37,27 @@
     send_rows = send_rows.reshape(experts, capacity, model_width)
     send_grads = send_grads.reshape(experts, capacity, model_width)
     recv_rows = lax.all_to_all(send_rows, "expert", split_axis=0, concat_axis=0, tiled=True)
+    recv_rows, send_grads = lax.optimization_barrier((recv_rows, send_grads))
     recv_grads = lax.all_to_all(send_grads, "expert", split_axis=0, concat_axis=0, tiled=True)
     in_rows = recv_rows.reshape(slots, model_width)
     out_grads = recv_grads.reshape(slots, model_width)
     w_gate = weight_gate[0]
     w_up = weight_up[0]
     w_down = weight_down[0]
-    gate_pre = jnp.dot(in_rows, w_gate.T, preferred_element_type=jnp.float32)
-    up_pre = jnp.dot(in_rows, w_up.T, preferred_element_type=jnp.float32)
-    sigmoid_gate = jax.nn.sigmoid(gate_pre)
-    activated = (gate_pre * sigmoid_gate * up_pre).astype(jnp.bfloat16)
-    expert_out = jnp.dot(activated, w_down, preferred_element_type=jnp.float32).astype(jnp.bfloat16)
+    def forward(rows):
+        gate_pre = jnp.dot(rows, w_gate.T, preferred_element_type=jnp.float32)
+        up_pre = jnp.dot(rows, w_up.T, preferred_element_type=jnp.float32)
+        sigmoid_gate = jax.nn.sigmoid(gate_pre)
+        activated = (gate_pre * sigmoid_gate * up_pre).astype(jnp.bfloat16)
+        expert_out = jnp.dot(activated, w_down, preferred_element_type=jnp.float32).astype(
+            jnp.bfloat16
+        )
+        return gate_pre, up_pre, sigmoid_gate, activated, expert_out
+
+    always = expert_ids[0, 0] >= 0
+    gate_pre, up_pre, sigmoid_gate, activated, expert_out = lax.cond(
+        always, forward, forward, in_rows
+    )
     back_out = lax.all_to_all(
         expert_out.reshape(experts, capacity, model_width),
         "expert",

time: 463 us -> 454 us (0.981)
  waiting for transfers between devices: 336 us -> 327 us
    all_to_all x1, waiting for transfers between devices: 90.7 us -> 70.8 us  [per_device(): lax.all_to_all(send_grads, 'expert', split_axis=0, concat_axis=0, tiled=T...]
    reduce_scatter x1, waiting for transfers between devices: 0.01 us -> 6.18 us  [per_device(): lax.psum_scatter(down_term, 'dp', scatter_dimension=0, tiled=True)]
    all_to_all x1, waiting for transfers between devices: 85.1 us -> 90.7 us  [per_device(): lax.all_to_all(send_rows, 'expert', split_axis=0, concat_axis=0, tiled=True)]
  transfers between devices with their start and end apart: 7 -> 7, of which waited for: 4 -> 5; matrix products, arithmetic and copies ran while one was open for 13% -> 15% of each run, Pallas kernels for 0% -> 0%
where the time goes in v2:
time: 454 us; the launch traced here: 453 us
  waiting for transfers between devices  327 us (72%)
  matrix products  82.3 us (18%)
  starting transfers between devices  20.6 us (5%)
  between operations  14.5 us (3%)
  other arithmetic  5.47 us (1%)
    all_to_all x1, waiting for transfers between devices, per_device(): lax.all_to_all(send_rows, 'expert', split_axis=0, concat_axis=0, tiled=True)  90.7 us
    all_to_all x1, waiting for transfers between devices, per_device(): lax.all_to_all(row_grads.reshape(experts, capacity, model_width), 'expert...  87.8 us
    all_to_all x1, waiting for transfers between devices, per_device(): lax.all_to_all(expert_out.reshape(experts, capacity, model_width), 'exper...  71.5 us
    all_to_all x1, waiting for transfers between devices, per_device(): lax.all_to_all(send_grads, 'expert', split_axis=0, concat_axis=0, tiled=T...  70.8 us
    dot_general x1, matrix products, per_device(): grad_act = jnp.dot(out_grads, w_down.T, preferred_element_type=jnp.float32)  9.44 us
  transfers between devices with their start and end apart: 7, of which 5 were waited for; matrix products, arithmetic and copies ran while one was open for 15% of the time, Pallas kernels for 0%

profile of v2, /device:TPU:0, one launch (start us, length us, event | category | flops | bytes accessed | tf_op | source)
XLA Modules:
  0.0 453.3 jit_solution(12383229305500997010)
XLA Ops:
  7.2 0.9 copy.30
  8.4 0.6 reduce-window.6
  9.5 0.7 fusion.16
  10.3 3.3 convolution_convert_fusion
  13.6 6.5 %all-to-all-start = ((bf16[8,64,4096]{2,1,0:T(8,128)(2,1)}), bf16[8,64,4096]{2,1,0:T(8,128)(2,1)}, u32[]{:S(2)}, u32[]{:S(2)}) async-start(bf16[8,64,4096]{2,1,0:T(8,128)(2,1)} %bitcast.71), calls=%async_computation | async-start | bytes 8388608 | tf_op jit(solution)/shard_map/all_to_all | solution.py:39
  20.2 3.3 multiply_convert_fusion.3
  23.5 90.7 %all-to-all-done = bf16[8,64,4096]{2,1,0:T(8,128)(2,1)} async-done(((bf16[8,64,4096]{2,1,0:T(8,128)(2,1)}), bf16[8,64,4096]{2,1,0:T(8,128)(2,1)}, u32[]{:S(2)}, u32[]{:S(2)}) %all-to-all-start) | async-done | bytes 4194336 | tf_op jit(solution)/shard_map/all_to_all | solution.py:39
  114.2 4.7 %all-to-all-start.2 = ((bf16[8,64,4096]{2,1,0:T(8,128)(2,1)}), bf16[8,64,4096]{2,1,0:T(8,128)(2,1)}, u32[]{:S(2)}, u32[]{:S(2)}) async-start(bf16[8,64,4096]{2,1,0:T(8,128)(2,1)} %bitcast.70), calls=%async_computation.2 | async-start | bytes 8388608 | tf_op jit(solution)/shard_map/all_to_all | solution.py:41
  118.9 0.5 slice.36
  120.1 21.9 %conditional.2 = (f32[512,768]{1,0:T(8,128)S(1)}, f32[512,768]{1,0:T(8,128)}, f32[512,768]{1,0:T(8,128)}, bf16[512,768]{1,0:T(8,128)(2,1)}, bf16[512,4096]{1,0:T(8,128)(2,1)}) conditional(s32[]{:T(128)} %bitcast.5, (bf16[512,4096]{1,0:T(8,128)(2,1)}, bf16[768,4096]{1,0:T(8,128)(2,1)}, bf16[768,4096]{1,0:T(8,128)(2,1)}, ...), branch_computations={%region_5.6_spmd, %region_6.7_spmd} | conditional | flops 9666035712 | bytes 95944872
  120.3 7.3 %fusion.25 = f32[512,768]{1,0:T(8,128)S(1)} fusion(bf16[512,4096]{1,0:T(8,128)(2,1)} %get-tuple-element.27, bf16[768,4096]{1,0:T(8,128)(2,1)} %get-tuple-element.28), kind=kOutput, calls=%fused_computation.52 | convolution fusion | flops 3221225472 | bytes 12058624 | tf_op jit(solution)/shard_map/cond/branch_1_fun/dot_general | solution.py:48
  127.6 8.2 %multiply_multiply_fusion.1 = (bf16[512,768]{1,0:T(8,128)(2,1)}, f32[512,768]{1,0:T(8,128)}, f32[512,768]{1,0:T(8,128)}) fusion(f32[512,768]{1,0:T(8,128)S(1)} %fusion.25, bf16[512,4096]{1,0:T(8,128)(2,1)} %get-tuple-element.27, bf16[768,4096]{1,0:T(8,128)(2,1)S(1)} %copy-done.6), kind=kOutput, calls=%fused_computation.4 | convolution fusion | flops 3223584768 | bytes 15990784 | tf_op jit(solution)/shard_map/cond/branch_1_fun/dot_general | solution.py:49
  135.9 6.2 %fusion.26 = bf16[512,4096]{1,0:T(8,128)(2,1)} fusion(bf16[512,768]{1,0:T(8,128)(2,1)} %get-tuple-element.74, bf16[768,4096]{1,0:T(8,128)(2,1)S(1)} %bitcast.83), kind=kOutput, calls=%fused_computation.53 | convolution fusion | flops 3221225472 | bytes 11272192 | tf_op jit(solution)/shard_map/cond/branch_1_fun/dot_general | solution.py:52
  142.0 70.8 %all-to-all-done.2 = bf16[8,64,4096]{2,1,0:T(8,128)(2,1)} async-done(((bf16[8,64,4096]{2,1,0:T(8,128)(2,1)}), bf16[8,64,4096]{2,1,0:T(8,128)(2,1)}, u32[]{:S(2)}, u32[]{:S(2)}) %all-to-all-start.2) | async-done | bytes 4194336 | tf_op jit(solution)/shard_map/all_to_all | solution.py:41
  212.9 9.4 %multiply_convert_fusion.4 = (bf16[512,768]{1,0:T(8,128)(2,1)}, bf16[512,768]{1,0:T(8,128)(2,1)S(1)}) fusion(f32[512,768]{1,0:T(8,128)} %get-tuple-element.48, f32[512,768]{1,0:T(8,128)S(1)} %get-tuple-element.49, f32[512,768]{1,0:T(8,128)} %get-tuple-element.47, bf16[512,4096]{1,0:T(8,128)(2,1)} %bitcast.16, bf16[1,768,4096]{2,1,0:T(8,128)(2,1)} %param.14), kind=kOutput, calls=%fused_computation.21 | convolution fusion | flops 3225157632 | bytes 16777216 | tf_op jit(solution)/shard_map/dot_general | solution.py:69
  222.3 7.6 %multiply_convert_fusion.2 = bf16[768,4096]{1,0:T(8,128)(2,1)} fusion(bf16[512,768]{1,0:T(8,128)(2,1)S(1)} %get-tuple-element.60, bf16[512,4096]{1,0:T(8,128)(2,1)} %bitcast.9), kind=kOutput, calls=%fused_computation.10 | convolution fusion | flops 3227516928 | bytes 11272192 | tf_op jit(solution)/shard_map/weight_grads/rf,rd->fd/dot_general | solution.py:90
  229.9 0.3 reduce-scatter.6.cloned.1.call-start
  230.2 0.8 copy-done.9
  231.0 7.6 %multiply_convert_fusion.1 = bf16[768,4096]{1,0:T(8,128)(2,1)} fusion(bf16[512,768]{1,0:T(8,128)(2,1)S(1)} %copy-done.9, bf16[512,4096]{1,0:T(8,128)(2,1)} %bitcast.9), kind=kOutput, calls=%fused_computation.9 | convolution fusion | flops 3227516928 | bytes 11272192 | tf_op jit(solution)/shard_map/weight_grads/rf,rd->fd/dot_general | solution.py:93
  238.6 4.6 %all-to-all-start.1 = ((bf16[8,64,4096]{2,1,0:T(8,128)(2,1)}), bf16[8,64,4096]{2,1,0:T(8,128)(2,1)}, u32[]{:S(2)}, u32[]{:S(2)}) async-start(bf16[8,64,4096]{2,1,0:T(8,128)(2,1)} %bitcast.13), calls=%async_computation.1 | async-start | bytes 8388608 | tf_op jit(solution)/shard_map/all_to_all | solution.py:61
  243.3 8.7 %multiply_convert_fusion = bf16[768,4096]{1,0:T(8,128)(2,1)} fusion(bf16[512,4096]{1,0:T(8,128)(2,1)} %bitcast.16, bf16[512,768]{1,0:T(8,128)(2,1)} %get-tuple-element.50), kind=kOutput, calls=%fused_computation.8 | convolution fusion | flops 3227516928 | bytes 11272192 | tf_op jit(solution)/shard_map/weight_grads/rf,rd->fd/dot_general | solution.py:87
  252.0 5.6 %fusion.21 = f32[512,4096]{1,0:T(8,128)S(1)} fusion(bf16[512,768]{1,0:T(8,128)(2,1)S(1)} %get-tuple-element.60, bf16[1,768,4096]{2,1,0:T(8,128)(2,1)} %param.12), kind=kOutput, calls=%fused_computation.48 | convolution fusion | flops 3221225472 | bytes 15466496 | tf_op jit(solution)/shard_map/dot_general | solution.py:75
  257.6 8.0 %add_convert_fusion = bf16[512,4096]{1,0:T(8,128)(2,1)} fusion(f32[512,4096]{1,0:T(8,128)S(1)} %fusion.21, bf16[512,768]{1,0:T(8,128)(2,1)S(1)} %copy-done.9, bf16[1,768,4096]{2,1,0:T(8,128)(2,1)} %param.13), kind=kOutput, calls=%fused_computation.11 | convolution fusion | flops 3225419776 | bytes 19660800 | tf_op jit(solution)/shard_map/dot_general | solution.py:76
  265.7 71.5 %all-to-all-done.1 = bf16[8,64,4096]{2,1,0:T(8,128)(2,1)} async-done(((bf16[8,64,4096]{2,1,0:T(8,128)(2,1)}), bf16[8,64,4096]{2,1,0:T(8,128)(2,1)}, u32[]{:S(2)}, u32[]{:S(2)}) %all-to-all-start.1) | async-done | bytes 4194336 | tf_op jit(solution)/shard_map/all_to_all | solution.py:61
  337.2 4.6 %all-to-all-start.3 = ((bf16[8,64,4096]{2,1,0:T(8,128)(2,1)}), bf16[8,64,4096]{2,1,0:T(8,128)(2,1)}, u32[]{:S(2)}, u32[]{:S(2)}) async-start(bf16[8,64,4096]{2,1,0:T(8,128)(2,1)} %bitcast.74), calls=%async_computation.3 | async-start | bytes 8388608 | tf_op jit(solution)/shard_map/all_to_all | solution.py:78
  341.8 3.6 fusion.10
  345.4 2.0 fusion.4
  347.4 0.6 pad_maximum_fusion
  348.0 87.8 %all-to-all-done.3 = bf16[8,64,4096]{2,1,0:T(8,128)(2,1)} async-done(((bf16[8,64,4096]{2,1,0:T(8,128)(2,1)}), bf16[8,64,4096]{2,1,0:T(8,128)(2,1)}, u32[]{:S(2)}, u32[]{:S(2)}) %all-to-all-start.3) | async-done | bytes 4194336 | tf_op jit(solution)/shard_map/all_to_all | solution.py:78
  435.8 3.6 fusion.9
  439.4 1.2 fusion.6
  440.6 6.2 %reduce-scatter.8.cloned.1.call-done = bf16[192,4096]{1,0:T(8,128)(2,1)} async-done(((bf16[768,4096]{1,0:T(8,128)(2,1)}), bf16[192,4096]{1,0:T(8,128)(2,1)}) %reduce-scatter.8.cloned.1.call-update) | async-done | bytes 1572880 | tf_op jit(solution)/shard_map/reduce_scatter | solution.py:95
  (41 shorter events, 1.3 us)
Async XLA Ops:
  7.2 3.2 copy-start
  13.6 6.5 %copy-start.4 = (f32[128,2]{0,1:T(2,128)S(1)}, f32[128,2]{0,1:T(2,128)}, u32[]{:S(2)}) copy-start(f32[128,2]{0,1:T(2,128)} %param.11) | copy-start | bytes 3076
  13.6 6.6 %copy-start.2 = (bf16[128,4096]{1,0:T(8,128)(2,1)S(1)}, bf16[128,4096]{1,0:T(8,128)(2,1)}, u32[]{:S(2)}) copy-start(bf16[128,4096]{1,0:T(8,128)(2,1)} %param.15) | copy-start | bytes 3145732
  13.6 100.6 %all-to-all-start = ((bf16[8,64,4096]{2,1,0:T(8,128)(2,1)}), bf16[8,64,4096]{2,1,0:T(8,128)(2,1)}, u32[]{:S(2)}, u32[]{:S(2)}) async-start(bf16[8,64,4096]{2,1,0:T(8,128)(2,1)} %bitcast.71), calls=%async_computation | async-start | bytes 8388608 | tf_op jit(solution)/shard_map/all_to_all | solution.py:39
  114.2 4.7 %copy-start.3 = (s32[128,2]{0,1:T(2,128)S(1)}, s32[128,2]{0,1:T(2,128)}, u32[]{:S(2)}) copy-start(s32[128,2]{0,1:T(2,128)} %param.10) | copy-start | bytes 3076
  114.2 98.7 %all-to-all-start.2 = ((bf16[8,64,4096]{2,1,0:T(8,128)(2,1)}), bf16[8,64,4096]{2,1,0:T(8,128)(2,1)}, u32[]{:S(2)}, u32[]{:S(2)}) async-start(bf16[8,64,4096]{2,1,0:T(8,128)(2,1)} %bitcast.70), calls=%async_computation.2 | async-start | bytes 8388608 | tf_op jit(solution)/shard_map/all_to_all | solution.py:41
  118.9 321.7 %reduce-scatter.4.cloned.1.call-start = ((), (), s32[]{:S(2)}) async-start(), calls=%async_computation.7 | async-start | bytes 7864320 | tf_op jit(solution)/shard_map/reduce_scatter | solution.py:96
  120.3 7.3 %copy-start.6 = (bf16[768,4096]{1,0:T(8,128)(2,1)S(1)}, bf16[768,4096]{1,0:T(8,128)(2,1)}, u32[]{:S(2)}) copy-start(bf16[768,4096]{1,0:T(8,128)(2,1)} %get-tuple-element.29) | copy-start | bytes 18874372 | tf_op jit(solution)/shard_map/conditional
  120.3 15.5 %slice-start.2 = ((s8[6291456]{0:T(1024)(128)(4,1)}), s8[4194304]{0:T(1024)(128)(4,1)S(1)}, s32[]{:S(2)}) async-start(s8[6291456]{0:T(1024)(128)(4,1)} %bitcast.82), calls=%async_computation.12 | async-start | bytes 8388608 | tf_op jit(solution)/shard_map/conditional
  127.6 8.2 %copy-start.7 = (f32[512,768]{1,0:T(8,128)}, f32[512,768]{1,0:T(8,128)S(1)}, u32[]{:S(2)}) copy-start(f32[512,768]{1,0:T(8,128)S(1)} %fusion.25) | copy-start | bytes 4718596 | tf_op jit(solution)/shard_map/conditional
  127.6 8.2 %slice-start.3 = ((s8[6291456]{0:T(1024)(128)(4,1)}), s8[2097152]{0:T(1024)(128)(4,1)S(1)}, s32[]{:S(2)}) async-start(s8[6291456]{0:T(1024)(128)(4,1)} %bitcast.82), calls=%async_computation.13 | async-start | bytes 4194304 | tf_op jit(solution)/shard_map/conditional
  135.8 6.2 %copy-start.8 = (f32[512,768]{1,0:T(8,128)S(1)}, f32[512,768]{1,0:T(8,128)}, u32[]{:S(2)}) copy-start(f32[512,768]{1,0:T(8,128)} %copy-done.7) | copy-start | bytes 4718596 | tf_op jit(solution)/shard_map/conditional
  229.9 1.1 copy-start.9
  229.9 210.6 %reduce-scatter.6.cloned.1.call-start = ((), (), s32[]{:S(2)}) async-start(), calls=%async_computation.8 | async-start | bytes 7864320 | tf_op jit(solution)/shard_map/reduce_scatter | solution.py:97
  238.6 98.6 %all-to-all-start.1 = ((bf16[8,64,4096]{2,1,0:T(8,128)(2,1)}), bf16[8,64,4096]{2,1,0:T(8,128)(2,1)}, u32[]{:S(2)}, u32[]{:S(2)}) async-start(bf16[8,64,4096]{2,1,0:T(8,128)(2,1)} %bitcast.13), calls=%async_computation.1 | async-start | bytes 8388608 | tf_op jit(solution)/shard_map/all_to_all | solution.py:61
  243.2 203.5 %reduce-scatter.8.cloned.1.call-start = ((), (), s32[]{:S(2)}) async-start(), calls=%async_computation.9 | async-start | bytes 7864320 | tf_op jit(solution)/shard_map/reduce_scatter | solution.py:95
  337.2 98.6 %all-to-all-start.3 = ((bf16[8,64,4096]{2,1,0:T(8,128)(2,1)}), bf16[8,64,4096]{2,1,0:T(8,128)(2,1)}, u32[]{:S(2)}, u32[]{:S(2)}) async-start(bf16[8,64,4096]{2,1,0:T(8,128)(2,1)} %bitcast.74), calls=%async_computation.3 | async-start | bytes 8388608 | tf_op jit(solution)/shard_map/all_to_all | solution.py:78
  435.8 11.0 %copy-start.1 = (bf16[128,4096]{1,0:T(8,128)(2,1)S(1)}, bf16[128,4096]{1,0:T(8,128)(2,1)}, u32[]{:S(2)}) copy-start(bf16[128,4096]{1,0:T(8,128)(2,1)} %param.9) | copy-start | bytes 3145732
Sparse Core Ops, SparseCore 0:
  230.0 69.0 reduce-scatter.3
  302.7 70.1 reduce-scatter.5
  376.5 70.1 reduce-scatter.7

commit v3 on v2

--- a/solution.py
+++ b/solution.py
@@ -82,19 +82,25 @@
         concat_axis=0,
         tiled=True,
     )
+    ff_share = w_gate.shape[0] // copies
     with jax.named_scope("weight_grads"):
         down_term = (
             scale * jnp.einsum("rf,rd->fd", activated, out_grads, preferred_element_type=jnp.float32)
         ).astype(jnp.bfloat16)
-        gate_term = (
-            scale * jnp.einsum("rf,rd->fd", grad_gate_pre, in_rows, preferred_element_type=jnp.float32)
-        ).astype(jnp.bfloat16)
-        up_term = (
-            scale * jnp.einsum("rf,rd->fd", grad_up_pre, in_rows, preferred_element_type=jnp.float32)
+        gate_up_pre = jnp.stack(
+            [
+                grad_gate_pre.reshape(slots, copies, ff_share),
+                grad_up_pre.reshape(slots, copies, ff_share),
+            ],
+            axis=2,
+        ).reshape(slots, copies * 2 * ff_share)
+        gate_up_term = (
+            scale * jnp.einsum("rf,rd->fd", gate_up_pre, in_rows, preferred_element_type=jnp.float32)
         ).astype(jnp.bfloat16)
     down_share = lax.psum_scatter(down_term, "dp", scatter_dimension=0, tiled=True)
-    gate_share = lax.psum_scatter(gate_term, "dp", scatter_dimension=0, tiled=True)
-    up_share = lax.psum_scatter(up_term, "dp", scatter_dimension=0, tiled=True)
+    gate_up_share = lax.psum_scatter(gate_up_term, "dp", scatter_dimension=0, tiled=True)
+    gate_share = gate_up_share[:ff_share]
+    up_share = gate_up_share[ff_share:]
     pick_onehot = hit.reshape(top_count * tok_count, slots).astype(jnp.bfloat16)
     with jax.named_scope("combine_rows"):
         picked_out = jnp.dot(

time: 454 us -> 449 us (0.989)
  waiting for transfers between devices: 327 us -> 319 us
    reduce_scatter x1, waiting for transfers between devices: 6.18 us -> 0.01 us  [per_device(): lax.psum_scatter(down_term, 'dp', scatter_dimension=0, tiled=True)]
    dot_general x2 -> x1, matrix products: 15.2 us -> 11.9 us  [per_device(): jnp.einsum('rf,rd->fd', gate_up_pre, in_rows, preferred_element_type=jnp....]
  transfers between devices with their start and end apart: 7 -> 6, of which waited for: 5 -> 4; matrix products, arithmetic and copies ran while one was open for 15% -> 14% of each run, Pallas kernels for 0% -> 0%
where the time goes in v3:
time: 449 us; the launch traced here: 448 us
  waiting for transfers between devices  319 us (71%)
  matrix products  80.4 us (18%)
  starting transfers between devices  20.6 us (5%)
  between operations  14.9 us (3%)
  local copies, waits for them, and re-layouts  7.34 us (2%)
  other arithmetic  5.62 us (1%)
    all_to_all x1, waiting for transfers between devices, per_device(): lax.all_to_all(send_rows, 'expert', split_axis=0, concat_axis=0, tiled=True)  90.7 us
    all_to_all x1, waiting for transfers between devices, per_device(): lax.all_to_all(row_grads.reshape(experts, capacity, model_width), 'expert...  87.9 us
    all_to_all x1, waiting for transfers between devices, per_device(): lax.all_to_all(expert_out.reshape(experts, capacity, model_width), 'exper...  70.7 us
    all_to_all x1, waiting for transfers between devices, per_device(): lax.all_to_all(send_grads, 'expert', split_axis=0, concat_axis=0, tiled=T...  69.5 us
    dot_general x1, matrix products, per_device(): jnp.einsum('rf,rd->fd', gate_up_pre, in_rows, preferred_element_type=jnp....  11.9 us
    dot_general x1, matrix products, per_device(): jnp.einsum('rf,rd->fd', activated, out_grads, preferred_element_type=jnp....  9.37 us
    dot_general x1, matrix products, per_device(): grad_act = jnp.dot(out_grads, w_down.T, preferred_element_type=jnp.float32)  9.04 us
  transfers between devices with their start and end apart: 6, of which 4 were waited for; matrix products, arithmetic and copies ran while one was open for 14% of the time, Pallas kernels for 0%

profile of v3, /device:TPU:0, one launch (start us, length us, event | category | flops | bytes accessed | tf_op | source)
XLA Modules:
  0.0 447.9 jit_solution(6531942509474616164)
XLA Ops:
  7.2 0.9 copy.39
  8.4 0.6 reduce-window.6
  9.5 0.7 fusion.16
  10.3 3.3 convolution_convert_fusion
  13.6 6.5 %all-to-all-start = ((bf16[8,64,4096]{2,1,0:T(8,128)(2,1)}), bf16[8,64,4096]{2,1,0:T(8,128)(2,1)}, u32[]{:S(2)}, u32[]{:S(2)}) async-start(bf16[8,64,4096]{2,1,0:T(8,128)(2,1)} %bitcast.74), calls=%async_computation | async-start | bytes 8388608 | tf_op jit(solution)/shard_map/all_to_all | solution.py:39
  20.2 3.3 multiply_convert_fusion.2
  23.5 90.7 %all-to-all-done = bf16[8,64,4096]{2,1,0:T(8,128)(2,1)} async-done(((bf16[8,64,4096]{2,1,0:T(8,128)(2,1)}), bf16[8,64,4096]{2,1,0:T(8,128)(2,1)}, u32[]{:S(2)}, u32[]{:S(2)}) %all-to-all-start) | async-done | bytes 4194336 | tf_op jit(solution)/shard_map/all_to_all | solution.py:39
  114.2 4.7 %all-to-all-start.2 = ((bf16[8,64,4096]{2,1,0:T(8,128)(2,1)}), bf16[8,64,4096]{2,1,0:T(8,128)(2,1)}, u32[]{:S(2)}, u32[]{:S(2)}) async-start(bf16[8,64,4096]{2,1,0:T(8,128)(2,1)} %bitcast.73), calls=%async_computation.2 | async-start | bytes 8388608 | tf_op jit(solution)/shard_map/all_to_all | solution.py:41
  118.9 0.5 slice.42
  120.1 23.3 %conditional.2 = (f32[512,768]{1,0:T(8,128)}, f32[512,768]{1,0:T(8,128)}, f32[512,768]{1,0:T(8,128)}, bf16[512,768]{1,0:T(8,128)(2,1)}, bf16[512,4096]{1,0:T(8,128)(2,1)}) conditional(s32[]{:T(128)} %bitcast.5, (bf16[512,4096]{1,0:T(8,128)(2,1)}, bf16[768,4096]{1,0:T(8,128)(2,1)}, bf16[768,4096]{1,0:T(8,128)(2,1)}, ...), branch_computations={%region_5.6_spmd, %region_6.7_spmd} | conditional | flops 9666035712 | bytes 83361904
  120.3 8.8 %fusion.25 = f32[512,768]{1,0:T(8,128)} fusion(bf16[512,4096]{1,0:T(8,128)(2,1)} %get-tuple-element.27, bf16[768,4096]{1,0:T(8,128)(2,1)} %get-tuple-element.28), kind=kOutput, calls=%fused_computation.54 | convolution fusion | flops 3221225472 | bytes 12058624 | tf_op jit(solution)/shard_map/cond/branch_1_fun/dot_general | solution.py:48
  129.1 8.2 %multiply_multiply_fusion.1 = (bf16[512,768]{1,0:T(8,128)(2,1)}, f32[512,768]{1,0:T(8,128)}, f32[512,768]{1,0:T(8,128)}) fusion(f32[512,768]{1,0:T(8,128)} %fusion.25, bf16[512,4096]{1,0:T(8,128)(2,1)} %get-tuple-element.27, bf16[768,4096]{1,0:T(8,128)(2,1)S(1)} %copy-done.8), kind=kOutput, calls=%fused_computation.4 | convolution fusion | flops 3223584768 | bytes 15990784 | tf_op jit(solution)/shard_map/cond/branch_1_fun/dot_general | solution.py:49
  137.3 6.1 %fusion.26 = bf16[512,4096]{1,0:T(8,128)(2,1)} fusion(bf16[512,768]{1,0:T(8,128)(2,1)} %get-tuple-element.76, bf16[768,4096]{1,0:T(8,128)(2,1)S(1)} %bitcast.89), kind=kOutput, calls=%fused_computation.55 | convolution fusion | flops 3221225472 | bytes 11272192 | tf_op jit(solution)/shard_map/cond/branch_1_fun/dot_general | solution.py:52
  143.4 69.5 %all-to-all-done.2 = bf16[8,64,4096]{2,1,0:T(8,128)(2,1)} async-done(((bf16[8,64,4096]{2,1,0:T(8,128)(2,1)}), bf16[8,64,4096]{2,1,0:T(8,128)(2,1)}, u32[]{:S(2)}, u32[]{:S(2)}) %all-to-all-start.2) | async-done | bytes 4194336 | tf_op jit(solution)/shard_map/all_to_all | solution.py:41
  212.9 9.0 %multiply_convert_fusion.3 = (bf16[512,768]{1,0:T(8,128)(2,1)S(1)}, bf16[512,768]{1,0:T(8,128)(2,1)S(1)}) fusion(f32[512,768]{1,0:T(8,128)} %get-tuple-element.48, f32[512,768]{1,0:T(8,128)} %get-tuple-element.49, f32[512,768]{1,0:T(8,128)} %get-tuple-element.47, bf16[512,4096]{1,0:T(8,128)(2,1)} %bitcast.16, bf16[1,768,4096]{2,1,0:T(8,128)(2,1)} %param.14), kind=kOutput, calls=%fused_computation.23 | convolution fusion | flops 3225157632 | bytes 16777216 | tf_op jit(solution)/shard_map/dot_general | solution.py:69
  221.9 0.3 copy.43
  222.2 0.6 copy-done.3
  222.8 0.3 copy.42
  223.4 11.9 %multiply_convert_fusion = bf16[1536,4096]{1,0:T(8,128)(2,1)} fusion(bf16[512,1536]{0,1:T(8,128)(2,1)S(1)} %bitcast.80, bf16[512,4096]{1,0:T(8,128)(2,1)} %bitcast.9), kind=kOutput, calls=%fused_computation.8 | convolution fusion | flops 6455033856 | bytes 18350080 | tf_op jit(solution)/shard_map/weight_grads/rf,rd->fd/dot_general | solution.py:98
  235.3 4.6 %all-to-all-start.1 = ((bf16[8,64,4096]{2,1,0:T(8,128)(2,1)}), bf16[8,64,4096]{2,1,0:T(8,128)(2,1)}, u32[]{:S(2)}, u32[]{:S(2)}) async-start(bf16[8,64,4096]{2,1,0:T(8,128)(2,1)} %bitcast.13), calls=%async_computation.1 | async-start | bytes 8388608 | tf_op jit(solution)/shard_map/all_to_all | solution.py:61
  240.2 9.4 %multiply_convert_fusion.1 = bf16[768,4096]{1,0:T(8,128)(2,1)} fusion(bf16[512,4096]{1,0:T(8,128)(2,1)} %bitcast.16, bf16[512,768]{1,0:T(8,128)(2,1)} %get-tuple-element.50), kind=kOutput, calls=%fused_computation.9 | convolution fusion | flops 3227516928 | bytes 11272192 | tf_op jit(solution)/shard_map/weight_grads/rf,rd->fd/dot_general | solution.py:88
  249.6 5.6 %fusion.21 = f32[512,4096]{1,0:T(8,128)S(1)} fusion(bf16[512,768]{1,0:T(8,128)(2,1)S(1)} %get-tuple-element.60, bf16[1,768,4096]{2,1,0:T(8,128)(2,1)} %param.12), kind=kOutput, calls=%fused_computation.50 | convolution fusion | flops 3221225472 | bytes 15466496 | tf_op jit(solution)/shard_map/dot_general | solution.py:75
  255.2 8.0 %add_convert_fusion = bf16[512,4096]{1,0:T(8,128)(2,1)} fusion(f32[512,4096]{1,0:T(8,128)S(1)} %fusion.21, bf16[512,768]{1,0:T(8,128)(2,1)S(1)} %copy-done.4, bf16[1,768,4096]{2,1,0:T(8,128)(2,1)} %param.13), kind=kOutput, calls=%fused_computation.10 | convolution fusion | flops 3225419776 | bytes 19660800 | tf_op jit(solution)/shard_map/dot_general | solution.py:76
  263.2 70.7 %all-to-all-done.1 = bf16[8,64,4096]{2,1,0:T(8,128)(2,1)} async-done(((bf16[8,64,4096]{2,1,0:T(8,128)(2,1)}), bf16[8,64,4096]{2,1,0:T(8,128)(2,1)}, u32[]{:S(2)}, u32[]{:S(2)}) %all-to-all-start.1) | async-done | bytes 4194336 | tf_op jit(solution)/shard_map/all_to_all | solution.py:61
  333.9 4.6 %all-to-all-start.3 = ((bf16[8,64,4096]{2,1,0:T(8,128)(2,1)}), bf16[8,64,4096]{2,1,0:T(8,128)(2,1)}, u32[]{:S(2)}, u32[]{:S(2)}) async-start(bf16[8,64,4096]{2,1,0:T(8,128)(2,1)} %bitcast.77), calls=%async_computation.3 | async-start | bytes 8388608 | tf_op jit(solution)/shard_map/all_to_all | solution.py:78
  338.5 3.5 fusion.10
  342.0 2.0 fusion.4
  344.0 0.6 pad_maximum_fusion.1
  344.6 87.9 %all-to-all-done.3 = bf16[8,64,4096]{2,1,0:T(8,128)(2,1)} async-done(((bf16[8,64,4096]{2,1,0:T(8,128)(2,1)}), bf16[8,64,4096]{2,1,0:T(8,128)(2,1)}, u32[]{:S(2)}, u32[]{:S(2)}) %all-to-all-start.3) | async-done | bytes 4194336 | tf_op jit(solution)/shard_map/all_to_all | solution.py:78
  432.5 3.5 fusion.9
  436.0 1.2 fusion.6
  437.1 3.9 slice_bitcast_fusion
  (40 shorter events, 1.8 us)
Async XLA Ops:
  7.2 3.2 copy-start
  13.6 6.5 %copy-start.6 = (f32[128,2]{0,1:T(2,128)S(1)}, f32[128,2]{0,1:T(2,128)}, u32[]{:S(2)}) copy-start(f32[128,2]{0,1:T(2,128)} %param.11) | copy-start | bytes 3076
  13.6 6.6 %copy-start.2 = (bf16[128,4096]{1,0:T(8,128)(2,1)S(1)}, bf16[128,4096]{1,0:T(8,128)(2,1)}, u32[]{:S(2)}) copy-start(bf16[128,4096]{1,0:T(8,128)(2,1)} %param.15) | copy-start | bytes 3145732
  13.6 100.6 %all-to-all-start = ((bf16[8,64,4096]{2,1,0:T(8,128)(2,1)}), bf16[8,64,4096]{2,1,0:T(8,128)(2,1)}, u32[]{:S(2)}, u32[]{:S(2)}) async-start(bf16[8,64,4096]{2,1,0:T(8,128)(2,1)} %bitcast.74), calls=%async_computation | async-start | bytes 8388608 | tf_op jit(solution)/shard_map/all_to_all | solution.py:39
  114.2 4.7 %copy-start.5 = (s32[128,2]{0,1:T(2,128)S(1)}, s32[128,2]{0,1:T(2,128)}, u32[]{:S(2)}) copy-start(s32[128,2]{0,1:T(2,128)} %param.10) | copy-start | bytes 3076
  114.2 98.7 %all-to-all-start.2 = ((bf16[8,64,4096]{2,1,0:T(8,128)(2,1)}), bf16[8,64,4096]{2,1,0:T(8,128)(2,1)}, u32[]{:S(2)}, u32[]{:S(2)}) async-start(bf16[8,64,4096]{2,1,0:T(8,128)(2,1)} %bitcast.73), calls=%async_computation.2 | async-start | bytes 8388608 | tf_op jit(solution)/shard_map/all_to_all | solution.py:41
  118.9 318.3 %reduce-scatter.3.cloned.1.call-start = ((), (), s32[]{:S(2)}) async-start(), calls=%async_computation.6 | async-start | bytes 15728640 | tf_op jit(solution)/shard_map/reduce_scatter | solution.py:101
  120.3 8.8 %copy-start.8 = (bf16[768,4096]{1,0:T(8,128)(2,1)S(1)}, bf16[768,4096]{1,0:T(8,128)(2,1)}, u32[]{:S(2)}) copy-start(bf16[768,4096]{1,0:T(8,128)(2,1)} %get-tuple-element.29) | copy-start | bytes 18874372 | tf_op jit(solution)/shard_map/conditional
  120.3 17.0 %slice-start.2 = ((s8[6291456]{0:T(1024)(128)(4,1)}), s8[4194304]{0:T(1024)(128)(4,1)S(1)}, s32[]{:S(2)}) async-start(s8[6291456]{0:T(1024)(128)(4,1)} %bitcast.88), calls=%async_computation.10 | async-start | bytes 8388608 | tf_op jit(solution)/shard_map/conditional
  129.1 8.2 %slice-start.3 = ((s8[6291456]{0:T(1024)(128)(4,1)}), s8[2097152]{0:T(1024)(128)(4,1)S(1)}, s32[]{:S(2)}) async-start(s8[6291456]{0:T(1024)(128)(4,1)} %bitcast.88), calls=%async_computation.11 | async-start | bytes 4194304 | tf_op jit(solution)/shard_map/conditional
  221.9 0.9 copy-start.3
  235.3 98.6 %all-to-all-start.1 = ((bf16[8,64,4096]{2,1,0:T(8,128)(2,1)}), bf16[8,64,4096]{2,1,0:T(8,128)(2,1)}, u32[]{:S(2)}, u32[]{:S(2)}) async-start(bf16[8,64,4096]{2,1,0:T(8,128)(2,1)} %bitcast.13), calls=%async_computation.1 | async-start | bytes 8388608 | tf_op jit(solution)/shard_map/all_to_all | solution.py:61
  239.9 201.2 %reduce-scatter.5.cloned.1.call-start = ((), (), s32[]{:S(2)}) async-start(), calls=%async_computation.7 | async-start | bytes 7864320 | tf_op jit(solution)/shard_map/reduce_scatter | solution.py:100
  249.5 5.6 %copy-start.4 = (bf16[512,768]{1,0:T(8,128)(2,1)S(1)}, bf16[512,768]{1,0:T(8,128)(2,1)}, u32[]{:S(2)}) copy-start(bf16[512,768]{1,0:T(8,128)(2,1)} %copy-done.3) | copy-start | bytes 2359300
  333.9 98.6 %all-to-all-start.3 = ((bf16[8,64,4096]{2,1,0:T(8,128)(2,1)}), bf16[8,64,4096]{2,1,0:T(8,128)(2,1)}, u32[]{:S(2)}, u32[]{:S(2)}) async-start(bf16[8,64,4096]{2,1,0:T(8,128)(2,1)} %bitcast.77), calls=%async_computation.3 | async-start | bytes 8388608 | tf_op jit(solution)/shard_map/all_to_all | solution.py:78
  435.9 5.1 %copy-start.1 = (bf16[128,4096]{1,0:T(8,128)(2,1)S(1)}, bf16[128,4096]{1,0:T(8,128)(2,1)}, u32[]{:S(2)}) copy-start(bf16[128,4096]{1,0:T(8,128)(2,1)} %param.9) | copy-start | bytes 3145732
Sparse Core Ops, SparseCore 0:
  235.4 119.6 reduce-scatter.2
  358.6 70.1 reduce-scatter.4

commit v4 on v3

--- a/solution.py
+++ b/solution.py
@@ -101,6 +101,9 @@
     gate_up_share = lax.psum_scatter(gate_up_term, "dp", scatter_dimension=0, tiled=True)
     gate_share = gate_up_share[:ff_share]
     up_share = gate_up_share[ff_share:]
+    back_grads, gate_share, up_share, down_share = lax.optimization_barrier(
+        (back_grads, gate_share, up_share, down_share)
+    )
     pick_onehot = hit.reshape(top_count * tok_count, slots).astype(jnp.bfloat16)
     with jax.named_scope("combine_rows"):
         picked_out = jnp.dot(

time: 449 us -> 449 us (level)
  waiting for transfers between devices: 319 us -> 314 us
    all_to_all x1, waiting for transfers between devices: 87.9 us -> 73.5 us  [per_device(): lax.all_to_all(row_grads.reshape(experts, capacity, model_width), 'expert...]
    reduce_scatter x1, waiting for transfers between devices: 0.01 us -> 11.1 us  [per_device(): lax.psum_scatter(gate_up_term, 'dp', scatter_dimension=0, tiled=True)]
  transfers between devices with their start and end apart: 6 -> 6, of which waited for: 4 -> 5; matrix products, arithmetic and copies ran while one was open for 14% -> 13% of each run, Pallas kernels for 0% -> 0%
where the time goes in v4:
time: 449 us; the launch traced here: 448 us
  waiting for transfers between devices  314 us (70%)
  matrix products  83.6 us (19%)
  starting transfers between devices  20.6 us (5%)
  between operations  14.9 us (3%)
  local copies, waits for them, and re-layouts  9.59 us (2%)
  other arithmetic  5.17 us (1%)
    all_to_all x1, waiting for transfers between devices, per_device(): lax.all_to_all(send_rows, 'expert', split_axis=0, concat_axis=0, tiled=True)  90.7 us
    all_to_all x1, waiting for transfers between devices, per_device(): lax.all_to_all(row_grads.reshape(experts, capacity, model_width), 'expert...  73.5 us
    all_to_all x1, waiting for transfers between devices, per_device(): lax.all_to_all(expert_out.reshape(experts, capacity, model_width), 'exper...  69.4 us
    all_to_all x1, waiting for transfers between devices, per_device(): lax.all_to_all(send_grads, 'expert', split_axis=0, concat_axis=0, tiled=T...  69.4 us
    dot_general x1, matrix products, per_device(): jnp.einsum('rf,rd->fd', gate_up_pre, in_rows, preferred_element_type=jnp....  11.8 us
    reduce_scatter x1, waiting for transfers between devices, per_device(): lax.psum_scatter(gate_up_term, 'dp', scatter_dimension=0, tiled=True)  11.1 us
    dot_general x1, matrix products, per_device(): grad_act = jnp.dot(out_grads, w_down.T, preferred_element_type=jnp.float32)  9.81 us
    dot_general x1, matrix products, per_device(): jnp.einsum('rf,rd->fd', activated, out_grads, preferred_element_type=jnp....  9.38 us
  transfers between devices with their start and end apart: 6, of which 5 were waited for; matrix products, arithmetic and copies ran while one was open for 13% of the time, Pallas kernels for 0%

profile of v4, /device:TPU:0, one launch (start us, length us, event | category | flops | bytes accessed | tf_op | source)
XLA Modules:
  0.0 448.2 jit_solution(4389721683912385611)
XLA Ops:
  7.2 0.9 copy.39
  8.4 0.6 reduce-window.6
  9.5 0.7 fusion.16
  10.3 3.3 convolution_convert_fusion
  13.6 6.5 %all-to-all-start = ((bf16[8,64,4096]{2,1,0:T(8,128)(2,1)}), bf16[8,64,4096]{2,1,0:T(8,128)(2,1)}, u32[]{:S(2)}, u32[]{:S(2)}) async-start(bf16[8,64,4096]{2,1,0:T(8,128)(2,1)} %bitcast.72), calls=%async_computation | async-start | bytes 8388608 | tf_op jit(solution)/shard_map/all_to_all | solution.py:39
  20.2 3.2 multiply_convert_fusion.2
  23.5 90.7 %all-to-all-done = bf16[8,64,4096]{2,1,0:T(8,128)(2,1)} async-done(((bf16[8,64,4096]{2,1,0:T(8,128)(2,1)}), bf16[8,64,4096]{2,1,0:T(8,128)(2,1)}, u32[]{:S(2)}, u32[]{:S(2)}) %all-to-all-start) | async-done | bytes 4194336 | tf_op jit(solution)/shard_map/all_to_all | solution.py:39
  114.2 4.7 %all-to-all-start.2 = ((bf16[8,64,4096]{2,1,0:T(8,128)(2,1)}), bf16[8,64,4096]{2,1,0:T(8,128)(2,1)}, u32[]{:S(2)}, u32[]{:S(2)}) async-start(bf16[8,64,4096]{2,1,0:T(8,128)(2,1)} %bitcast.71), calls=%async_computation.2 | async-start | bytes 8388608 | tf_op jit(solution)/shard_map/all_to_all | solution.py:41
  118.9 0.5 slice.42
  120.1 23.3 %conditional.2 = (f32[512,768]{1,0:T(8,128)}, f32[512,768]{1,0:T(8,128)}, f32[512,768]{1,0:T(8,128)}, bf16[512,768]{1,0:T(8,128)(2,1)}, bf16[512,4096]{1,0:T(8,128)(2,1)}) conditional(s32[]{:T(128)} %bitcast.5, (bf16[512,4096]{1,0:T(8,128)(2,1)}, bf16[768,4096]{1,0:T(8,128)(2,1)}, bf16[768,4096]{1,0:T(8,128)(2,1)}, ...), branch_computations={%region_5.6_spmd, %region_6.7_spmd} | conditional | flops 9666035712 | bytes 83361904
  120.3 8.8 %fusion.26 = f32[512,768]{1,0:T(8,128)} fusion(bf16[512,4096]{1,0:T(8,128)(2,1)} %get-tuple-element.27, bf16[768,4096]{1,0:T(8,128)(2,1)} %get-tuple-element.28), kind=kOutput, calls=%fused_computation.53 | convolution fusion | flops 3221225472 | bytes 12058624 | tf_op jit(solution)/shard_map/cond/branch_1_fun/dot_general | solution.py:48
  129.1 8.2 %multiply_multiply_fusion.1 = (bf16[512,768]{1,0:T(8,128)(2,1)}, f32[512,768]{1,0:T(8,128)}, f32[512,768]{1,0:T(8,128)}) fusion(f32[512,768]{1,0:T(8,128)} %fusion.26, bf16[512,4096]{1,0:T(8,128)(2,1)} %get-tuple-element.27, bf16[768,4096]{1,0:T(8,128)(2,1)S(1)} %copy-done.10), kind=kOutput, calls=%fused_computation.4 | convolution fusion | flops 3223584768 | bytes 15990784 | tf_op jit(solution)/shard_map/cond/branch_1_fun/dot_general | solution.py:49
  137.3 6.1 %fusion.27 = bf16[512,4096]{1,0:T(8,128)(2,1)} fusion(bf16[512,768]{1,0:T(8,128)(2,1)} %get-tuple-element.85, bf16[768,4096]{1,0:T(8,128)(2,1)S(1)} %bitcast.89), kind=kOutput, calls=%fused_computation.54 | convolution fusion | flops 3221225472 | bytes 11272192 | tf_op jit(solution)/shard_map/cond/branch_1_fun/dot_general | solution.py:52
  143.5 69.4 %all-to-all-done.2 = bf16[8,64,4096]{2,1,0:T(8,128)(2,1)} async-done(((bf16[8,64,4096]{2,1,0:T(8,128)(2,1)}), bf16[8,64,4096]{2,1,0:T(8,128)(2,1)}, u32[]{:S(2)}, u32[]{:S(2)}) %all-to-all-start.2) | async-done | bytes 4194336 | tf_op jit(solution)/shard_map/all_to_all | solution.py:41
  212.9 9.8 %multiply_convert_fusion.3 = (bf16[512,768]{1,0:T(8,128)(2,1)S(1)}, bf16[512,768]{1,0:T(8,128)(2,1)}) fusion(f32[512,768]{1,0:T(8,128)} %get-tuple-element.52, f32[512,768]{1,0:T(8,128)} %get-tuple-element.53, f32[512,768]{1,0:T(8,128)} %get-tuple-element.51, bf16[512,4096]{1,0:T(8,128)(2,1)} %bitcast.16, bf16[1,768,4096]{2,1,0:T(8,128)(2,1)} %param.14), kind=kOutput, calls=%fused_computation.21 | convolution fusion | flops 3225157632 | bytes 16777216 | tf_op jit(solution)/shard_map/dot_general | solution.py:69
  223.0 0.6 copy-done.5
  223.6 1.4 copy.42
  225.3 11.8 %multiply_convert_fusion = bf16[1536,4096]{1,0:T(8,128)(2,1)} fusion(bf16[512,1536]{0,1:T(8,128)(2,1)S(1)} %bitcast.78, bf16[512,4096]{1,0:T(8,128)(2,1)} %bitcast.9), kind=kOutput, calls=%fused_computation.8 | convolution fusion | flops 6455033856 | bytes 18350080 | tf_op jit(solution)/shard_map/weight_grads/rf,rd->fd/dot_general | solution.py:98
  237.2 4.6 %all-to-all-start.1 = ((bf16[8,64,4096]{2,1,0:T(8,128)(2,1)}), bf16[8,64,4096]{2,1,0:T(8,128)(2,1)}, u32[]{:S(2)}, u32[]{:S(2)}) async-start(bf16[8,64,4096]{2,1,0:T(8,128)(2,1)} %bitcast.13), calls=%async_computation.1 | async-start | bytes 8388608 | tf_op jit(solution)/shard_map/all_to_all | solution.py:61
  242.0 9.4 %multiply_convert_fusion.1 = bf16[768,4096]{1,0:T(8,128)(2,1)} fusion(bf16[512,4096]{1,0:T(8,128)(2,1)} %bitcast.16, bf16[512,768]{1,0:T(8,128)(2,1)} %get-tuple-element.54), kind=kOutput, calls=%fused_computation.9 | convolution fusion | flops 3227516928 | bytes 11272192 | tf_op jit(solution)/shard_map/weight_grads/rf,rd->fd/dot_general | solution.py:88
  251.4 1.1 copy-done.4
  252.5 5.6 %fusion.21 = f32[512,4096]{1,0:T(8,128)S(1)} fusion(bf16[512,768]{1,0:T(8,128)(2,1)S(1)} %copy-done.4, bf16[1,768,4096]{2,1,0:T(8,128)(2,1)} %param.12), kind=kOutput, calls=%fused_computation.48 | convolution fusion | flops 3221225472 | bytes 15466496 | tf_op jit(solution)/shard_map/dot_general | solution.py:75
  258.1 8.2 %add_convert_fusion = bf16[512,4096]{1,0:T(8,128)(2,1)} fusion(f32[512,4096]{1,0:T(8,128)S(1)} %fusion.21, bf16[512,768]{1,0:T(8,128)(2,1)S(1)} %copy-done.6, bf16[1,768,4096]{2,1,0:T(8,128)(2,1)} %param.13), kind=kOutput, calls=%fused_computation.10 | convolution fusion | flops 3225419776 | bytes 19660800 | tf_op jit(solution)/shard_map/dot_general | solution.py:76
  266.3 69.4 %all-to-all-done.1 = bf16[8,64,4096]{2,1,0:T(8,128)(2,1)} async-done(((bf16[8,64,4096]{2,1,0:T(8,128)(2,1)}), bf16[8,64,4096]{2,1,0:T(8,128)(2,1)}, u32[]{:S(2)}, u32[]{:S(2)}) %all-to-all-start.1) | async-done | bytes 4194336 | tf_op jit(solution)/shard_map/all_to_all | solution.py:61
  335.8 4.6 %all-to-all-start.3 = ((bf16[8,64,4096]{2,1,0:T(8,128)(2,1)}), bf16[8,64,4096]{2,1,0:T(8,128)(2,1)}, u32[]{:S(2)}, u32[]{:S(2)}) async-start(bf16[8,64,4096]{2,1,0:T(8,128)(2,1)} %bitcast.75), calls=%async_computation.3 | async-start | bytes 8388608 | tf_op jit(solution)/shard_map/all_to_all | solution.py:78
  340.3 5.6 %fusion.10 = f32[256,4096]{1,0:T(8,128)} fusion(bf16[512,4096]{1,0:T(8,128)(2,1)} %bitcast.14, s32[256]{0:T(256)S(1)} %get-tuple-element.72), kind=kOutput, calls=%fused_computation.29 | convolution fusion | flops 1073872896 | bytes 8389632 | tf_op jit(solution)/shard_map/combine_rows/dot_general | solution.py:109
  345.9 11.1 %reduce-scatter.3.cloned.1.call-done = bf16[384,4096]{1,0:T(8,128)(2,1)} async-done(((bf16[1536,4096]{1,0:T(8,128)(2,1)}), bf16[384,4096]{1,0:T(8,128)(2,1)}) %reduce-scatter.3.cloned.1.call-update) | async-done | bytes 3145744 | tf_op jit(solution)/shard_map/reduce_scatter | solution.py:101
  357.0 3.9 fusion.23
  360.9 73.5 %all-to-all-done.3 = bf16[8,64,4096]{2,1,0:T(8,128)(2,1)} async-done(((bf16[8,64,4096]{2,1,0:T(8,128)(2,1)}), bf16[8,64,4096]{2,1,0:T(8,128)(2,1)}, u32[]{:S(2)}, u32[]{:S(2)}) %all-to-all-start.3) | async-done | bytes 4194336 | tf_op jit(solution)/shard_map/all_to_all | solution.py:78
  434.3 3.6 fusion.9
  438.0 2.8 fusion.4
  440.8 0.6 pad_maximum_fusion.1
  (43 shorter events, 2.1 us)
Async XLA Ops:
  7.2 3.2 copy-start
  13.6 6.5 %copy-start.8 = (f32[128,2]{0,1:T(2,128)S(1)}, f32[128,2]{0,1:T(2,128)}, u32[]{:S(2)}) copy-start(f32[128,2]{0,1:T(2,128)} %param.11) | copy-start | bytes 3076
  13.6 6.6 %copy-start.3 = (bf16[128,4096]{1,0:T(8,128)(2,1)S(1)}, bf16[128,4096]{1,0:T(8,128)(2,1)}, u32[]{:S(2)}) copy-start(bf16[128,4096]{1,0:T(8,128)(2,1)} %param.15) | copy-start | bytes 3145732
  13.6 100.6 %all-to-all-start = ((bf16[8,64,4096]{2,1,0:T(8,128)(2,1)}), bf16[8,64,4096]{2,1,0:T(8,128)(2,1)}, u32[]{:S(2)}, u32[]{:S(2)}) async-start(bf16[8,64,4096]{2,1,0:T(8,128)(2,1)} %bitcast.72), calls=%async_computation | async-start | bytes 8388608 | tf_op jit(solution)/shard_map/all_to_all | solution.py:39
  114.2 4.7 %copy-start.7 = (s32[128,2]{0,1:T(2,128)S(1)}, s32[128,2]{0,1:T(2,128)}, u32[]{:S(2)}) copy-start(s32[128,2]{0,1:T(2,128)} %param.10) | copy-start | bytes 3076
  114.2 98.7 %all-to-all-start.2 = ((bf16[8,64,4096]{2,1,0:T(8,128)(2,1)}), bf16[8,64,4096]{2,1,0:T(8,128)(2,1)}, u32[]{:S(2)}, u32[]{:S(2)}) async-start(bf16[8,64,4096]{2,1,0:T(8,128)(2,1)} %bitcast.71), calls=%async_computation.2 | async-start | bytes 8388608 | tf_op jit(solution)/shard_map/all_to_all | solution.py:41
  118.9 238.1 %reduce-scatter.3.cloned.1.call-start = ((), (), s32[]{:S(2)}) async-start(), calls=%async_computation.6 | async-start | bytes 15728640 | tf_op jit(solution)/shard_map/reduce_scatter | solution.py:101
  120.3 8.8 %copy-start.10 = (bf16[768,4096]{1,0:T(8,128)(2,1)S(1)}, bf16[768,4096]{1,0:T(8,128)(2,1)}, u32[]{:S(2)}) copy-start(bf16[768,4096]{1,0:T(8,128)(2,1)} %get-tuple-element.29) | copy-start | bytes 18874372 | tf_op jit(solution)/shard_map/conditional
  120.3 17.0 %slice-start.2 = ((s8[6291456]{0:T(1024)(128)(4,1)}), s8[4194304]{0:T(1024)(128)(4,1)S(1)}, s32[]{:S(2)}) async-start(s8[6291456]{0:T(1024)(128)(4,1)} %bitcast.88), calls=%async_computation.10 | async-start | bytes 8388608 | tf_op jit(solution)/shard_map/conditional
  129.1 8.2 %slice-start.3 = ((s8[6291456]{0:T(1024)(128)(4,1)}), s8[2097152]{0:T(1024)(128)(4,1)S(1)}, s32[]{:S(2)}) async-start(s8[6291456]{0:T(1024)(128)(4,1)} %bitcast.88), calls=%async_computation.11 | async-start | bytes 4194304 | tf_op jit(solution)/shard_map/conditional
  222.7 0.9 copy-start.5
  237.2 98.6 %all-to-all-start.1 = ((bf16[8,64,4096]{2,1,0:T(8,128)(2,1)}), bf16[8,64,4096]{2,1,0:T(8,128)(2,1)}, u32[]{:S(2)}, u32[]{:S(2)}) async-start(bf16[8,64,4096]{2,1,0:T(8,128)(2,1)} %bitcast.13), calls=%async_computation.1 | async-start | bytes 8388608 | tf_op jit(solution)/shard_map/all_to_all | solution.py:61
  241.8 192.6 %reduce-scatter.5.cloned.1.call-start = ((), (), s32[]{:S(2)}) async-start(), calls=%async_computation.7 | async-start | bytes 7864320 | tf_op jit(solution)/shard_map/reduce_scatter | solution.py:100
  251.4 1.1 copy-start.4
  252.5 5.6 %copy-start.6 = (bf16[512,768]{1,0:T(8,128)(2,1)S(1)}, bf16[512,768]{1,0:T(8,128)(2,1)}, u32[]{:S(2)}) copy-start(bf16[512,768]{1,0:T(8,128)(2,1)} %copy-done.5) | copy-start | bytes 2359300
  335.8 98.6 %all-to-all-start.3 = ((bf16[8,64,4096]{2,1,0:T(8,128)(2,1)}), bf16[8,64,4096]{2,1,0:T(8,128)(2,1)}, u32[]{:S(2)}, u32[]{:S(2)}) async-start(bf16[8,64,4096]{2,1,0:T(8,128)(2,1)} %bitcast.75), calls=%async_computation.3 | async-start | bytes 8388608 | tf_op jit(solution)/shard_map/all_to_all | solution.py:78
  434.3 3.7 copy-start.2
  438.0 3.4 copy-start.1
Sparse Core Ops, SparseCore 0:
  237.3 119.6 reduce-scatter.2
  360.5 70.1 reduce-scatter.4

commit v5 on v3

--- a/solution.py
+++ b/solution.py
@@ -114,6 +114,9 @@
         grad_combine = jnp.stack(
             [jnp.sum(grad_f32 * picked_out[k], axis=1) for k in range(top_count)], axis=1
         )
+        back_grads, gate_share, up_share, mixed, grad_combine = lax.optimization_barrier(
+            (back_grads, gate_share, up_share, mixed, grad_combine)
+        )
         picked_grads = jnp.dot(
             pick_onehot, back_grads.reshape(slots, model_width), preferred_element_type=jnp.float32
         ).reshape(top_count, tok_count, model_width)

time: 449 us -> 445 us (level)
    all_to_all x1, waiting for transfers between devices: 87.9 us -> 73.5 us  [per_device(): lax.all_to_all(row_grads.reshape(experts, capacity, model_width), 'expert...]
    reduce_scatter x1, waiting for transfers between devices: 0.01 us -> 10.5 us  [per_device(): lax.psum_scatter(gate_up_term, 'dp', scatter_dimension=0, tiled=True)]
  transfers between devices with their start and end apart: 6 -> 6, of which waited for: 4 -> 5; matrix products, arithmetic and copies ran while one was open for 14% -> 15% of each run, Pallas kernels for 0% -> 0%
where the time goes in v5:
time: 445 us; the launch traced here: 444 us
  waiting for transfers between devices  315 us (71%)
  matrix products  80.5 us (18%)
  starting transfers between devices  20.6 us (5%)
  between operations  14.9 us (3%)
  local copies, waits for them, and re-layouts  7.34 us (2%)
  other arithmetic  5.62 us (1%)
    all_to_all x1, waiting for transfers between devices, per_device(): lax.all_to_all(send_rows, 'expert', split_axis=0, concat_axis=0, tiled=True)  90.7 us
    all_to_all x1, waiting for transfers between devices, per_device(): lax.all_to_all(row_grads.reshape(experts, capacity, model_width), 'expert...  73.5 us
    all_to_all x1, waiting for transfers between devices, per_device(): lax.all_to_all(expert_out.reshape(experts, capacity, model_width), 'exper...  70.7 us
    all_to_all x1, waiting for transfers between devices, per_device(): lax.all_to_all(send_grads, 'expert', split_axis=0, concat_axis=0, tiled=T...  69.5 us
    dot_general x1, matrix products, per_device(): jnp.einsum('rf,rd->fd', gate_up_pre, in_rows, preferred_element_type=jnp....  11.9 us
    reduce_scatter x1, waiting for transfers between devices, per_device(): lax.psum_scatter(gate_up_term, 'dp', scatter_dimension=0, tiled=True)  10.5 us
    dot_general x1, matrix products, per_device(): jnp.einsum('rf,rd->fd', activated, out_grads, preferred_element_type=jnp....  9.37 us
    dot_general x1, matrix products, per_device(): grad_act = jnp.dot(out_grads, w_down.T, preferred_element_type=jnp.float32)  9.04 us
  transfers between devices with their start and end apart: 6, of which 5 were waited for; matrix products, arithmetic and copies ran while one was open for 15% of the time, Pallas kernels for 0%

profile of v5, /device:TPU:0, one launch (start us, length us, event | category | flops | bytes accessed | tf_op | source)
XLA Modules:
  0.0 444.1 jit_solution(5403019087634908775)
XLA Ops:
  7.2 0.9 copy.39
  8.4 0.6 reduce-window.6
  9.5 0.7 fusion.16
  10.3 3.3 convolution_convert_fusion
  13.6 6.5 %all-to-all-start = ((bf16[8,64,4096]{2,1,0:T(8,128)(2,1)}), bf16[8,64,4096]{2,1,0:T(8,128)(2,1)}, u32[]{:S(2)}, u32[]{:S(2)}) async-start(bf16[8,64,4096]{2,1,0:T(8,128)(2,1)} %bitcast.72), calls=%async_computation | async-start | bytes 8388608 | tf_op jit(solution)/shard_map/all_to_all | solution.py:39
  20.2 3.3 multiply_convert_fusion.2
  23.5 90.7 %all-to-all-done = bf16[8,64,4096]{2,1,0:T(8,128)(2,1)} async-done(((bf16[8,64,4096]{2,1,0:T(8,128)(2,1)}), bf16[8,64,4096]{2,1,0:T(8,128)(2,1)}, u32[]{:S(2)}, u32[]{:S(2)}) %all-to-all-start) | async-done | bytes 4194336 | tf_op jit(solution)/shard_map/all_to_all | solution.py:39
  114.2 4.7 %all-to-all-start.1 = ((bf16[8,64,4096]{2,1,0:T(8,128)(2,1)}), bf16[8,64,4096]{2,1,0:T(8,128)(2,1)}, u32[]{:S(2)}, u32[]{:S(2)}) async-start(bf16[8,64,4096]{2,1,0:T(8,128)(2,1)} %bitcast.71), calls=%async_computation.1 | async-start | bytes 8388608 | tf_op jit(solution)/shard_map/all_to_all | solution.py:41
  118.9 0.5 slice.41
  120.1 23.3 %conditional.2 = (f32[512,768]{1,0:T(8,128)}, f32[512,768]{1,0:T(8,128)}, f32[512,768]{1,0:T(8,128)}, bf16[512,768]{1,0:T(8,128)(2,1)}, bf16[512,4096]{1,0:T(8,128)(2,1)}) conditional(s32[]{:T(128)} %bitcast.8, (bf16[512,4096]{1,0:T(8,128)(2,1)}, bf16[768,4096]{1,0:T(8,128)(2,1)}, bf16[768,4096]{1,0:T(8,128)(2,1)}, ...), branch_computations={%region_5.6_spmd, %region_6.7_spmd} | conditional | flops 9666035712 | bytes 83361904
  120.3 8.8 %fusion.26 = f32[512,768]{1,0:T(8,128)} fusion(bf16[512,4096]{1,0:T(8,128)(2,1)} %get-tuple-element.27, bf16[768,4096]{1,0:T(8,128)(2,1)} %get-tuple-element.28), kind=kOutput, calls=%fused_computation.53 | convolution fusion | flops 3221225472 | bytes 12058624 | tf_op jit(solution)/shard_map/cond/branch_1_fun/dot_general | solution.py:48
  129.1 8.2 %multiply_multiply_fusion.1 = (bf16[512,768]{1,0:T(8,128)(2,1)}, f32[512,768]{1,0:T(8,128)}, f32[512,768]{1,0:T(8,128)}) fusion(f32[512,768]{1,0:T(8,128)} %fusion.26, bf16[512,4096]{1,0:T(8,128)(2,1)} %get-tuple-element.27, bf16[768,4096]{1,0:T(8,128)(2,1)S(1)} %copy-done.8), kind=kOutput, calls=%fused_computation.4 | convolution fusion | flops 3223584768 | bytes 15990784 | tf_op jit(solution)/shard_map/cond/branch_1_fun/dot_general | solution.py:49
  137.3 6.1 %fusion.27 = bf16[512,4096]{1,0:T(8,128)(2,1)} fusion(bf16[512,768]{1,0:T(8,128)(2,1)} %get-tuple-element.86, bf16[768,4096]{1,0:T(8,128)(2,1)S(1)} %bitcast.89), kind=kOutput, calls=%fused_computation.54 | convolution fusion | flops 3221225472 | bytes 11272192 | tf_op jit(solution)/shard_map/cond/branch_1_fun/dot_general | solution.py:52
  143.4 69.5 %all-to-all-done.1 = bf16[8,64,4096]{2,1,0:T(8,128)(2,1)} async-done(((bf16[8,64,4096]{2,1,0:T(8,128)(2,1)}), bf16[8,64,4096]{2,1,0:T(8,128)(2,1)}, u32[]{:S(2)}, u32[]{:S(2)}) %all-to-all-start.1) | async-done | bytes 4194336 | tf_op jit(solution)/shard_map/all_to_all | solution.py:41
  212.9 9.0 %multiply_convert_fusion.3 = (bf16[512,768]{1,0:T(8,128)(2,1)S(1)}, bf16[512,768]{1,0:T(8,128)(2,1)S(1)}) fusion(f32[512,768]{1,0:T(8,128)} %get-tuple-element.52, f32[512,768]{1,0:T(8,128)} %get-tuple-element.53, f32[512,768]{1,0:T(8,128)} %get-tuple-element.51, bf16[512,4096]{1,0:T(8,128)(2,1)} %bitcast.6, bf16[1,768,4096]{2,1,0:T(8,128)(2,1)} %param.14), kind=kOutput, calls=%fused_computation.21 | convolution fusion | flops 3225157632 | bytes 16777216 | tf_op jit(solution)/shard_map/dot_general | solution.py:69
  221.9 0.3 copy.43
  222.2 0.6 copy-done.3
  223.4 11.9 %multiply_convert_fusion = bf16[1536,4096]{1,0:T(8,128)(2,1)} fusion(bf16[512,1536]{0,1:T(8,128)(2,1)S(1)} %bitcast.78, bf16[512,4096]{1,0:T(8,128)(2,1)} %bitcast.9), kind=kOutput, calls=%fused_computation.8 | convolution fusion | flops 6455033856 | bytes 18350080 | tf_op jit(solution)/shard_map/weight_grads/rf,rd->fd/dot_general | solution.py:98
  235.3 4.6 %all-to-all-start.3 = ((bf16[8,64,4096]{2,1,0:T(8,128)(2,1)}), bf16[8,64,4096]{2,1,0:T(8,128)(2,1)}, u32[]{:S(2)}, u32[]{:S(2)}) async-start(bf16[8,64,4096]{2,1,0:T(8,128)(2,1)} %bitcast.18), calls=%async_computation.4 | async-start | bytes 8388608 | tf_op jit(solution)/shard_map/all_to_all | solution.py:61
  240.2 9.4 %multiply_convert_fusion.1 = bf16[768,4096]{1,0:T(8,128)(2,1)} fusion(bf16[512,4096]{1,0:T(8,128)(2,1)} %bitcast.6, bf16[512,768]{1,0:T(8,128)(2,1)} %get-tuple-element.60), kind=kOutput, calls=%fused_computation.9 | convolution fusion | flops 3227516928 | bytes 11272192 | tf_op jit(solution)/shard_map/weight_grads/rf,rd->fd/dot_general | solution.py:88
  249.6 5.6 %fusion.19 = f32[512,4096]{1,0:T(8,128)S(1)} fusion(bf16[512,768]{1,0:T(8,128)(2,1)S(1)} %get-tuple-element.70, bf16[1,768,4096]{2,1,0:T(8,128)(2,1)} %param.12), kind=kOutput, calls=%fused_computation.46 | convolution fusion | flops 3221225472 | bytes 15466496 | tf_op jit(solution)/shard_map/dot_general | solution.py:75
  255.2 8.0 %add_convert_fusion = bf16[512,4096]{1,0:T(8,128)(2,1)} fusion(f32[512,4096]{1,0:T(8,128)S(1)} %fusion.19, bf16[512,768]{1,0:T(8,128)(2,1)S(1)} %copy-done.4, bf16[1,768,4096]{2,1,0:T(8,128)(2,1)} %param.13), kind=kOutput, calls=%fused_computation.10 | convolution fusion | flops 3225419776 | bytes 19660800 | tf_op jit(solution)/shard_map/dot_general | solution.py:76
  263.2 70.7 %all-to-all-done.3 = bf16[8,64,4096]{2,1,0:T(8,128)(2,1)} async-done(((bf16[8,64,4096]{2,1,0:T(8,128)(2,1)}), bf16[8,64,4096]{2,1,0:T(8,128)(2,1)}, u32[]{:S(2)}, u32[]{:S(2)}) %all-to-all-start.3) | async-done | bytes 4194336 | tf_op jit(solution)/shard_map/all_to_all | solution.py:61
  333.9 4.6 %all-to-all-start.2 = ((bf16[8,64,4096]{2,1,0:T(8,128)(2,1)}), bf16[8,64,4096]{2,1,0:T(8,128)(2,1)}, u32[]{:S(2)}, u32[]{:S(2)}) async-start(bf16[8,64,4096]{2,1,0:T(8,128)(2,1)} %bitcast.75), calls=%async_computation.2 | async-start | bytes 8388608 | tf_op jit(solution)/shard_map/all_to_all | solution.py:78
  338.5 3.5 fusion.9
  342.0 2.0 fusion.4
  344.0 0.6 pad_maximum_fusion.1
  344.6 10.5 %reduce-scatter.3.cloned.1.call-done = bf16[384,4096]{1,0:T(8,128)(2,1)} async-done(((bf16[1536,4096]{1,0:T(8,128)(2,1)}), bf16[384,4096]{1,0:T(8,128)(2,1)}) %reduce-scatter.3.cloned.1.call-update) | async-done | bytes 3145744 | tf_op jit(solution)/shard_map/reduce_scatter | solution.py:101
  355.1 3.9 fusion.23
  359.0 73.5 %all-to-all-done.2 = bf16[8,64,4096]{2,1,0:T(8,128)(2,1)} async-done(((bf16[8,64,4096]{2,1,0:T(8,128)(2,1)}), bf16[8,64,4096]{2,1,0:T(8,128)(2,1)}, u32[]{:S(2)}, u32[]{:S(2)}) %all-to-all-start.2) | async-done | bytes 4194336 | tf_op jit(solution)/shard_map/all_to_all | solution.py:78
  432.5 3.6 fusion.8
  436.0 1.2 fusion.6
  (40 shorter events, 2.1 us)
Async XLA Ops:
  7.2 3.2 copy-start
  13.6 6.5 %copy-start.6 = (f32[128,2]{0,1:T(2,128)S(1)}, f32[128,2]{0,1:T(2,128)}, u32[]{:S(2)}) copy-start(f32[128,2]{0,1:T(2,128)} %param.11) | copy-start | bytes 3076
  13.6 6.6 %copy-start.2 = (bf16[128,4096]{1,0:T(8,128)(2,1)S(1)}, bf16[128,4096]{1,0:T(8,128)(2,1)}, u32[]{:S(2)}) copy-start(bf16[128,4096]{1,0:T(8,128)(2,1)} %param.15) | copy-start | bytes 3145732
  13.6 100.6 %all-to-all-start = ((bf16[8,64,4096]{2,1,0:T(8,128)(2,1)}), bf16[8,64,4096]{2,1,0:T(8,128)(2,1)}, u32[]{:S(2)}, u32[]{:S(2)}) async-start(bf16[8,64,4096]{2,1,0:T(8,128)(2,1)} %bitcast.72), calls=%async_computation | async-start | bytes 8388608 | tf_op jit(solution)/shard_map/all_to_all | solution.py:39
  114.2 4.7 %copy-start.5 = (s32[128,2]{0,1:T(2,128)S(1)}, s32[128,2]{0,1:T(2,128)}, u32[]{:S(2)}) copy-start(s32[128,2]{0,1:T(2,128)} %param.10) | copy-start | bytes 3076
  114.2 98.7 %all-to-all-start.1 = ((bf16[8,64,4096]{2,1,0:T(8,128)(2,1)}), bf16[8,64,4096]{2,1,0:T(8,128)(2,1)}, u32[]{:S(2)}, u32[]{:S(2)}) async-start(bf16[8,64,4096]{2,1,0:T(8,128)(2,1)} %bitcast.71), calls=%async_computation.1 | async-start | bytes 8388608 | tf_op jit(solution)/shard_map/all_to_all | solution.py:41
  118.9 236.2 %reduce-scatter.3.cloned.1.call-start = ((), (), s32[]{:S(2)}) async-start(), calls=%async_computation.6 | async-start | bytes 15728640 | tf_op jit(solution)/shard_map/reduce_scatter | solution.py:101
  120.3 8.8 %copy-start.8 = (bf16[768,4096]{1,0:T(8,128)(2,1)S(1)}, bf16[768,4096]{1,0:T(8,128)(2,1)}, u32[]{:S(2)}) copy-start(bf16[768,4096]{1,0:T(8,128)(2,1)} %get-tuple-element.29) | copy-start | bytes 18874372 | tf_op jit(solution)/shard_map/conditional
  120.3 17.0 %slice-start.2 = ((s8[6291456]{0:T(1024)(128)(4,1)}), s8[4194304]{0:T(1024)(128)(4,1)S(1)}, s32[]{:S(2)}) async-start(s8[6291456]{0:T(1024)(128)(4,1)} %bitcast.88), calls=%async_computation.10 | async-start | bytes 8388608 | tf_op jit(solution)/shard_map/conditional
  129.1 8.2 %slice-start.3 = ((s8[6291456]{0:T(1024)(128)(4,1)}), s8[2097152]{0:T(1024)(128)(4,1)S(1)}, s32[]{:S(2)}) async-start(s8[6291456]{0:T(1024)(128)(4,1)} %bitcast.88), calls=%async_computation.11 | async-start | bytes 4194304 | tf_op jit(solution)/shard_map/conditional
  221.9 0.9 copy-start.3
  235.3 98.6 %all-to-all-start.3 = ((bf16[8,64,4096]{2,1,0:T(8,128)(2,1)}), bf16[8,64,4096]{2,1,0:T(8,128)(2,1)}, u32[]{:S(2)}, u32[]{:S(2)}) async-start(bf16[8,64,4096]{2,1,0:T(8,128)(2,1)} %bitcast.18), calls=%async_computation.4 | async-start | bytes 8388608 | tf_op jit(solution)/shard_map/all_to_all | solution.py:61
  239.9 197.3 %reduce-scatter.5.cloned.1.call-start = ((), (), s32[]{:S(2)}) async-start(), calls=%async_computation.7 | async-start | bytes 7864320 | tf_op jit(solution)/shard_map/reduce_scatter | solution.py:100
  249.5 5.6 %copy-start.4 = (bf16[512,768]{1,0:T(8,128)(2,1)S(1)}, bf16[512,768]{1,0:T(8,128)(2,1)}, u32[]{:S(2)}) copy-start(bf16[512,768]{1,0:T(8,128)(2,1)} %copy-done.3) | copy-start | bytes 2359300
  333.9 98.6 %all-to-all-start.2 = ((bf16[8,64,4096]{2,1,0:T(8,128)(2,1)}), bf16[8,64,4096]{2,1,0:T(8,128)(2,1)}, u32[]{:S(2)}, u32[]{:S(2)}) async-start(bf16[8,64,4096]{2,1,0:T(8,128)(2,1)} %bitcast.75), calls=%async_computation.2 | async-start | bytes 8388608 | tf_op jit(solution)/shard_map/all_to_all | solution.py:78
  432.5 4.8 %copy-start.1 = (bf16[128,4096]{1,0:T(8,128)(2,1)S(1)}, bf16[128,4096]{1,0:T(8,128)(2,1)}, u32[]{:S(2)}) copy-start(bf16[128,4096]{1,0:T(8,128)(2,1)} %param.9) | copy-start | bytes 3145732
Sparse Core Ops, SparseCore 0:
  235.4 119.6 reduce-scatter.2
  358.6 70.1 reduce-scatter.4

commit v6 on v5

--- a/solution.py
+++ b/solution.py
@@ -58,13 +58,17 @@
     gate_pre, up_pre, sigmoid_gate, activated, expert_out = lax.cond(
         always, forward, forward, in_rows
     )
-    back_out = lax.all_to_all(
-        expert_out.reshape(experts, capacity, model_width),
-        "expert",
-        split_axis=0,
-        concat_axis=0,
-        tiled=True,
-    )
+    me = lax.axis_index("expert")
+    expert_out, out_grads = lax.optimization_barrier((expert_out, out_grads))
+    back_out = []
+    for shift in range(experts):
+        chunk = lax.dynamic_slice_in_dim(expert_out, ((me + shift) % experts) * capacity, capacity, 0)
+        if shift:
+            chunk = lax.ppermute(
+                chunk, "expert", [(j, (j + shift) % experts) for j in range(experts)]
+            )
+        back_out.append(chunk)
+    back_out = jnp.concatenate(back_out, axis=0)
     scale = (tok_count * top_count * copies) ** (-0.5)
     grad_act = jnp.dot(out_grads, w_down.T, preferred_element_type=jnp.float32)
     grad_gate_pre = (
@@ -75,6 +79,7 @@
         jnp.dot(grad_gate_pre, w_gate, preferred_element_type=jnp.float32)
         + jnp.dot(grad_up_pre, w_up, preferred_element_type=jnp.float32)
     ).astype(jnp.bfloat16)
+    row_grads, back_out = lax.optimization_barrier((row_grads, back_out))
     back_grads = lax.all_to_all(
         row_grads.reshape(experts, capacity, model_width),
         "expert",
@@ -87,6 +92,9 @@
         down_term = (
             scale * jnp.einsum("rf,rd->fd", activated, out_grads, preferred_element_type=jnp.float32)
         ).astype(jnp.bfloat16)
+        down_term, grad_gate_pre, grad_up_pre = lax.optimization_barrier(
+            (down_term, grad_gate_pre, grad_up_pre)
+        )
         gate_up_pre = jnp.stack(
             [
                 grad_gate_pre.reshape(slots, copies, ff_share),
@@ -103,9 +111,15 @@
     up_share = gate_up_share[ff_share:]
     pick_onehot = hit.reshape(top_count * tok_count, slots).astype(jnp.bfloat16)
     with jax.named_scope("combine_rows"):
-        picked_out = jnp.dot(
-            pick_onehot, back_out.reshape(slots, model_width), preferred_element_type=jnp.float32
-        ).reshape(top_count, tok_count, model_width)
+        shift_target = ((me - expert_ids) % experts) * capacity + target % capacity
+        shift_onehot = (
+            (shift_target.T[:, :, None] == slot_iota[None, None, :])
+            .reshape(top_count * tok_count, slots)
+            .astype(jnp.bfloat16)
+        )
+        picked_out = jnp.dot(shift_onehot, back_out, preferred_element_type=jnp.float32).reshape(
+            top_count, tok_count, model_width
+        )
         grad_f32 = grad_out.astype(jnp.float32)
         mixed = combine[:, 0:1] * picked_out[0]
         for k in range(1, top_count):

time: 445 us -> 458 us (1.029)
  waiting for transfers between devices: 315 us -> 297 us
  local copies, waits for them, and re-layouts: 7.34 us -> 23.4 us
  starting transfers between devices: 20.6 us -> 33.1 us
    all_to_all x1 -> x0, waiting for transfers between devices: 70.7 us -> none  [per_device(): lax.all_to_all(expert_out.reshape(experts, capacity, model_width), 'exper...]
    ppermute x0 -> x7, waiting for transfers between devices: none -> 51.5 us  [per_device(): lax.ppermute(chunk, 'expert', [(j, (j + shift) % experts) for j in range(...]
    ppermute x0 -> x7, starting transfers between devices: none -> 11.6 us  [per_device(): lax.ppermute(chunk, 'expert', [(j, (j + shift) % experts) for j in range(...]
    unnamed x15 -> x23, local copies, waits for them, and re-layouts: 1.5 us -> 11.3 us
    all_to_all x1, starting transfers between devices: 4.56 us -> 10.3 us  [per_device(): lax.all_to_all(row_grads.reshape(experts, capacity, model_width), 'expert...]
    all_to_all x1 -> x0, starting transfers between devices: 4.58 us -> none  [per_device(): lax.all_to_all(expert_out.reshape(experts, capacity, model_width), 'exper...]
  transfers between devices with their start and end apart: 6 -> 12, of which waited for: 5 -> 7; matrix products, arithmetic and copies ran while one was open for 15% -> 16% of each run, Pallas kernels for 0% -> 0%
where the time goes in v6:
time: 458 us; the launch traced here: 457 us
  waiting for transfers between devices  297 us (65%)
  matrix products  83 us (18%)
  starting transfers between devices  33.1 us (7%)
  local copies, waits for them, and re-layouts  23.4 us (5%)
  between operations  14.9 us (3%)
  other arithmetic  5.62 us (1%)
    all_to_all x1, waiting for transfers between devices, per_device(): lax.all_to_all(send_rows, 'expert', split_axis=0, concat_axis=0, tiled=True)  90.7 us
    all_to_all x1, waiting for transfers between devices, per_device(): lax.all_to_all(row_grads.reshape(experts, capacity, model_width), 'expert...  77.4 us
    all_to_all x1, waiting for transfers between devices, per_device(): lax.all_to_all(send_grads, 'expert', split_axis=0, concat_axis=0, tiled=T...  70.7 us
    ppermute x7, waiting for transfers between devices, per_device(): lax.ppermute(chunk, 'expert', [(j, (j + shift) % experts) for j in range(...  51.5 us
    dot_general x1, matrix products, per_device(): jnp.einsum('rf,rd->fd', gate_up_pre, in_rows, preferred_element_type=jnp....  11.8 us
    ppermute x7, starting transfers between devices, per_device(): lax.ppermute(chunk, 'expert', [(j, (j + shift) % experts) for j in range(...  11.6 us
    unnamed x23, local copies, waits for them, and re-layouts  11.3 us
    all_to_all x1, starting transfers between devices, per_device(): lax.all_to_all(row_grads.reshape(experts, capacity, model_width), 'expert...  10.3 us
  transfers between devices with their start and end apart: 12, of which 7 were waited for; matrix products, arithmetic and copies ran while one was open for 16% of the time, Pallas kernels for 0%

profile of v6, /device:TPU:0, one launch (start us, length us, event | category | flops | bytes accessed | tf_op | source)
XLA Modules:
  0.0 457.4 jit_solution(7400493731424712334)
XLA Ops:
  10.3 3.3 convolution_convert_fusion
  13.6 6.5 %all-to-all-start = ((bf16[8,64,4096]{2,1,0:T(8,128)(2,1)}), bf16[8,64,4096]{2,1,0:T(8,128)(2,1)}, u32[]{:S(2)}, u32[]{:S(2)}) async-start(bf16[8,64,4096]{2,1,0:T(8,128)(2,1)} %bitcast.74), calls=%async_computation | async-start | bytes 8388608 | tf_op jit(solution)/shard_map/all_to_all | solution.py:39
  20.2 3.2 multiply_convert_fusion.2
  23.5 90.7 %all-to-all-done = bf16[8,64,4096]{2,1,0:T(8,128)(2,1)} async-done(((bf16[8,64,4096]{2,1,0:T(8,128)(2,1)}), bf16[8,64,4096]{2,1,0:T(8,128)(2,1)}, u32[]{:S(2)}, u32[]{:S(2)}) %all-to-all-start) | async-done | bytes 4194336 | tf_op jit(solution)/shard_map/all_to_all | solution.py:39
  114.2 4.7 %all-to-all-start.1 = ((bf16[8,64,4096]{2,1,0:T(8,128)(2,1)}), bf16[8,64,4096]{2,1,0:T(8,128)(2,1)}, u32[]{:S(2)}, u32[]{:S(2)}) async-start(bf16[8,64,4096]{2,1,0:T(8,128)(2,1)} %bitcast.73), calls=%async_computation.1 | async-start | bytes 8388608 | tf_op jit(solution)/shard_map/all_to_all | solution.py:41
  120.1 22.1 %conditional.2 = (f32[512,768]{1,0:T(8,128)S(1)}, f32[512,768]{1,0:T(8,128)}, f32[512,768]{1,0:T(8,128)}, bf16[512,768]{1,0:T(8,128)(2,1)}, bf16[512,4096]{1,0:T(8,128)(2,1)}) conditional(s32[]{:T(128)} %bitcast, (bf16[512,4096]{1,0:T(8,128)(2,1)}, bf16[768,4096]{1,0:T(8,128)(2,1)}, bf16[768,4096]{1,0:T(8,128)(2,1)}, ...), branch_computations={%region_5.6_spmd, %region_6.7_spmd} | conditional | flops 9666035712 | bytes 95944872
  120.3 7.3 %fusion.31 = f32[512,768]{1,0:T(8,128)S(1)} fusion(bf16[512,4096]{1,0:T(8,128)(2,1)} %get-tuple-element.27, bf16[768,4096]{1,0:T(8,128)(2,1)} %get-tuple-element.28), kind=kOutput, calls=%fused_computation.80 | convolution fusion | flops 3221225472 | bytes 12058624 | tf_op jit(solution)/shard_map/cond/branch_1_fun/dot_general | solution.py:48
  127.6 8.2 %multiply_multiply_fusion.1 = (bf16[512,768]{1,0:T(8,128)(2,1)}, f32[512,768]{1,0:T(8,128)}, f32[512,768]{1,0:T(8,128)}) fusion(f32[512,768]{1,0:T(8,128)S(1)} %fusion.31, bf16[512,4096]{1,0:T(8,128)(2,1)} %get-tuple-element.27, bf16[768,4096]{1,0:T(8,128)(2,1)S(1)} %copy-done.9), kind=kOutput, calls=%fused_computation.4 | convolution fusion | flops 3223584768 | bytes 15990784 | tf_op jit(solution)/shard_map/cond/branch_1_fun/dot_general | solution.py:49
  135.9 6.3 %fusion.32 = bf16[512,4096]{1,0:T(8,128)(2,1)} fusion(bf16[512,768]{1,0:T(8,128)(2,1)} %get-tuple-element.109, bf16[768,4096]{1,0:T(8,128)(2,1)S(1)} %bitcast.91), kind=kOutput, calls=%fused_computation.81 | convolution fusion | flops 3221225472 | bytes 11272192 | tf_op jit(solution)/shard_map/cond/branch_1_fun/dot_general | solution.py:52
  142.2 70.7 %all-to-all-done.1 = bf16[8,64,4096]{2,1,0:T(8,128)(2,1)} async-done(((bf16[8,64,4096]{2,1,0:T(8,128)(2,1)}), bf16[8,64,4096]{2,1,0:T(8,128)(2,1)}, u32[]{:S(2)}, u32[]{:S(2)}) %all-to-all-start.1) | async-done | bytes 4194336 | tf_op jit(solution)/shard_map/all_to_all | solution.py:41
  212.9 8.6 %multiply_convert_fusion.1 = bf16[768,4096]{1,0:T(8,128)(2,1)} fusion(bf16[512,4096]{1,0:T(8,128)(2,1)} %bitcast.11, bf16[512,768]{1,0:T(8,128)(2,1)} %get-tuple-element.65), kind=kOutput, calls=%fused_computation.9 | convolution fusion | flops 3227516928 | bytes 11272192 | tf_op jit(solution)/shard_map/weight_grads/rf,rd->fd/dot_general | solution.py:93
  221.5 9.4 %multiply_convert_fusion.3 = (bf16[512,768]{1,0:T(8,128)(2,1)}, bf16[512,768]{1,0:T(8,128)(2,1)S(1)}) fusion(f32[512,768]{1,0:T(8,128)} %get-tuple-element.61, f32[512,768]{1,0:T(8,128)S(1)} %get-tuple-element.62, f32[512,768]{1,0:T(8,128)} %get-tuple-element.60, bf16[512,4096]{1,0:T(8,128)(2,1)} %bitcast.11, bf16[1,768,4096]{2,1,0:T(8,128)(2,1)} %param.14), kind=kOutput, calls=%fused_computation.21 | convolution fusion | flops 3225157632 | bytes 16777216 | tf_op jit(solution)/shard_map/dot_general | solution.py:73
  232.9 11.8 %multiply_convert_fusion = bf16[1536,4096]{1,0:T(8,128)(2,1)} fusion(bf16[512,1536]{0,1:T(8,128)(2,1)S(1)} %bitcast.80, bf16[512,4096]{1,0:T(8,128)(2,1)} %bitcast.7), kind=kOutput, calls=%fused_computation.8 | convolution fusion | flops 6455033856 | bytes 18350080 | tf_op jit(solution)/shard_map/weight_grads/rf,rd->fd/dot_general | solution.py:106
  244.9 4.2 constant_dynamic-slice_fusion
  250.4 1.7 collective-permute-start.1
  252.2 8.3 %fusion.24 = f32[512,4096]{1,0:T(8,128)} fusion(bf16[512,768]{1,0:T(8,128)(2,1)S(1)} %get-tuple-element.66, bf16[1,768,4096]{2,1,0:T(8,128)(2,1)} %param.12), kind=kOutput, calls=%fused_computation.73 | convolution fusion | flops 3221225472 | bytes 15466496 | tf_op jit(solution)/shard_map/dot_general | solution.py:79
  261.7 9.5 %add_convert_fusion = bf16[512,4096]{1,0:T(8,128)(2,1)} fusion(f32[512,4096]{1,0:T(8,128)} %fusion.24, bf16[512,768]{1,0:T(8,128)(2,1)S(1)} %copy-done.3, bf16[1,768,4096]{2,1,0:T(8,128)(2,1)} %param.13), kind=kOutput, calls=%fused_computation.10 | convolution fusion | flops 3225419776 | bytes 19660800 | tf_op jit(solution)/shard_map/dot_general | solution.py:80
  271.2 25.6 %collective-permute-done = bf16[64,4096]{1,0:T(8,128)(2,1)} collective-permute-done((bf16[64,4096]{1,0:T(8,128)(2,1)}, bf16[64,4096]{1,0:T(8,128)(2,1)}, u32[]{:S(2)}, u32[]{:S(2)}) %collective-permute-start) | collective-permute-done | bytes 524320 | tf_op jit(solution)/shard_map/ppermute | solution.py:67
  296.9 6.3 %collective-permute-start.2 = (bf16[64,4096]{1,0:T(8,128)(2,1)S(1)}, bf16[64,4096]{1,0:T(8,128)(2,1)S(1)}, u32[]{:S(2)}, u32[]{:S(2)}) collective-permute-start(bf16[64,4096]{1,0:T(8,128)(2,1)S(1)} %copy-done.5), channel_id=1, source_target_pairs={{0,3},{1,4},{2,5},{3,6},{4,7},{5,0},{6,1},{7,2},{8,11},{9,12},{10,... | collective-permute-start | bytes 1572872 | tf_op jit(solution)/shard_map/ppermute | solution.py:67
  303.1 1.9 constant_dynamic-update-slice_fusion.6
  305.0 2.2 collective-permute-start.3
  307.2 1.9 constant_dynamic-update-slice_fusion.5
  309.1 24.2 %collective-permute-done.2 = bf16[64,4096]{1,0:T(8,128)(2,1)S(1)} collective-permute-done((bf16[64,4096]{1,0:T(8,128)(2,1)S(1)}, bf16[64,4096]{1,0:T(8,128)(2,1)S(1)}, u32[]{:S(2)}, u32[]{:S(2)}) %collective-permute-start.2) | collective-permute-done | bytes 524320 | tf_op jit(solution)/shard_map/ppermute | solution.py:67
  336.6 1.9 constant_dynamic-update-slice_fusion.2
  338.6 2.0 constant_dynamic-update-slice_fusion.1
  341.3 10.3 %all-to-all-start.2 = ((bf16[8,64,4096]{2,1,0:T(8,128)(2,1)}), bf16[8,64,4096]{2,1,0:T(8,128)(2,1)}, u32[]{:S(2)}, u32[]{:S(2)}) async-start(bf16[8,64,4096]{2,1,0:T(8,128)(2,1)} %bitcast.77), calls=%async_computation.2 | async-start | bytes 8388608 | tf_op jit(solution)/shard_map/all_to_all | solution.py:83
  351.6 3.5 fusion.9
  355.2 2.0 fusion.4
  357.8 6.7 %reduce-scatter.3.cloned.1.call-done = bf16[384,4096]{1,0:T(8,128)(2,1)} async-done(((bf16[1536,4096]{1,0:T(8,128)(2,1)}), bf16[384,4096]{1,0:T(8,128)(2,1)}) %reduce-scatter.3.cloned.1.call-update) | async-done | bytes 3145744 | tf_op jit(solution)/shard_map/reduce_scatter | solution.py:109
  364.5 3.9 fusion.28
  368.4 77.4 %all-to-all-done.2 = bf16[8,64,4096]{2,1,0:T(8,128)(2,1)} async-done(((bf16[8,64,4096]{2,1,0:T(8,128)(2,1)}), bf16[8,64,4096]{2,1,0:T(8,128)(2,1)}, u32[]{:S(2)}, u32[]{:S(2)}) %all-to-all-start.2) | async-done | bytes 4194336 | tf_op jit(solution)/shard_map/all_to_all | solution.py:83
  445.8 3.6 fusion.10
  (66 shorter events, 14.5 us)
Async XLA Ops:
  7.2 3.2 copy-start
  13.6 6.5 %copy-start.7 = (f32[128,2]{0,1:T(2,128)S(1)}, f32[128,2]{0,1:T(2,128)}, u32[]{:S(2)}) copy-start(f32[128,2]{0,1:T(2,128)} %param.11) | copy-start | bytes 3076
  13.6 6.6 %copy-start.2 = (bf16[128,4096]{1,0:T(8,128)(2,1)S(1)}, bf16[128,4096]{1,0:T(8,128)(2,1)}, u32[]{:S(2)}) copy-start(bf16[128,4096]{1,0:T(8,128)(2,1)} %param.15) | copy-start | bytes 3145732
  13.6 100.6 %all-to-all-start = ((bf16[8,64,4096]{2,1,0:T(8,128)(2,1)}), bf16[8,64,4096]{2,1,0:T(8,128)(2,1)}, u32[]{:S(2)}, u32[]{:S(2)}) async-start(bf16[8,64,4096]{2,1,0:T(8,128)(2,1)} %bitcast.74), calls=%async_computation | async-start | bytes 8388608 | tf_op jit(solution)/shard_map/all_to_all | solution.py:39
  114.2 4.7 %copy-start.6 = (s32[128,2]{0,1:T(2,128)S(1)}, s32[128,2]{0,1:T(2,128)}, u32[]{:S(2)}) copy-start(s32[128,2]{0,1:T(2,128)} %param.10) | copy-start | bytes 3076
  114.2 98.7 %all-to-all-start.1 = ((bf16[8,64,4096]{2,1,0:T(8,128)(2,1)}), bf16[8,64,4096]{2,1,0:T(8,128)(2,1)}, u32[]{:S(2)}, u32[]{:S(2)}) async-start(bf16[8,64,4096]{2,1,0:T(8,128)(2,1)} %bitcast.73), calls=%async_computation.1 | async-start | bytes 8388608 | tf_op jit(solution)/shard_map/all_to_all | solution.py:41
  118.9 245.6 %reduce-scatter.3.cloned.1.call-start = ((), (), s32[]{:S(2)}) async-start(), calls=%async_computation.5 | async-start | bytes 15728640 | tf_op jit(solution)/shard_map/reduce_scatter | solution.py:109
  120.3 7.3 %copy-start.9 = (bf16[768,4096]{1,0:T(8,128)(2,1)S(1)}, bf16[768,4096]{1,0:T(8,128)(2,1)}, u32[]{:S(2)}) copy-start(bf16[768,4096]{1,0:T(8,128)(2,1)} %get-tuple-element.29) | copy-start | bytes 18874372 | tf_op jit(solution)/shard_map/conditional
  120.3 15.5 %slice-start.2 = ((s8[6291456]{0:T(1024)(128)(4,1)}), s8[4194304]{0:T(1024)(128)(4,1)S(1)}, s32[]{:S(2)}) async-start(s8[6291456]{0:T(1024)(128)(4,1)} %bitcast.90), calls=%async_computation.9 | async-start | bytes 8388608 | tf_op jit(solution)/shard_map/conditional
  127.6 8.2 %copy-start.10 = (f32[512,768]{1,0:T(8,128)}, f32[512,768]{1,0:T(8,128)S(1)}, u32[]{:S(2)}) copy-start(f32[512,768]{1,0:T(8,128)S(1)} %fusion.31) | copy-start | bytes 4718596 | tf_op jit(solution)/shard_map/conditional
  127.6 8.2 %slice-start.3 = ((s8[6291456]{0:T(1024)(128)(4,1)}), s8[2097152]{0:T(1024)(128)(4,1)S(1)}, s32[]{:S(2)}) async-start(s8[6291456]{0:T(1024)(128)(4,1)} %bitcast.90), calls=%async_computation.10 | async-start | bytes 4194304 | tf_op jit(solution)/shard_map/conditional
  135.8 6.4 %copy-start.11 = (f32[512,768]{1,0:T(8,128)S(1)}, f32[512,768]{1,0:T(8,128)}, u32[]{:S(2)}) copy-start(f32[512,768]{1,0:T(8,128)} %copy-done.10) | copy-start | bytes 4718596 | tf_op jit(solution)/shard_map/conditional
  244.7 205.8 %reduce-scatter.5.cloned.1.call-start = ((), (), s32[]{:S(2)}) async-start(), calls=%async_computation.6 | async-start | bytes 7864320 | tf_op jit(solution)/shard_map/reduce_scatter | solution.py:108
  249.1 91.4 %collective-permute-start.6 = (bf16[64,4096]{1,0:T(8,128)(2,1)}, bf16[64,4096]{1,0:T(8,128)(2,1)S(1)}, u32[]{:S(2)}, u32[]{:S(2)}) collective-permute-start(bf16[64,4096]{1,0:T(8,128)(2,1)} %get-tuple-element.86), channel_id=1, source_target_pairs={{0,7},{1,0},{2,1},{3,2},{4,3},{5,4},{6,5},{7,6},{8,15},{9,8},{10,9... | collective-permute-start | bytes 1572872 | tf_op jit(solution)/shard_map/ppermute | solution.py:67
  250.0 88.6 %collective-permute-start.5 = (bf16[64,4096]{1,0:T(8,128)(2,1)}, bf16[64,4096]{1,0:T(8,128)(2,1)}, u32[]{:S(2)}, u32[]{:S(2)}) collective-permute-start(bf16[64,4096]{1,0:T(8,128)(2,1)} %get-tuple-element.87), channel_id=1, source_target_pairs={{0,6},{1,7},{2,0},{3,1},{4,2},{5,3},{6,4},{7,5},{8,14},{9,15},{10,... | collective-permute-start | bytes 1572872 | tf_op jit(solution)/shard_map/ppermute | solution.py:67
  250.4 86.3 %collective-permute-start.4 = (bf16[64,4096]{1,0:T(8,128)(2,1)}, bf16[64,4096]{1,0:T(8,128)(2,1)}, u32[]{:S(2)}, u32[]{:S(2)}) collective-permute-start(bf16[64,4096]{1,0:T(8,128)(2,1)} %get-tuple-element.88), channel_id=1, source_target_pairs={{0,5},{1,6},{2,7},{3,0},{4,1},{5,2},{6,3},{7,4},{8,13},{9,14},{10,... | collective-permute-start | bytes 1572872 | tf_op jit(solution)/shard_map/ppermute | solution.py:67
  250.4 54.6 %collective-permute-start.1 = (bf16[64,4096]{1,0:T(8,128)(2,1)}, bf16[64,4096]{1,0:T(8,128)(2,1)}, u32[]{:S(2)}, u32[]{:S(2)}) collective-permute-start(bf16[64,4096]{1,0:T(8,128)(2,1)} %get-tuple-element.91), channel_id=1, source_target_pairs={{0,2},{1,3},{2,4},{3,5},{4,6},{5,7},{6,0},{7,1},{8,10},{9,11},{10,... | collective-permute-start | bytes 1572872 | tf_op jit(solution)/shard_map/ppermute | solution.py:67
  252.0 44.8 %collective-permute-start = (bf16[64,4096]{1,0:T(8,128)(2,1)}, bf16[64,4096]{1,0:T(8,128)(2,1)}, u32[]{:S(2)}, u32[]{:S(2)}) collective-permute-start(bf16[64,4096]{1,0:T(8,128)(2,1)} %get-tuple-element.92), channel_id=1, source_target_pairs={{0,1},{1,2},{2,3},{3,4},{4,5},{5,6},{6,7},{7,0},{8,9},{9,10},{10,1... | collective-permute-start | bytes 1572872 | tf_op jit(solution)/shard_map/ppermute | solution.py:67
  260.6 1.1 copy-start.3
  261.7 35.2 %copy-start.5 = (bf16[64,4096]{1,0:T(8,128)(2,1)S(1)}, bf16[64,4096]{1,0:T(8,128)(2,1)}, u32[]{:S(2)}) copy-start(bf16[64,4096]{1,0:T(8,128)(2,1)} %get-tuple-element.90) | copy-start | bytes 1572868
  261.7 43.3 %copy-start.4 = (bf16[64,4096]{1,0:T(8,128)(2,1)S(1)}, bf16[64,4096]{1,0:T(8,128)(2,1)}, u32[]{:S(2)}) copy-start(bf16[64,4096]{1,0:T(8,128)(2,1)} %get-tuple-element.89) | copy-start | bytes 1572868
  296.9 36.5 %collective-permute-start.2 = (bf16[64,4096]{1,0:T(8,128)(2,1)S(1)}, bf16[64,4096]{1,0:T(8,128)(2,1)S(1)}, u32[]{:S(2)}, u32[]{:S(2)}) collective-permute-start(bf16[64,4096]{1,0:T(8,128)(2,1)S(1)} %copy-done.5), channel_id=1, source_target_pairs={{0,3},{1,4},{2,5},{3,6},{4,7},{5,0},{6,1},{7,2},{8,11},{9,12},{10,... | collective-permute-start | bytes 1572872 | tf_op jit(solution)/shard_map/ppermute | solution.py:67
  305.0 30.8 %collective-permute-start.3 = (bf16[64,4096]{1,0:T(8,128)(2,1)S(1)}, bf16[64,4096]{1,0:T(8,128)(2,1)S(1)}, u32[]{:S(2)}, u32[]{:S(2)}) collective-permute-start(bf16[64,4096]{1,0:T(8,128)(2,1)S(1)} %copy-done.4), channel_id=1, source_target_pairs={{0,4},{1,5},{2,6},{3,7},{4,0},{5,1},{6,2},{7,3},{8,12},{9,13},{10,... | collective-permute-start | bytes 1572872 | tf_op jit(solution)/shard_map/ppermute | solution.py:67
  341.3 104.4 %all-to-all-start.2 = ((bf16[8,64,4096]{2,1,0:T(8,128)(2,1)}), bf16[8,64,4096]{2,1,0:T(8,128)(2,1)}, u32[]{:S(2)}, u32[]{:S(2)}) async-start(bf16[8,64,4096]{2,1,0:T(8,128)(2,1)} %bitcast.77), calls=%async_computation.2 | async-start | bytes 8388608 | tf_op jit(solution)/shard_map/all_to_all | solution.py:83
  445.8 4.8 %copy-start.1 = (bf16[128,4096]{1,0:T(8,128)(2,1)S(1)}, bf16[128,4096]{1,0:T(8,128)(2,1)}, u32[]{:S(2)}) copy-start(bf16[128,4096]{1,0:T(8,128)(2,1)} %param.9) | copy-start | bytes 3145732
Sparse Core Ops, SparseCore 0:
  244.8 119.6 reduce-scatter.2
  368.1 70.1 reduce-scatter.4

commit v7 on v2

--- a/solution.py
+++ b/solution.py
@@ -82,19 +82,25 @@
         concat_axis=0,
         tiled=True,
     )
+    ff_share = w_gate.shape[0] // copies
     with jax.named_scope("weight_grads"):
         down_term = (
             scale * jnp.einsum("rf,rd->fd", activated, out_grads, preferred_element_type=jnp.float32)
         ).astype(jnp.bfloat16)
-        gate_term = (
-            scale * jnp.einsum("rf,rd->fd", grad_gate_pre, in_rows, preferred_element_type=jnp.float32)
+        rows_all = lax.all_gather(in_rows, "dp", axis=0, tiled=True)
+        grads_pre = jnp.concatenate([grad_gate_pre, grad_up_pre], axis=1)
+        grads_all = lax.all_gather(grads_pre, "dp", axis=0, tiled=True)
+        me_dp = lax.axis_index("dp")
+        ff = w_gate.shape[0]
+        gate_cols = lax.dynamic_slice_in_dim(grads_all, me_dp * ff_share, ff_share, 1)
+        up_cols = lax.dynamic_slice_in_dim(grads_all, ff + me_dp * ff_share, ff_share, 1)
+        gate_share = (
+            scale * jnp.einsum("rf,rd->fd", gate_cols, rows_all, preferred_element_type=jnp.float32)
         ).astype(jnp.bfloat16)
-        up_term = (
-            scale * jnp.einsum("rf,rd->fd", grad_up_pre, in_rows, preferred_element_type=jnp.float32)
+        up_share = (
+            scale * jnp.einsum("rf,rd->fd", up_cols, rows_all, preferred_element_type=jnp.float32)
         ).astype(jnp.bfloat16)
     down_share = lax.psum_scatter(down_term, "dp", scatter_dimension=0, tiled=True)
-    gate_share = lax.psum_scatter(gate_term, "dp", scatter_dimension=0, tiled=True)
-    up_share = lax.psum_scatter(up_term, "dp", scatter_dimension=0, tiled=True)
     pick_onehot = hit.reshape(top_count * tok_count, slots).astype(jnp.bfloat16)
     with jax.named_scope("combine_rows"):
         picked_out = jnp.dot(
@@ -107,6 +113,9 @@
         mixed = mixed.astype(jnp.bfloat16)
         grad_combine = jnp.stack(
             [jnp.sum(grad_f32 * picked_out[k], axis=1) for k in range(top_count)], axis=1
+        )
+        back_grads, gate_share, up_share, mixed, grad_combine = lax.optimization_barrier(
+            (back_grads, gate_share, up_share, mixed, grad_combine)
         )
         picked_grads = jnp.dot(
             pick_onehot, back_grads.reshape(slots, model_width), preferred_element_type=jnp.float32

time: 454 us -> 540 us (1.19); the launches traced: 453 us -> 532 us
  waiting for transfers between devices: 327 us -> 401 us
    all_gather x0 -> x2, waiting for transfers between devices: none -> 118 us  [the longest x1 118 us: per_device(): rows_all = lax.all_gather(in_rows, 'dp', axis=0, tiled=True)]
    all_to_all x1, waiting for transfers between devices: 87.8 us -> 0.01 us  [per_device(): lax.all_to_all(row_grads.reshape(experts, capacity, model_width), 'expert...]
    reduce_scatter x1, waiting for transfers between devices: 6.18 us -> 50.6 us  [per_device(): lax.psum_scatter(down_term, 'dp', scatter_dimension=0, tiled=True)]
where the time goes in v7:
time: 540 us; the launch traced here: 532 us
  waiting for transfers between devices  401 us (74%)
  matrix products  85.8 us (16%)
  starting transfers between devices  20.8 us (4%)
  between operations  14.8 us (3%)
  other arithmetic  6.73 us (1%)
    all_gather x1, waiting for transfers between devices, per_device(): rows_all = lax.all_gather(in_rows, 'dp', axis=0, tiled=True)  118 us
    all_to_all x1, waiting for transfers between devices, per_device(): lax.all_to_all(send_rows, 'expert', split_axis=0, concat_axis=0, tiled=True)  90.7 us
    all_to_all x1, waiting for transfers between devices, per_device(): lax.all_to_all(expert_out.reshape(experts, capacity, model_width), 'exper...  71.1 us
    all_to_all x1, waiting for transfers between devices, per_device(): lax.all_to_all(send_grads, 'expert', split_axis=0, concat_axis=0, tiled=T...  69.2 us
    reduce_scatter x1, waiting for transfers between devices, per_device(): lax.psum_scatter(down_term, 'dp', scatter_dimension=0, tiled=True)  50.6 us
    dot_general x1, matrix products, per_device(): jnp.einsum('rf,rd->fd', up_cols, rows_all, preferred_element_type=jnp.flo...  11.2 us
  transfers between devices with their start and end apart: 7, of which 5 were waited for; matrix products, arithmetic and copies ran while one was open for 15% of the time, Pallas kernels for 0%

profile of v7, /device:TPU:0, one launch (start us, length us, event | category | flops | bytes accessed | tf_op | source)
XLA Modules:
  0.0 532.3 jit_solution(12989310316587515665)
XLA Ops:
  7.2 0.9 copy.30
  8.4 0.6 reduce-window.6
  9.5 0.7 fusion.22
  10.3 3.3 convolution_convert_fusion
  13.6 6.5 %all-to-all-start = ((bf16[8,64,4096]{2,1,0:T(8,128)(2,1)}), bf16[8,64,4096]{2,1,0:T(8,128)(2,1)}, u32[]{:S(2)}, u32[]{:S(2)}) async-start(bf16[8,64,4096]{2,1,0:T(8,128)(2,1)} %bitcast.69), calls=%async_computation | async-start | bytes 8388608 | tf_op jit(solution)/shard_map/all_to_all | solution.py:39
  20.2 3.3 multiply_convert_fusion.1
  23.5 90.7 %all-to-all-done = bf16[8,64,4096]{2,1,0:T(8,128)(2,1)} async-done(((bf16[8,64,4096]{2,1,0:T(8,128)(2,1)}), bf16[8,64,4096]{2,1,0:T(8,128)(2,1)}, u32[]{:S(2)}, u32[]{:S(2)}) %all-to-all-start) | async-done | bytes 4194336 | tf_op jit(solution)/shard_map/all_to_all | solution.py:39
  114.2 4.7 all-to-all-start.1
  120.1 23.6 %conditional.2 = (f32[512,768]{1,0:T(8,128)}, f32[512,768]{1,0:T(8,128)}, f32[512,768]{1,0:T(8,128)}, bf16[512,768]{1,0:T(8,128)(2,1)}, bf16[512,4096]{1,0:T(8,128)(2,1)}) conditional(s32[]{:T(128)} %bitcast.8, (bf16[512,4096]{1,0:T(8,128)(2,1)}, bf16[768,4096]{1,0:T(8,128)(2,1)}, bf16[768,4096]{1,0:T(8,128)(2,1)}, ...), branch_computations={%region_5.6_spmd, %region_6.7_spmd} | conditional | flops 9666035712 | bytes 83361904
  120.6 8.8 %fusion.31 = f32[512,768]{1,0:T(8,128)} fusion(bf16[512,4096]{1,0:T(8,128)(2,1)} %get-tuple-element.27, bf16[768,4096]{1,0:T(8,128)(2,1)} %get-tuple-element.28), kind=kOutput, calls=%fused_computation.59 | convolution fusion | flops 3221225472 | bytes 12058624 | tf_op jit(solution)/shard_map/cond/branch_1_fun/dot_general | solution.py:48
  129.4 8.2 %multiply_multiply_fusion.1 = (bf16[512,768]{1,0:T(8,128)(2,1)}, f32[512,768]{1,0:T(8,128)}, f32[512,768]{1,0:T(8,128)}) fusion(f32[512,768]{1,0:T(8,128)} %fusion.31, bf16[512,4096]{1,0:T(8,128)(2,1)} %get-tuple-element.27, bf16[768,4096]{1,0:T(8,128)(2,1)S(1)} %copy-done.7), kind=kOutput, calls=%fused_computation.4 | convolution fusion | flops 3223584768 | bytes 15990784 | tf_op jit(solution)/shard_map/cond/branch_1_fun/dot_general | solution.py:49
  137.6 6.1 %fusion.32 = bf16[512,4096]{1,0:T(8,128)(2,1)} fusion(bf16[512,768]{1,0:T(8,128)(2,1)} %get-tuple-element.84, bf16[768,4096]{1,0:T(8,128)(2,1)S(1)} %bitcast.83), kind=kOutput, calls=%fused_computation.60 | convolution fusion | flops 3221225472 | bytes 11272192 | tf_op jit(solution)/shard_map/cond/branch_1_fun/dot_general | solution.py:52
  143.7 69.2 %all-to-all-done.1 = bf16[8,64,4096]{2,1,0:T(8,128)(2,1)} async-done(((bf16[8,64,4096]{2,1,0:T(8,128)(2,1)}), bf16[8,64,4096]{2,1,0:T(8,128)(2,1)}, u32[]{:S(2)}, u32[]{:S(2)}) %all-to-all-start.1) | async-done | bytes 4194336 | tf_op jit(solution)/shard_map/all_to_all | solution.py:41
  212.9 9.1 %multiply_convert_fusion.2 = (bf16[512,768]{1,0:T(8,128)(2,1)S(1)}, bf16[512,768]{1,0:T(8,128)(2,1)S(1)}) fusion(f32[512,768]{1,0:T(8,128)} %get-tuple-element.52, f32[512,768]{1,0:T(8,128)} %get-tuple-element.53, f32[512,768]{1,0:T(8,128)} %get-tuple-element.51, bf16[512,4096]{1,0:T(8,128)(2,1)} %bitcast.6, bf16[1,768,4096]{2,1,0:T(8,128)(2,1)} %param.14), kind=kOutput, calls=%fused_computation.24 | convolution fusion | flops 3225157632 | bytes 16777216 | tf_op jit(solution)/shard_map/dot_general | solution.py:69
  221.9 1.3 pad_maximum_fusion
  223.3 0.7 all-gather.5.cloned.1.call-update
  224.0 4.6 all-to-all-start.3
  228.8 9.3 %multiply_convert_fusion = bf16[768,4096]{1,0:T(8,128)(2,1)} fusion(bf16[512,4096]{1,0:T(8,128)(2,1)} %bitcast.6, bf16[512,768]{1,0:T(8,128)(2,1)} %get-tuple-element.60), kind=kOutput, calls=%fused_computation.8 | convolution fusion | flops 3227516928 | bytes 11272192 | tf_op jit(solution)/shard_map/weight_grads/rf,rd->fd/dot_general | solution.py:88
  238.1 5.5 %fusion.25 = f32[512,4096]{1,0:T(8,128)S(1)} fusion(bf16[512,768]{1,0:T(8,128)(2,1)S(1)} %get-tuple-element.70, bf16[1,768,4096]{2,1,0:T(8,128)(2,1)} %param.12), kind=kOutput, calls=%fused_computation.53 | convolution fusion | flops 3221225472 | bytes 15466496 | tf_op jit(solution)/shard_map/dot_general | solution.py:75
  243.6 7.8 %add_convert_fusion = bf16[512,4096]{1,0:T(8,128)(2,1)} fusion(f32[512,4096]{1,0:T(8,128)S(1)} %fusion.25, bf16[512,768]{1,0:T(8,128)(2,1)S(1)} %get-tuple-element.69, bf16[1,768,4096]{2,1,0:T(8,128)(2,1)} %param.13), kind=kOutput, calls=%fused_computation.9 | convolution fusion | flops 3225419776 | bytes 19660800 | tf_op jit(solution)/shard_map/dot_general | solution.py:76
  251.4 71.1 %all-to-all-done.3 = bf16[8,64,4096]{2,1,0:T(8,128)(2,1)} async-done(((bf16[8,64,4096]{2,1,0:T(8,128)(2,1)}), bf16[8,64,4096]{2,1,0:T(8,128)(2,1)}, u32[]{:S(2)}, u32[]{:S(2)}) %all-to-all-start.3) | async-done | bytes 4194336 | tf_op jit(solution)/shard_map/all_to_all | solution.py:61
  322.6 4.8 all-to-all-start.2
  327.3 3.5 fusion.13
  330.8 2.0 fusion.6
  332.9 0.6 pad_maximum_fusion.1
  333.4 118.3 %all-gather.5.cloned.1.call-done = bf16[2048,4096]{1,0:T(8,128)(2,1)} async-done(((bf16[512,4096]{1,0:T(8,128)(2,1)}), bf16[2048,4096]{1,0:T(8,128)(2,1)}) %all-gather.5.cloned.1.call-update) | async-done | bytes 16777232 | tf_op jit(solution)/shard_map/weight_grads/all_gather | solution.py:90
  451.7 11.2 %fusion.5 = bf16[192,4096]{1,0:T(8,128)(2,1)} fusion(bf16[2048,4096]{1,0:T(8,128)(2,1)} %all-gather.5.cloned.1.call-done, bf16[2048,1536]{1,0:T(8,128)(2,1)} %all-gather.3.cloned.1.call-done, s32[]{:T(128)S(6)} %select_n.12), kind=kOutput, calls=%fused_computation.15 | convolution fusion | flops 3222798336 | bytes 19398660 | tf_op jit(solution)/shard_map/weight_grads/rf,rd->fd/dot_general | solution.py:101
  462.9 1.0 copy-done.2
  464.0 6.2 %fusion.4 = bf16[192,4096]{1,0:T(8,128)(2,1)} fusion(bf16[2048,4096]{1,0:T(8,128)(2,1)S(1)} %copy-done.2, bf16[2048,1536]{1,0:T(8,128)(2,1)} %all-gather.3.cloned.1.call-done, s32[]{:T(128)S(6)} %select_n.11), kind=kOutput, calls=%fused_computation.14 | convolution fusion | flops 3222798336 | bytes 19398660 | tf_op jit(solution)/shard_map/weight_grads/rf,rd->fd/dot_general | solution.py:98
  470.2 3.6 fusion.12
  473.8 1.2 fusion.8
  475.0 50.6 %reduce-scatter.2.cloned.1.call-done = bf16[192,4096]{1,0:T(8,128)(2,1)} async-done(((bf16[768,4096]{1,0:T(8,128)(2,1)}), bf16[192,4096]{1,0:T(8,128)(2,1)}) %reduce-scatter.2.cloned.1.call-update) | async-done | bytes 1572880 | tf_op jit(solution)/shard_map/reduce_scatter | solution.py:103
  (38 shorter events, 2.0 us)
Async XLA Ops:
  7.2 3.2 copy-start
  13.6 6.5 %copy-start.5 = (f32[128,2]{0,1:T(2,128)S(1)}, f32[128,2]{0,1:T(2,128)}, u32[]{:S(2)}) copy-start(f32[128,2]{0,1:T(2,128)} %param.11) | copy-start | bytes 3076
  13.6 6.6 %copy-start.3 = (bf16[128,4096]{1,0:T(8,128)(2,1)S(1)}, bf16[128,4096]{1,0:T(8,128)(2,1)}, u32[]{:S(2)}) copy-start(bf16[128,4096]{1,0:T(8,128)(2,1)} %param.15) | copy-start | bytes 3145732
  13.6 100.6 %all-to-all-start = ((bf16[8,64,4096]{2,1,0:T(8,128)(2,1)}), bf16[8,64,4096]{2,1,0:T(8,128)(2,1)}, u32[]{:S(2)}, u32[]{:S(2)}) async-start(bf16[8,64,4096]{2,1,0:T(8,128)(2,1)} %bitcast.69), calls=%async_computation | async-start | bytes 8388608 | tf_op jit(solution)/shard_map/all_to_all | solution.py:39
  114.2 4.7 copy-start.4
  114.2 98.7 %all-to-all-start.1 = ((bf16[8,64,4096]{2,1,0:T(8,128)(2,1)}), bf16[8,64,4096]{2,1,0:T(8,128)(2,1)}, u32[]{:S(2)}, u32[]{:S(2)}) async-start(bf16[8,64,4096]{2,1,0:T(8,128)(2,1)} %bitcast.68), calls=%async_computation.1 | async-start | bytes 8388608 | tf_op jit(solution)/shard_map/all_to_all | solution.py:41
  118.9 214.6 %all-gather.3.cloned.1.call-start = ((), (), s32[]{:S(2)}) async-start(), calls=%async_computation.5 | async-start | bytes 7864320 | tf_op jit(solution)/shard_map/weight_grads/all_gather | solution.py:92
  120.6 8.8 %copy-start.7 = (bf16[768,4096]{1,0:T(8,128)(2,1)S(1)}, bf16[768,4096]{1,0:T(8,128)(2,1)}, u32[]{:S(2)}) copy-start(bf16[768,4096]{1,0:T(8,128)(2,1)} %get-tuple-element.29) | copy-start | bytes 18874372 | tf_op jit(solution)/shard_map/conditional
  120.6 17.0 %slice-start.2 = ((s8[6291456]{0:T(1024)(128)(4,1)}), s8[4194304]{0:T(1024)(128)(4,1)S(1)}, s32[]{:S(2)}) async-start(s8[6291456]{0:T(1024)(128)(4,1)} %bitcast.82), calls=%async_computation.10 | async-start | bytes 8388608 | tf_op jit(solution)/shard_map/conditional
  129.4 8.2 %slice-start.3 = ((s8[6291456]{0:T(1024)(128)(4,1)}), s8[2097152]{0:T(1024)(128)(4,1)S(1)}, s32[]{:S(2)}) async-start(s8[6291456]{0:T(1024)(128)(4,1)} %bitcast.82), calls=%async_computation.11 | async-start | bytes 4194304 | tf_op jit(solution)/shard_map/conditional
  223.2 228.5 %all-gather.5.cloned.1.call-start = ((), (), s32[]{:S(2)}) async-start(), calls=%async_computation.6 | async-start | bytes 20971520 | tf_op jit(solution)/shard_map/weight_grads/all_gather | solution.py:90
  224.0 98.6 %all-to-all-start.3 = ((bf16[8,64,4096]{2,1,0:T(8,128)(2,1)}), bf16[8,64,4096]{2,1,0:T(8,128)(2,1)}, u32[]{:S(2)}, u32[]{:S(2)}) async-start(bf16[8,64,4096]{2,1,0:T(8,128)(2,1)} %bitcast.15), calls=%async_computation.3 | async-start | bytes 8388608 | tf_op jit(solution)/shard_map/all_to_all | solution.py:61
  228.6 297.0 %reduce-scatter.2.cloned.1.call-start = ((), (), s32[]{:S(2)}) async-start(), calls=%async_computation.7 | async-start | bytes 7864320 | tf_op jit(solution)/shard_map/reduce_scatter | solution.py:103
  322.6 147.6 %all-to-all-start.2 = ((bf16[8,64,4096]{2,1,0:T(8,128)(2,1)}), bf16[8,64,4096]{2,1,0:T(8,128)(2,1)}, u32[]{:S(2)}, u32[]{:S(2)}) async-start(bf16[8,64,4096]{2,1,0:T(8,128)(2,1)} %bitcast.72), calls=%async_computation.2 | async-start | bytes 8388608 | tf_op jit(solution)/shard_map/all_to_all | solution.py:78
  451.7 12.2 %copy-start.2 = (bf16[2048,4096]{1,0:T(8,128)(2,1)S(1)}, bf16[2048,4096]{1,0:T(8,128)(2,1)}, u32[]{:S(2)}) copy-start(bf16[2048,4096]{1,0:T(8,128)(2,1)} %all-gather.5.cloned.1.call-done) | copy-start | bytes 50331652
  470.2 55.4 %copy-start.1 = (bf16[128,4096]{1,0:T(8,128)(2,1)S(1)}, bf16[128,4096]{1,0:T(8,128)(2,1)}, u32[]{:S(2)}) copy-start(bf16[128,4096]{1,0:T(8,128)(2,1)} %param.9) | copy-start | bytes 3145732
Sparse Core Ops, SparseCore 0:
  223.3 69.0 all-gather.2
  294.3 157.4 all-gather.4
  455.3 70.2 reduce-scatter.1

commit v8 on v5

--- a/solution.py
+++ b/solution.py
@@ -117,13 +117,10 @@
         back_grads, gate_share, up_share, mixed, grad_combine = lax.optimization_barrier(
             (back_grads, gate_share, up_share, mixed, grad_combine)
         )
-        picked_grads = jnp.dot(
-            pick_onehot, back_grads.reshape(slots, model_width), preferred_element_type=jnp.float32
-        ).reshape(top_count, tok_count, model_width)
-        grad_tokens = picked_grads[0]
-        for k in range(1, top_count):
-            grad_tokens = grad_tokens + picked_grads[k]
-        grad_tokens = grad_tokens.astype(jnp.bfloat16)
+        token_onehot = send_onehot.T
+        grad_tokens = jnp.dot(
+            token_onehot, back_grads.reshape(slots, model_width), preferred_element_type=jnp.float32
+        ).astype(jnp.bfloat16)
     return (mixed, grad_tokens, grad_combine, gate_share[None], up_share[None], down_share[None])
 
 

time: 445 us -> 444 us (level)
  transfers between devices with their start and end apart: 6 -> 6, of which waited for: 5 -> 5; matrix products, arithmetic and copies ran while one was open for 15% -> 14% of each run, Pallas kernels for 0% -> 0%
where the time goes in v8:
time: 444 us; the launch traced here: 443 us
  waiting for transfers between devices  315 us (71%)
  matrix products  80.8 us (18%)
  starting transfers between devices  20.6 us (5%)
  between operations  14.9 us (3%)
  local copies, waits for them, and re-layouts  7.43 us (2%)
    all_to_all x1, waiting for transfers between devices, per_device(): lax.all_to_all(send_rows, 'expert', split_axis=0, concat_axis=0, tiled=True)  90.7 us
    all_to_all x1, waiting for transfers between devices, per_device(): lax.all_to_all(row_grads.reshape(experts, capacity, model_width), 'expert...  73.4 us
    all_to_all x1, waiting for transfers between devices, per_device(): lax.all_to_all(expert_out.reshape(experts, capacity, model_width), 'exper...  70.7 us
    all_to_all x1, waiting for transfers between devices, per_device(): lax.all_to_all(send_grads, 'expert', split_axis=0, concat_axis=0, tiled=T...  69.5 us
    dot_general x1, matrix products, per_device(): jnp.einsum('rf,rd->fd', gate_up_pre, in_rows, preferred_element_type=jnp....  11.9 us
    reduce_scatter x1, waiting for transfers between devices, per_device(): lax.psum_scatter(gate_up_term, 'dp', scatter_dimension=0, tiled=True)  10.5 us
    dot_general x1, matrix products, per_device(): jnp.einsum('rf,rd->fd', activated, out_grads, preferred_element_type=jnp....  9.35 us
    dot_general x1, matrix products, per_device(): grad_act = jnp.dot(out_grads, w_down.T, preferred_element_type=jnp.float32)  9.04 us
  transfers between devices with their start and end apart: 6, of which 5 were waited for; matrix products, arithmetic and copies ran while one was open for 14% of the time, Pallas kernels for 0%

profile of v8, /device:TPU:0, one launch (start us, length us, event | category | flops | bytes accessed | tf_op | source)
XLA Modules:
  0.0 443.2 jit_solution(1335812787889430451)
XLA Ops:
  7.2 0.9 copy.39
  8.4 0.6 reduce-window.6
  9.5 0.7 fusion.13
  10.3 3.3 convolution_convert_fusion
  13.6 6.5 %all-to-all-start = ((bf16[8,64,4096]{2,1,0:T(8,128)(2,1)}), bf16[8,64,4096]{2,1,0:T(8,128)(2,1)}, u32[]{:S(2)}, u32[]{:S(2)}) async-start(bf16[8,64,4096]{2,1,0:T(8,128)(2,1)} %bitcast.73), calls=%async_computation | async-start | bytes 8388608 | tf_op jit(solution)/shard_map/all_to_all | solution.py:39
  20.2 3.3 multiply_convert_fusion.2
  23.5 90.7 %all-to-all-done = bf16[8,64,4096]{2,1,0:T(8,128)(2,1)} async-done(((bf16[8,64,4096]{2,1,0:T(8,128)(2,1)}), bf16[8,64,4096]{2,1,0:T(8,128)(2,1)}, u32[]{:S(2)}, u32[]{:S(2)}) %all-to-all-start) | async-done | bytes 4194336 | tf_op jit(solution)/shard_map/all_to_all | solution.py:39
  114.2 4.7 %all-to-all-start.1 = ((bf16[8,64,4096]{2,1,0:T(8,128)(2,1)}), bf16[8,64,4096]{2,1,0:T(8,128)(2,1)}, u32[]{:S(2)}, u32[]{:S(2)}) async-start(bf16[8,64,4096]{2,1,0:T(8,128)(2,1)} %bitcast.72), calls=%async_computation.1 | async-start | bytes 8388608 | tf_op jit(solution)/shard_map/all_to_all | solution.py:41
  118.9 0.5 slice.33
  120.1 23.3 %conditional.2 = (f32[512,768]{1,0:T(8,128)}, f32[512,768]{1,0:T(8,128)}, f32[512,768]{1,0:T(8,128)}, bf16[512,768]{1,0:T(8,128)(2,1)}, bf16[512,4096]{1,0:T(8,128)(2,1)}) conditional(s32[]{:T(128)} %bitcast.8, (bf16[512,4096]{1,0:T(8,128)(2,1)}, bf16[768,4096]{1,0:T(8,128)(2,1)}, bf16[768,4096]{1,0:T(8,128)(2,1)}, ...), branch_computations={%region_5.6_spmd, %region_6.7_spmd} | conditional | flops 9666035712 | bytes 83361904
  120.3 8.8 %fusion.23 = f32[512,768]{1,0:T(8,128)} fusion(bf16[512,4096]{1,0:T(8,128)(2,1)} %get-tuple-element.27, bf16[768,4096]{1,0:T(8,128)(2,1)} %get-tuple-element.28), kind=kOutput, calls=%fused_computation.50 | convolution fusion | flops 3221225472 | bytes 12058624 | tf_op jit(solution)/shard_map/cond/branch_1_fun/dot_general | solution.py:48
  129.1 8.2 %multiply_multiply_fusion.1 = (bf16[512,768]{1,0:T(8,128)(2,1)}, f32[512,768]{1,0:T(8,128)}, f32[512,768]{1,0:T(8,128)}) fusion(f32[512,768]{1,0:T(8,128)} %fusion.23, bf16[512,4096]{1,0:T(8,128)(2,1)} %get-tuple-element.27, bf16[768,4096]{1,0:T(8,128)(2,1)S(1)} %copy-done.8), kind=kOutput, calls=%fused_computation.4 | convolution fusion | flops 3223584768 | bytes 15990784 | tf_op jit(solution)/shard_map/cond/branch_1_fun/dot_general | solution.py:49
  137.3 6.1 %fusion.24 = bf16[512,4096]{1,0:T(8,128)(2,1)} fusion(bf16[512,768]{1,0:T(8,128)(2,1)} %get-tuple-element.86, bf16[768,4096]{1,0:T(8,128)(2,1)S(1)} %bitcast.90), kind=kOutput, calls=%fused_computation.51 | convolution fusion | flops 3221225472 | bytes 11272192 | tf_op jit(solution)/shard_map/cond/branch_1_fun/dot_general | solution.py:52
  143.4 69.5 %all-to-all-done.1 = bf16[8,64,4096]{2,1,0:T(8,128)(2,1)} async-done(((bf16[8,64,4096]{2,1,0:T(8,128)(2,1)}), bf16[8,64,4096]{2,1,0:T(8,128)(2,1)}, u32[]{:S(2)}, u32[]{:S(2)}) %all-to-all-start.1) | async-done | bytes 4194336 | tf_op jit(solution)/shard_map/all_to_all | solution.py:41
  212.9 9.0 %multiply_convert_fusion.3 = (bf16[512,768]{1,0:T(8,128)(2,1)S(1)}, bf16[512,768]{1,0:T(8,128)(2,1)S(1)}) fusion(f32[512,768]{1,0:T(8,128)} %get-tuple-element.52, f32[512,768]{1,0:T(8,128)} %get-tuple-element.53, f32[512,768]{1,0:T(8,128)} %get-tuple-element.51, bf16[512,4096]{1,0:T(8,128)(2,1)} %bitcast.6, bf16[1,768,4096]{2,1,0:T(8,128)(2,1)} %param.14), kind=kOutput, calls=%fused_computation.20 | convolution fusion | flops 3225157632 | bytes 16777216 | tf_op jit(solution)/shard_map/dot_general | solution.py:69
  221.9 0.3 copy.43
  222.2 0.6 copy-done.3
  223.4 11.9 %multiply_convert_fusion = bf16[1536,4096]{1,0:T(8,128)(2,1)} fusion(bf16[512,1536]{0,1:T(8,128)(2,1)S(1)} %bitcast.79, bf16[512,4096]{1,0:T(8,128)(2,1)} %bitcast.9), kind=kOutput, calls=%fused_computation.8 | convolution fusion | flops 6455033856 | bytes 18350080 | tf_op jit(solution)/shard_map/weight_grads/rf,rd->fd/dot_general | solution.py:98
  235.3 4.6 %all-to-all-start.3 = ((bf16[8,64,4096]{2,1,0:T(8,128)(2,1)}), bf16[8,64,4096]{2,1,0:T(8,128)(2,1)}, u32[]{:S(2)}, u32[]{:S(2)}) async-start(bf16[8,64,4096]{2,1,0:T(8,128)(2,1)} %bitcast.18), calls=%async_computation.4 | async-start | bytes 8388608 | tf_op jit(solution)/shard_map/all_to_all | solution.py:61
  239.9 0.3 reduce-scatter.5.cloned.1.call-start
  240.2 9.3 %multiply_convert_fusion.1 = bf16[768,4096]{1,0:T(8,128)(2,1)} fusion(bf16[512,4096]{1,0:T(8,128)(2,1)} %bitcast.6, bf16[512,768]{1,0:T(8,128)(2,1)} %get-tuple-element.60), kind=kOutput, calls=%fused_computation.9 | convolution fusion | flops 3227516928 | bytes 11272192 | tf_op jit(solution)/shard_map/weight_grads/rf,rd->fd/dot_general | solution.py:88
  249.6 5.6 %fusion.16 = f32[512,4096]{1,0:T(8,128)S(1)} fusion(bf16[512,768]{1,0:T(8,128)(2,1)S(1)} %get-tuple-element.70, bf16[1,768,4096]{2,1,0:T(8,128)(2,1)} %param.12), kind=kOutput, calls=%fused_computation.43 | convolution fusion | flops 3221225472 | bytes 15466496 | tf_op jit(solution)/shard_map/dot_general | solution.py:75
  255.2 8.0 %add_convert_fusion = bf16[512,4096]{1,0:T(8,128)(2,1)} fusion(f32[512,4096]{1,0:T(8,128)S(1)} %fusion.16, bf16[512,768]{1,0:T(8,128)(2,1)S(1)} %copy-done.4, bf16[1,768,4096]{2,1,0:T(8,128)(2,1)} %param.13), kind=kOutput, calls=%fused_computation.10 | convolution fusion | flops 3225419776 | bytes 19660800 | tf_op jit(solution)/shard_map/dot_general | solution.py:76
  263.2 70.7 %all-to-all-done.3 = bf16[8,64,4096]{2,1,0:T(8,128)(2,1)} async-done(((bf16[8,64,4096]{2,1,0:T(8,128)(2,1)}), bf16[8,64,4096]{2,1,0:T(8,128)(2,1)}, u32[]{:S(2)}, u32[]{:S(2)}) %all-to-all-start.3) | async-done | bytes 4194336 | tf_op jit(solution)/shard_map/all_to_all | solution.py:61
  333.9 4.6 %all-to-all-start.2 = ((bf16[8,64,4096]{2,1,0:T(8,128)(2,1)}), bf16[8,64,4096]{2,1,0:T(8,128)(2,1)}, u32[]{:S(2)}, u32[]{:S(2)}) async-start(bf16[8,64,4096]{2,1,0:T(8,128)(2,1)} %bitcast.76), calls=%async_computation.2 | async-start | bytes 8388608 | tf_op jit(solution)/shard_map/all_to_all | solution.py:78
  338.5 3.5 fusion.8
  342.0 2.0 fusion.4
  344.0 0.6 pad_maximum_fusion.1
  344.6 10.5 %reduce-scatter.3.cloned.1.call-done = bf16[384,4096]{1,0:T(8,128)(2,1)} async-done(((bf16[1536,4096]{1,0:T(8,128)(2,1)}), bf16[384,4096]{1,0:T(8,128)(2,1)}) %reduce-scatter.3.cloned.1.call-update) | async-done | bytes 3145744 | tf_op jit(solution)/shard_map/reduce_scatter | solution.py:101
  355.1 4.0 fusion.20
  359.1 73.4 %all-to-all-done.2 = bf16[8,64,4096]{2,1,0:T(8,128)(2,1)} async-done(((bf16[8,64,4096]{2,1,0:T(8,128)(2,1)}), bf16[8,64,4096]{2,1,0:T(8,128)(2,1)}, u32[]{:S(2)}, u32[]{:S(2)}) %all-to-all-start.2) | async-done | bytes 4194336 | tf_op jit(solution)/shard_map/all_to_all | solution.py:78
  432.5 3.9 convolution_convert_fusion.1
  (39 shorter events, 1.8 us)
Async XLA Ops:
  7.2 3.2 copy-start
  13.6 6.5 %copy-start.6 = (f32[128,2]{0,1:T(2,128)S(1)}, f32[128,2]{0,1:T(2,128)}, u32[]{:S(2)}) copy-start(f32[128,2]{0,1:T(2,128)} %param.11) | copy-start | bytes 3076
  13.6 6.6 %copy-start.2 = (bf16[128,4096]{1,0:T(8,128)(2,1)S(1)}, bf16[128,4096]{1,0:T(8,128)(2,1)}, u32[]{:S(2)}) copy-start(bf16[128,4096]{1,0:T(8,128)(2,1)} %param.15) | copy-start | bytes 3145732
  13.6 100.6 %all-to-all-start = ((bf16[8,64,4096]{2,1,0:T(8,128)(2,1)}), bf16[8,64,4096]{2,1,0:T(8,128)(2,1)}, u32[]{:S(2)}, u32[]{:S(2)}) async-start(bf16[8,64,4096]{2,1,0:T(8,128)(2,1)} %bitcast.73), calls=%async_computation | async-start | bytes 8388608 | tf_op jit(solution)/shard_map/all_to_all | solution.py:39
  114.2 4.7 %copy-start.5 = (s32[128,2]{0,1:T(2,128)S(1)}, s32[128,2]{0,1:T(2,128)}, u32[]{:S(2)}) copy-start(s32[128,2]{0,1:T(2,128)} %param.10) | copy-start | bytes 3076
  114.2 98.7 %all-to-all-start.1 = ((bf16[8,64,4096]{2,1,0:T(8,128)(2,1)}), bf16[8,64,4096]{2,1,0:T(8,128)(2,1)}, u32[]{:S(2)}, u32[]{:S(2)}) async-start(bf16[8,64,4096]{2,1,0:T(8,128)(2,1)} %bitcast.72), calls=%async_computation.1 | async-start | bytes 8388608 | tf_op jit(solution)/shard_map/all_to_all | solution.py:41
  118.9 236.2 %reduce-scatter.3.cloned.1.call-start = ((), (), s32[]{:S(2)}) async-start(), calls=%async_computation.6 | async-start | bytes 15728640 | tf_op jit(solution)/shard_map/reduce_scatter | solution.py:101
  120.3 8.8 %copy-start.8 = (bf16[768,4096]{1,0:T(8,128)(2,1)S(1)}, bf16[768,4096]{1,0:T(8,128)(2,1)}, u32[]{:S(2)}) copy-start(bf16[768,4096]{1,0:T(8,128)(2,1)} %get-tuple-element.29) | copy-start | bytes 18874372 | tf_op jit(solution)/shard_map/conditional
  120.3 17.0 %slice-start.2 = ((s8[6291456]{0:T(1024)(128)(4,1)}), s8[4194304]{0:T(1024)(128)(4,1)S(1)}, s32[]{:S(2)}) async-start(s8[6291456]{0:T(1024)(128)(4,1)} %bitcast.89), calls=%async_computation.10 | async-start | bytes 8388608 | tf_op jit(solution)/shard_map/conditional
  129.1 8.2 %slice-start.3 = ((s8[6291456]{0:T(1024)(128)(4,1)}), s8[2097152]{0:T(1024)(128)(4,1)S(1)}, s32[]{:S(2)}) async-start(s8[6291456]{0:T(1024)(128)(4,1)} %bitcast.89), calls=%async_computation.11 | async-start | bytes 4194304 | tf_op jit(solution)/shard_map/conditional
  221.9 0.9 copy-start.3
  235.3 98.6 %all-to-all-start.3 = ((bf16[8,64,4096]{2,1,0:T(8,128)(2,1)}), bf16[8,64,4096]{2,1,0:T(8,128)(2,1)}, u32[]{:S(2)}, u32[]{:S(2)}) async-start(bf16[8,64,4096]{2,1,0:T(8,128)(2,1)} %bitcast.18), calls=%async_computation.4 | async-start | bytes 8388608 | tf_op jit(solution)/shard_map/all_to_all | solution.py:61
  239.9 196.4 %reduce-scatter.5.cloned.1.call-start = ((), (), s32[]{:S(2)}) async-start(), calls=%async_computation.7 | async-start | bytes 7864320 | tf_op jit(solution)/shard_map/reduce_scatter | solution.py:100
  249.6 5.6 %copy-start.4 = (bf16[512,768]{1,0:T(8,128)(2,1)S(1)}, bf16[512,768]{1,0:T(8,128)(2,1)}, u32[]{:S(2)}) copy-start(bf16[512,768]{1,0:T(8,128)(2,1)} %copy-done.3) | copy-start | bytes 2359300
  333.9 98.6 %all-to-all-start.2 = ((bf16[8,64,4096]{2,1,0:T(8,128)(2,1)}), bf16[8,64,4096]{2,1,0:T(8,128)(2,1)}, u32[]{:S(2)}, u32[]{:S(2)}) async-start(bf16[8,64,4096]{2,1,0:T(8,128)(2,1)} %bitcast.76), calls=%async_computation.2 | async-start | bytes 8388608 | tf_op jit(solution)/shard_map/all_to_all | solution.py:78
  355.1 81.3 %copy-start.1 = (bf16[128,4096]{1,0:T(8,128)(2,1)S(1)}, bf16[128,4096]{1,0:T(8,128)(2,1)}, u32[]{:S(2)}) copy-start(bf16[128,4096]{1,0:T(8,128)(2,1)} %param.9) | copy-start | bytes 3145732
Sparse Core Ops, SparseCore 0:
  235.4 119.6 reduce-scatter.2
  358.6 70.1 reduce-scatter.4

commit v9 on v8

--- a/solution.py
+++ b/solution.py
@@ -75,13 +75,16 @@
         jnp.dot(grad_gate_pre, w_gate, preferred_element_type=jnp.float32)
         + jnp.dot(grad_up_pre, w_up, preferred_element_type=jnp.float32)
     ).astype(jnp.bfloat16)
-    back_grads = lax.all_to_all(
-        row_grads.reshape(experts, capacity, model_width),
-        "expert",
-        split_axis=0,
-        concat_axis=0,
-        tiled=True,
-    )
+    me = lax.axis_index("expert")
+    back_grads = []
+    for shift in range(experts):
+        chunk = lax.dynamic_slice_in_dim(row_grads, ((me + shift) % experts) * capacity, capacity, 0)
+        if shift:
+            chunk = lax.ppermute(
+                chunk, "expert", [(j, (j + shift) % experts) for j in range(experts)]
+            )
+        back_grads.append(chunk)
+    back_grads = jnp.concatenate(back_grads, axis=0)
     ff_share = w_gate.shape[0] // copies
     with jax.named_scope("weight_grads"):
         down_term = (
@@ -117,7 +120,10 @@
         back_grads, gate_share, up_share, mixed, grad_combine = lax.optimization_barrier(
             (back_grads, gate_share, up_share, mixed, grad_combine)
         )
-        token_onehot = send_onehot.T
+        shift_target = ((me - expert_ids) % experts) * capacity + target % capacity
+        token_onehot = jnp.any(
+            shift_target[:, :, None] == slot_iota[None, None, :], axis=1
+        ).astype(jnp.bfloat16)
         grad_tokens = jnp.dot(
             token_onehot, back_grads.reshape(slots, model_width), preferred_element_type=jnp.float32
         ).astype(jnp.bfloat16)

time: 444 us -> 443 us (level)
  waiting for transfers between devices: 315 us -> 276 us
  starting transfers between devices: 20.6 us -> 49.6 us
  local copies, waits for them, and re-layouts: 7.43 us -> 16.5 us
    all_to_all x1 -> x0, waiting for transfers between devices: 73.4 us -> none  [per_device(): lax.all_to_all(row_grads.reshape(experts, capacity, model_width), 'expert...]
    ppermute x0 -> x7, waiting for transfers between devices: none -> 51.8 us  [per_device(): lax.ppermute(chunk, 'expert', [(j, (j + shift) % experts) for j in range(...]
    ppermute x0 -> x7, starting transfers between devices: none -> 33.6 us  [per_device(): lax.ppermute(chunk, 'expert', [(j, (j + shift) % experts) for j in range(...]
    reduce_scatter x1, waiting for transfers between devices: 10.5 us -> 0.01 us  [per_device(): lax.psum_scatter(gate_up_term, 'dp', scatter_dimension=0, tiled=True)]
    all_to_all x1, waiting for transfers between devices: 70.7 us -> 64.3 us  [per_device(): lax.all_to_all(expert_out.reshape(experts, capacity, model_width), 'exper...]
    unnamed x15 -> x25, local copies, waits for them, and re-layouts: 1.5 us -> 7.6 us
    all_to_all x1 -> x0, starting transfers between devices: 4.56 us -> none  [per_device(): lax.all_to_all(row_grads.reshape(experts, capacity, model_width), 'expert...]
  transfers between devices with their start and end apart: 6 -> 12, of which waited for: 5 -> 6; matrix products, arithmetic and copies ran while one was open for 14% -> 16% of each run, Pallas kernels for 0% -> 0%
where the time goes in v9:
time: 443 us; the launch traced here: 442 us
  waiting for transfers between devices  276 us (62%)
  matrix products  79.8 us (18%)
  starting transfers between devices  49.6 us (11%)
  local copies, waits for them, and re-layouts  16.5 us (4%)
  between operations  15 us (3%)
  other arithmetic  4.55 us (1%)
    all_to_all x1, waiting for transfers between devices, per_device(): lax.all_to_all(send_rows, 'expert', split_axis=0, concat_axis=0, tiled=True)  90.7 us
    all_to_all x1, waiting for transfers between devices, per_device(): lax.all_to_all(send_grads, 'expert', split_axis=0, concat_axis=0, tiled=T...  69.3 us
    all_to_all x1, waiting for transfers between devices, per_device(): lax.all_to_all(expert_out.reshape(experts, capacity, model_width), 'exper...  64.3 us
    ppermute x7, waiting for transfers between devices, per_device(): lax.ppermute(chunk, 'expert', [(j, (j + shift) % experts) for j in range(...  51.8 us
    ppermute x7, starting transfers between devices, per_device(): lax.ppermute(chunk, 'expert', [(j, (j + shift) % experts) for j in range(...  33.6 us
    dot_general x1, matrix products, per_device(): jnp.einsum('rf,rd->fd', gate_up_pre, in_rows, preferred_element_type=jnp....  11.8 us
    dot_general x1, matrix products, per_device(): jnp.einsum('rf,rd->fd', activated, out_grads, preferred_element_type=jnp....  9.38 us
    dot_general x1, matrix products, per_device(): grad_act = jnp.dot(out_grads, w_down.T, preferred_element_type=jnp.float32)  9.06 us
  transfers between devices with their start and end apart: 12, of which 6 were waited for; matrix products, arithmetic and copies ran while one was open for 16% of the time, Pallas kernels for 0%

profile of v9, /device:TPU:0, one launch (start us, length us, event | category | flops | bytes accessed | tf_op | source)
XLA Modules:
  0.0 441.9 jit_solution(17747441992697515415)
XLA Ops:
  7.2 0.9 copy.59
  10.3 3.3 convolution_convert_fusion
  13.6 6.5 %all-to-all-start = ((bf16[8,64,4096]{2,1,0:T(8,128)(2,1)}), bf16[8,64,4096]{2,1,0:T(8,128)(2,1)}, u32[]{:S(2)}, u32[]{:S(2)}) async-start(bf16[8,64,4096]{2,1,0:T(8,128)(2,1)} %bitcast.71), calls=%async_computation | async-start | bytes 8388608 | tf_op jit(solution)/shard_map/all_to_all | solution.py:39
  20.3 3.3 multiply_convert_fusion.2
  23.5 90.7 %all-to-all-done = bf16[8,64,4096]{2,1,0:T(8,128)(2,1)} async-done(((bf16[8,64,4096]{2,1,0:T(8,128)(2,1)}), bf16[8,64,4096]{2,1,0:T(8,128)(2,1)}, u32[]{:S(2)}, u32[]{:S(2)}) %all-to-all-start) | async-done | bytes 4194336 | tf_op jit(solution)/shard_map/all_to_all | solution.py:39
  114.2 4.7 %all-to-all-start.1 = ((bf16[8,64,4096]{2,1,0:T(8,128)(2,1)}), bf16[8,64,4096]{2,1,0:T(8,128)(2,1)}, u32[]{:S(2)}, u32[]{:S(2)}) async-start(bf16[8,64,4096]{2,1,0:T(8,128)(2,1)} %bitcast.70), calls=%async_computation.1 | async-start | bytes 8388608 | tf_op jit(solution)/shard_map/all_to_all | solution.py:41
  120.1 23.4 %conditional.2 = (f32[512,768]{1,0:T(8,128)}, f32[512,768]{1,0:T(8,128)}, f32[512,768]{1,0:T(8,128)}, bf16[512,768]{1,0:T(8,128)(2,1)}, bf16[512,4096]{1,0:T(8,128)(2,1)}) conditional(s32[]{:T(128)} %bitcast.8, (bf16[512,4096]{1,0:T(8,128)(2,1)}, bf16[768,4096]{1,0:T(8,128)(2,1)}, bf16[768,4096]{1,0:T(8,128)(2,1)}, ...), branch_computations={%region_5.6_spmd, %region_6.7_spmd} | conditional | flops 9666035712 | bytes 83361904
  120.4 8.8 %fusion.28 = f32[512,768]{1,0:T(8,128)} fusion(bf16[512,4096]{1,0:T(8,128)(2,1)} %get-tuple-element.27, bf16[768,4096]{1,0:T(8,128)(2,1)} %get-tuple-element.28), kind=kOutput, calls=%fused_computation.77 | convolution fusion | flops 3221225472 | bytes 12058624 | tf_op jit(solution)/shard_map/cond/branch_1_fun/dot_general | solution.py:48
  129.2 8.2 %multiply_multiply_fusion.1 = (bf16[512,768]{1,0:T(8,128)(2,1)}, f32[512,768]{1,0:T(8,128)}, f32[512,768]{1,0:T(8,128)}) fusion(f32[512,768]{1,0:T(8,128)} %fusion.28, bf16[512,4096]{1,0:T(8,128)(2,1)} %get-tuple-element.27, bf16[768,4096]{1,0:T(8,128)(2,1)S(1)} %copy-done.10), kind=kOutput, calls=%fused_computation.4 | convolution fusion | flops 3223584768 | bytes 15990784 | tf_op jit(solution)/shard_map/cond/branch_1_fun/dot_general | solution.py:49
  137.4 6.2 %fusion.29 = bf16[512,4096]{1,0:T(8,128)(2,1)} fusion(bf16[512,768]{1,0:T(8,128)(2,1)} %get-tuple-element.95, bf16[768,4096]{1,0:T(8,128)(2,1)S(1)} %bitcast.87), kind=kOutput, calls=%fused_computation.78 | convolution fusion | flops 3221225472 | bytes 11272192 | tf_op jit(solution)/shard_map/cond/branch_1_fun/dot_general | solution.py:52
  143.6 69.3 %all-to-all-done.1 = bf16[8,64,4096]{2,1,0:T(8,128)(2,1)} async-done(((bf16[8,64,4096]{2,1,0:T(8,128)(2,1)}), bf16[8,64,4096]{2,1,0:T(8,128)(2,1)}, u32[]{:S(2)}, u32[]{:S(2)}) %all-to-all-start.1) | async-done | bytes 4194336 | tf_op jit(solution)/shard_map/all_to_all | solution.py:41
  212.9 9.1 %multiply_convert_fusion.3 = (bf16[512,768]{1,0:T(8,128)(2,1)S(1)}, bf16[512,768]{1,0:T(8,128)(2,1)S(1)}) fusion(f32[512,768]{1,0:T(8,128)} %get-tuple-element.52, f32[512,768]{1,0:T(8,128)} %get-tuple-element.53, f32[512,768]{1,0:T(8,128)} %get-tuple-element.51, bf16[512,4096]{1,0:T(8,128)(2,1)} %bitcast.6, bf16[1,768,4096]{2,1,0:T(8,128)(2,1)} %param.14), kind=kOutput, calls=%fused_computation.20 | convolution fusion | flops 3225157632 | bytes 16777216 | tf_op jit(solution)/shard_map/dot_general | solution.py:69
  223.5 11.8 %multiply_convert_fusion = bf16[1536,4096]{1,0:T(8,128)(2,1)} fusion(bf16[512,1536]{0,1:T(8,128)(2,1)S(1)} %bitcast.76, bf16[512,4096]{1,0:T(8,128)(2,1)} %bitcast.9), kind=kOutput, calls=%fused_computation.8 | convolution fusion | flops 6455033856 | bytes 18350080 | tf_op jit(solution)/shard_map/weight_grads/rf,rd->fd/dot_general | solution.py:101
  235.4 4.6 %all-to-all-start.2 = ((bf16[8,64,4096]{2,1,0:T(8,128)(2,1)}), bf16[8,64,4096]{2,1,0:T(8,128)(2,1)}, u32[]{:S(2)}, u32[]{:S(2)}) async-start(bf16[8,64,4096]{2,1,0:T(8,128)(2,1)} %bitcast.17), calls=%async_computation.3 | async-start | bytes 8388608 | tf_op jit(solution)/shard_map/all_to_all | solution.py:61
  240.2 9.4 %multiply_convert_fusion.1 = bf16[768,4096]{1,0:T(8,128)(2,1)} fusion(bf16[512,4096]{1,0:T(8,128)(2,1)} %bitcast.6, bf16[512,768]{1,0:T(8,128)(2,1)} %get-tuple-element.60), kind=kOutput, calls=%fused_computation.9 | convolution fusion | flops 3227516928 | bytes 11272192 | tf_op jit(solution)/shard_map/weight_grads/rf,rd->fd/dot_general | solution.py:91
  249.9 5.6 %fusion.19 = f32[512,4096]{1,0:T(8,128)S(1)} fusion(bf16[512,768]{1,0:T(8,128)(2,1)S(1)} %get-tuple-element.70, bf16[1,768,4096]{2,1,0:T(8,128)(2,1)} %param.12), kind=kOutput, calls=%fused_computation.68 | convolution fusion | flops 3221225472 | bytes 15466496 | tf_op jit(solution)/shard_map/dot_general | solution.py:75
  255.5 6.8 %add_convert_fusion = bf16[512,4096]{1,0:T(8,128)(2,1)S(1)} fusion(f32[512,4096]{1,0:T(8,128)S(1)} %fusion.19, bf16[512,768]{1,0:T(8,128)(2,1)S(1)} %copy-done.4, bf16[1,768,4096]{2,1,0:T(8,128)(2,1)} %param.13), kind=kOutput, calls=%fused_computation.10 | convolution fusion | flops 3225419776 | bytes 19660800 | tf_op jit(solution)/shard_map/dot_general | solution.py:76
  262.3 2.1 constant_dynamic-slice_fusion
  264.4 3.4 collective-permute-start.6
  268.3 1.5 collective-permute-start.1
  270.2 64.3 %all-to-all-done.2 = bf16[8,64,4096]{2,1,0:T(8,128)(2,1)} async-done(((bf16[8,64,4096]{2,1,0:T(8,128)(2,1)}), bf16[8,64,4096]{2,1,0:T(8,128)(2,1)}, u32[]{:S(2)}, u32[]{:S(2)}) %all-to-all-start.2) | async-done | bytes 4194336 | tf_op jit(solution)/shard_map/all_to_all | solution.py:61
  334.4 3.5 fusion.8
  337.9 2.0 fusion.4
  340.5 16.5 %collective-permute-done = bf16[64,4096]{1,0:T(8,128)(2,1)} collective-permute-done((bf16[64,4096]{1,0:T(8,128)(2,1)}, bf16[64,4096]{1,0:T(8,128)(2,1)}, u32[]{:S(2)}, u32[]{:S(2)}) %collective-permute-start) | collective-permute-done | bytes 524320 | tf_op jit(solution)/shard_map/ppermute | solution.py:83
  357.0 25.6 %collective-permute-start.2 = (bf16[64,4096]{1,0:T(8,128)(2,1)S(1)}, bf16[64,4096]{1,0:T(8,128)(2,1)S(1)}, u32[]{:S(2)}, u32[]{:S(2)}) collective-permute-start(bf16[64,4096]{1,0:T(8,128)(2,1)S(1)} %copy-done.6), channel_id=1, source_target_pairs={{0,3},{1,4},{2,5},{3,6},{4,7},{5,0},{6,1},{7,2},{8,11},{9,12},{10,... | collective-permute-start | bytes 1572872 | tf_op jit(solution)/shard_map/ppermute | solution.py:83
  382.6 1.9 constant_dynamic-update-slice_fusion.6
  384.5 2.2 collective-permute-start.3
  387.6 24.4 %collective-permute-done.2 = bf16[64,4096]{1,0:T(8,128)(2,1)S(1)} collective-permute-done((bf16[64,4096]{1,0:T(8,128)(2,1)S(1)}, bf16[64,4096]{1,0:T(8,128)(2,1)S(1)}, u32[]{:S(2)}, u32[]{:S(2)}) %collective-permute-start.2) | collective-permute-done | bytes 524320 | tf_op jit(solution)/shard_map/ppermute | solution.py:83
  412.8 10.9 %collective-permute-done.3 = bf16[64,4096]{1,0:T(8,128)(2,1)S(1)} collective-permute-done((bf16[64,4096]{1,0:T(8,128)(2,1)S(1)}, bf16[64,4096]{1,0:T(8,128)(2,1)S(1)}, u32[]{:S(2)}, u32[]{:S(2)}) %collective-permute-start.3) | collective-permute-done | bytes 524320 | tf_op jit(solution)/shard_map/ppermute | solution.py:83
  425.4 0.9 constant_dynamic-update-slice_fusion.1
  427.1 4.1 fusion.25
  431.2 3.9 convolution_convert_fusion.1
  (64 shorter events, 10.6 us)
Async XLA Ops:
  7.2 3.2 copy-start
  13.6 6.5 %copy-start.8 = (f32[128,2]{0,1:T(2,128)S(1)}, f32[128,2]{0,1:T(2,128)}, u32[]{:S(2)}) copy-start(f32[128,2]{0,1:T(2,128)} %param.11) | copy-start | bytes 3076
  13.6 6.6 %copy-start.2 = (bf16[128,4096]{1,0:T(8,128)(2,1)S(1)}, bf16[128,4096]{1,0:T(8,128)(2,1)}, u32[]{:S(2)}) copy-start(bf16[128,4096]{1,0:T(8,128)(2,1)} %param.15) | copy-start | bytes 3145732
  13.6 100.6 %all-to-all-start = ((bf16[8,64,4096]{2,1,0:T(8,128)(2,1)}), bf16[8,64,4096]{2,1,0:T(8,128)(2,1)}, u32[]{:S(2)}, u32[]{:S(2)}) async-start(bf16[8,64,4096]{2,1,0:T(8,128)(2,1)} %bitcast.71), calls=%async_computation | async-start | bytes 8388608 | tf_op jit(solution)/shard_map/all_to_all | solution.py:39
  114.2 4.8 %copy-start.7 = (s32[128,2]{0,1:T(2,128)S(1)}, s32[128,2]{0,1:T(2,128)}, u32[]{:S(2)}) copy-start(s32[128,2]{0,1:T(2,128)} %param.10) | copy-start | bytes 3076
  114.2 98.7 %all-to-all-start.1 = ((bf16[8,64,4096]{2,1,0:T(8,128)(2,1)}), bf16[8,64,4096]{2,1,0:T(8,128)(2,1)}, u32[]{:S(2)}, u32[]{:S(2)}) async-start(bf16[8,64,4096]{2,1,0:T(8,128)(2,1)} %bitcast.70), calls=%async_computation.1 | async-start | bytes 8388608 | tf_op jit(solution)/shard_map/all_to_all | solution.py:41
  118.9 308.2 %reduce-scatter.3.cloned.1.call-start = ((), (), s32[]{:S(2)}) async-start(), calls=%async_computation.5 | async-start | bytes 15728640 | tf_op jit(solution)/shard_map/reduce_scatter | solution.py:104
  120.3 8.8 %copy-start.10 = (bf16[768,4096]{1,0:T(8,128)(2,1)S(1)}, bf16[768,4096]{1,0:T(8,128)(2,1)}, u32[]{:S(2)}) copy-start(bf16[768,4096]{1,0:T(8,128)(2,1)} %get-tuple-element.29) | copy-start | bytes 18874372 | tf_op jit(solution)/shard_map/conditional
  120.4 17.0 %slice-start.2 = ((s8[6291456]{0:T(1024)(128)(4,1)}), s8[4194304]{0:T(1024)(128)(4,1)S(1)}, s32[]{:S(2)}) async-start(s8[6291456]{0:T(1024)(128)(4,1)} %bitcast.86), calls=%async_computation.9 | async-start | bytes 8388608 | tf_op jit(solution)/shard_map/conditional
  129.2 8.2 %slice-start.3 = ((s8[6291456]{0:T(1024)(128)(4,1)}), s8[2097152]{0:T(1024)(128)(4,1)S(1)}, s32[]{:S(2)}) async-start(s8[6291456]{0:T(1024)(128)(4,1)} %bitcast.86), calls=%async_computation.10 | async-start | bytes 4194304 | tf_op jit(solution)/shard_map/conditional
  222.0 0.9 copy-start.3
  235.4 99.1 %all-to-all-start.2 = ((bf16[8,64,4096]{2,1,0:T(8,128)(2,1)}), bf16[8,64,4096]{2,1,0:T(8,128)(2,1)}, u32[]{:S(2)}, u32[]{:S(2)}) async-start(bf16[8,64,4096]{2,1,0:T(8,128)(2,1)} %bitcast.17), calls=%async_computation.3 | async-start | bytes 8388608 | tf_op jit(solution)/shard_map/all_to_all | solution.py:61
  239.9 195.1 %reduce-scatter.5.cloned.1.call-start = ((), (), s32[]{:S(2)}) async-start(), calls=%async_computation.6 | async-start | bytes 7864320 | tf_op jit(solution)/shard_map/reduce_scatter | solution.py:103
  249.8 5.6 %copy-start.4 = (bf16[512,768]{1,0:T(8,128)(2,1)S(1)}, bf16[512,768]{1,0:T(8,128)(2,1)}, u32[]{:S(2)}) copy-start(bf16[512,768]{1,0:T(8,128)(2,1)} %copy-done.3) | copy-start | bytes 2359300
  264.4 161.9 %collective-permute-start.6 = (bf16[64,4096]{1,0:T(8,128)(2,1)}, bf16[64,4096]{1,0:T(8,128)(2,1)S(1)}, u32[]{:S(2)}, u32[]{:S(2)}) collective-permute-start(bf16[64,4096]{1,0:T(8,128)(2,1)} %get-tuple-element.72), channel_id=1, source_target_pairs={{0,7},{1,0},{2,1},{3,2},{4,3},{5,4},{6,5},{7,6},{8,15},{9,8},{10,9... | collective-permute-start | bytes 1572872 | tf_op jit(solution)/shard_map/ppermute | solution.py:83
  267.7 157.6 %collective-permute-start.5 = (bf16[64,4096]{1,0:T(8,128)(2,1)}, bf16[64,4096]{1,0:T(8,128)(2,1)S(1)}, u32[]{:S(2)}, u32[]{:S(2)}) collective-permute-start(bf16[64,4096]{1,0:T(8,128)(2,1)} %get-tuple-element.73), channel_id=1, source_target_pairs={{0,6},{1,7},{2,0},{3,1},{4,2},{5,3},{6,4},{7,5},{8,14},{9,15},{10,... | collective-permute-start | bytes 1572872 | tf_op jit(solution)/shard_map/ppermute | solution.py:83
  268.3 156.3 %collective-permute-start.4 = (bf16[64,4096]{1,0:T(8,128)(2,1)}, bf16[64,4096]{1,0:T(8,128)(2,1)S(1)}, u32[]{:S(2)}, u32[]{:S(2)}) collective-permute-start(bf16[64,4096]{1,0:T(8,128)(2,1)} %get-tuple-element.74), channel_id=1, source_target_pairs={{0,5},{1,6},{2,7},{3,0},{4,1},{5,2},{6,3},{7,4},{8,13},{9,14},{10,... | collective-permute-start | bytes 1572872 | tf_op jit(solution)/shard_map/ppermute | solution.py:83
  268.3 116.2 %collective-permute-start.1 = (bf16[64,4096]{1,0:T(8,128)(2,1)}, bf16[64,4096]{1,0:T(8,128)(2,1)S(1)}, u32[]{:S(2)}, u32[]{:S(2)}) collective-permute-start(bf16[64,4096]{1,0:T(8,128)(2,1)} %get-tuple-element.77), channel_id=1, source_target_pairs={{0,2},{1,3},{2,4},{3,5},{4,6},{5,7},{6,0},{7,1},{8,10},{9,11},{10,... | collective-permute-start | bytes 1572872 | tf_op jit(solution)/shard_map/ppermute | solution.py:83
  269.8 87.2 %collective-permute-start = (bf16[64,4096]{1,0:T(8,128)(2,1)}, bf16[64,4096]{1,0:T(8,128)(2,1)}, u32[]{:S(2)}, u32[]{:S(2)}) collective-permute-start(bf16[64,4096]{1,0:T(8,128)(2,1)} %get-tuple-element.78), channel_id=1, source_target_pairs={{0,1},{1,2},{2,3},{3,4},{4,5},{5,6},{6,7},{7,0},{8,9},{9,10},{10,1... | collective-permute-start | bytes 1572872 | tf_op jit(solution)/shard_map/ppermute | solution.py:83
  337.9 19.1 %copy-start.6 = (bf16[64,4096]{1,0:T(8,128)(2,1)S(1)}, bf16[64,4096]{1,0:T(8,128)(2,1)}, u32[]{:S(2)}) copy-start(bf16[64,4096]{1,0:T(8,128)(2,1)} %get-tuple-element.76) | copy-start | bytes 1572868
  337.9 46.6 %copy-start.5 = (bf16[64,4096]{1,0:T(8,128)(2,1)S(1)}, bf16[64,4096]{1,0:T(8,128)(2,1)}, u32[]{:S(2)}) copy-start(bf16[64,4096]{1,0:T(8,128)(2,1)} %get-tuple-element.75) | copy-start | bytes 1572868
  357.0 55.0 %collective-permute-start.2 = (bf16[64,4096]{1,0:T(8,128)(2,1)S(1)}, bf16[64,4096]{1,0:T(8,128)(2,1)S(1)}, u32[]{:S(2)}, u32[]{:S(2)}) collective-permute-start(bf16[64,4096]{1,0:T(8,128)(2,1)S(1)} %copy-done.6), channel_id=1, source_target_pairs={{0,3},{1,4},{2,5},{3,6},{4,7},{5,0},{6,1},{7,2},{8,11},{9,12},{10,... | collective-permute-start | bytes 1572872 | tf_op jit(solution)/shard_map/ppermute | solution.py:83
  384.5 39.2 %collective-permute-start.3 = (bf16[64,4096]{1,0:T(8,128)(2,1)S(1)}, bf16[64,4096]{1,0:T(8,128)(2,1)S(1)}, u32[]{:S(2)}, u32[]{:S(2)}) collective-permute-start(bf16[64,4096]{1,0:T(8,128)(2,1)S(1)} %copy-done.5), channel_id=1, source_target_pairs={{0,4},{1,5},{2,6},{3,7},{4,0},{5,1},{6,2},{7,3},{8,12},{9,13},{10,... | collective-permute-start | bytes 1572872 | tf_op jit(solution)/shard_map/ppermute | solution.py:83
  427.1 7.9 %copy-start.1 = (bf16[128,4096]{1,0:T(8,128)(2,1)S(1)}, bf16[128,4096]{1,0:T(8,128)(2,1)}, u32[]{:S(2)}) copy-start(bf16[128,4096]{1,0:T(8,128)(2,1)} %param.9) | copy-start | bytes 3145732
Sparse Core Ops, SparseCore 0:
  235.5 119.6 reduce-scatter.2
  358.7 70.1 reduce-scatter.4

commit v10 on v9

--- a/solution.py
+++ b/solution.py
@@ -75,16 +75,6 @@
         jnp.dot(grad_gate_pre, w_gate, preferred_element_type=jnp.float32)
         + jnp.dot(grad_up_pre, w_up, preferred_element_type=jnp.float32)
     ).astype(jnp.bfloat16)
-    me = lax.axis_index("expert")
-    back_grads = []
-    for shift in range(experts):
-        chunk = lax.dynamic_slice_in_dim(row_grads, ((me + shift) % experts) * capacity, capacity, 0)
-        if shift:
-            chunk = lax.ppermute(
-                chunk, "expert", [(j, (j + shift) % experts) for j in range(experts)]
-            )
-        back_grads.append(chunk)
-    back_grads = jnp.concatenate(back_grads, axis=0)
     ff_share = w_gate.shape[0] // copies
     with jax.named_scope("weight_grads"):
         down_term = (
@@ -104,6 +94,18 @@
     gate_up_share = lax.psum_scatter(gate_up_term, "dp", scatter_dimension=0, tiled=True)
     gate_share = gate_up_share[:ff_share]
     up_share = gate_up_share[ff_share:]
+    me = lax.axis_index("expert")
+    back_grads = []
+    for shift in range(experts):
+        chunk = lax.dynamic_slice_in_dim(row_grads, ((me + shift) % experts) * capacity, capacity, 0)
+        if shift == experts // 2:
+            chunk, gate_share, up_share = lax.optimization_barrier((chunk, gate_share, up_share))
+        if shift:
+            chunk = lax.ppermute(
+                chunk, "expert", [(j, (j + shift) % experts) for j in range(experts)]
+            )
+        back_grads.append(chunk)
+    back_grads = jnp.concatenate(back_grads, axis=0)
     pick_onehot = hit.reshape(top_count * tok_count, slots).astype(jnp.bfloat16)
     with jax.named_scope("combine_rows"):
         picked_out = jnp.dot(

time: 443 us -> 439 us (level)
  waiting for transfers between devices: 276 us -> 261 us
  starting transfers between devices: 49.6 us -> 61.2 us
    ppermute x7, waiting for transfers between devices: 51.8 us -> 36.9 us  [per_device(): lax.ppermute(chunk, 'expert', [(j, (j + shift) % experts) for j in range(...]
    ppermute x7, starting transfers between devices: 33.6 us -> 45.2 us  [per_device(): lax.ppermute(chunk, 'expert', [(j, (j + shift) % experts) for j in range(...]
where the time goes in v10:
time: 439 us; the launch traced here: 438 us
  waiting for transfers between devices  261 us (59%)
  matrix products  79.7 us (18%)
  starting transfers between devices  61.2 us (14%)
  local copies, waits for them, and re-layouts  16.4 us (4%)
  between operations  15 us (3%)
  other arithmetic  4.55 us (1%)
    all_to_all x1, waiting for transfers between devices, per_device(): lax.all_to_all(send_rows, 'expert', split_axis=0, concat_axis=0, tiled=True)  90.7 us
    all_to_all x1, waiting for transfers between devices, per_device(): lax.all_to_all(send_grads, 'expert', split_axis=0, concat_axis=0, tiled=T...  69.5 us
    all_to_all x1, waiting for transfers between devices, per_device(): lax.all_to_all(expert_out.reshape(experts, capacity, model_width), 'exper...  63.6 us
    ppermute x7, starting transfers between devices, per_device(): lax.ppermute(chunk, 'expert', [(j, (j + shift) % experts) for j in range(...  45.2 us
    ppermute x7, waiting for transfers between devices, per_device(): lax.ppermute(chunk, 'expert', [(j, (j + shift) % experts) for j in range(...  36.9 us
    dot_general x1, matrix products, per_device(): jnp.einsum('rf,rd->fd', gate_up_pre, in_rows, preferred_element_type=jnp....  11.8 us
    dot_general x1, matrix products, per_device(): jnp.einsum('rf,rd->fd', activated, out_grads, preferred_element_type=jnp....  9.38 us
    dot_general x1, matrix products, per_device(): grad_act = jnp.dot(out_grads, w_down.T, preferred_element_type=jnp.float32)  9.04 us
  transfers between devices with their start and end apart: 12, of which 6 were waited for; matrix products, arithmetic and copies ran while one was open for 16% of the time, Pallas kernels for 0%

profile of v10, /device:TPU:0, one launch (start us, length us, event | category | flops | bytes accessed | tf_op | source)
XLA Modules:
  0.0 437.9 jit_solution(6287979030497026794)
XLA Ops:
  7.2 0.9 copy.59
  10.3 3.3 convolution_convert_fusion
  13.6 6.5 %all-to-all-start = ((bf16[8,64,4096]{2,1,0:T(8,128)(2,1)}), bf16[8,64,4096]{2,1,0:T(8,128)(2,1)}, u32[]{:S(2)}, u32[]{:S(2)}) async-start(bf16[8,64,4096]{2,1,0:T(8,128)(2,1)} %bitcast.71), calls=%async_computation | async-start | bytes 8388608 | tf_op jit(solution)/shard_map/all_to_all | solution.py:39
  20.2 3.3 multiply_convert_fusion.2
  23.5 90.7 %all-to-all-done = bf16[8,64,4096]{2,1,0:T(8,128)(2,1)} async-done(((bf16[8,64,4096]{2,1,0:T(8,128)(2,1)}), bf16[8,64,4096]{2,1,0:T(8,128)(2,1)}, u32[]{:S(2)}, u32[]{:S(2)}) %all-to-all-start) | async-done | bytes 4194336 | tf_op jit(solution)/shard_map/all_to_all | solution.py:39
  114.2 4.7 %all-to-all-start.1 = ((bf16[8,64,4096]{2,1,0:T(8,128)(2,1)}), bf16[8,64,4096]{2,1,0:T(8,128)(2,1)}, u32[]{:S(2)}, u32[]{:S(2)}) async-start(bf16[8,64,4096]{2,1,0:T(8,128)(2,1)} %bitcast.70), calls=%async_computation.1 | async-start | bytes 8388608 | tf_op jit(solution)/shard_map/all_to_all | solution.py:41
  120.1 23.3 %conditional.2 = (f32[512,768]{1,0:T(8,128)}, f32[512,768]{1,0:T(8,128)}, f32[512,768]{1,0:T(8,128)}, bf16[512,768]{1,0:T(8,128)(2,1)}, bf16[512,4096]{1,0:T(8,128)(2,1)}) conditional(s32[]{:T(128)} %bitcast.8, (bf16[512,4096]{1,0:T(8,128)(2,1)}, bf16[768,4096]{1,0:T(8,128)(2,1)}, bf16[768,4096]{1,0:T(8,128)(2,1)}, ...), branch_computations={%region_5.6_spmd, %region_6.7_spmd} | conditional | flops 9666035712 | bytes 83361904
  120.3 8.8 %fusion.28 = f32[512,768]{1,0:T(8,128)} fusion(bf16[512,4096]{1,0:T(8,128)(2,1)} %get-tuple-element.27, bf16[768,4096]{1,0:T(8,128)(2,1)} %get-tuple-element.28), kind=kOutput, calls=%fused_computation.77 | convolution fusion | flops 3221225472 | bytes 12058624 | tf_op jit(solution)/shard_map/cond/branch_1_fun/dot_general | solution.py:48
  129.1 8.2 %multiply_multiply_fusion.1 = (bf16[512,768]{1,0:T(8,128)(2,1)}, f32[512,768]{1,0:T(8,128)}, f32[512,768]{1,0:T(8,128)}) fusion(f32[512,768]{1,0:T(8,128)} %fusion.28, bf16[512,4096]{1,0:T(8,128)(2,1)} %get-tuple-element.27, bf16[768,4096]{1,0:T(8,128)(2,1)S(1)} %copy-done.9), kind=kOutput, calls=%fused_computation.4 | convolution fusion | flops 3223584768 | bytes 15990784 | tf_op jit(solution)/shard_map/cond/branch_1_fun/dot_general | solution.py:49
  137.3 6.1 %fusion.29 = bf16[512,4096]{1,0:T(8,128)(2,1)} fusion(bf16[512,768]{1,0:T(8,128)(2,1)} %get-tuple-element.101, bf16[768,4096]{1,0:T(8,128)(2,1)S(1)} %bitcast.87), kind=kOutput, calls=%fused_computation.78 | convolution fusion | flops 3221225472 | bytes 11272192 | tf_op jit(solution)/shard_map/cond/branch_1_fun/dot_general | solution.py:52
  143.4 69.5 %all-to-all-done.1 = bf16[8,64,4096]{2,1,0:T(8,128)(2,1)} async-done(((bf16[8,64,4096]{2,1,0:T(8,128)(2,1)}), bf16[8,64,4096]{2,1,0:T(8,128)(2,1)}, u32[]{:S(2)}, u32[]{:S(2)}) %all-to-all-start.1) | async-done | bytes 4194336 | tf_op jit(solution)/shard_map/all_to_all | solution.py:41
  212.9 9.0 %multiply_convert_fusion.3 = (bf16[512,768]{1,0:T(8,128)(2,1)S(1)}, bf16[512,768]{1,0:T(8,128)(2,1)S(1)}) fusion(f32[512,768]{1,0:T(8,128)} %get-tuple-element.55, f32[512,768]{1,0:T(8,128)} %get-tuple-element.56, f32[512,768]{1,0:T(8,128)} %get-tuple-element.54, bf16[512,4096]{1,0:T(8,128)(2,1)} %bitcast.6, bf16[1,768,4096]{2,1,0:T(8,128)(2,1)} %param.14), kind=kOutput, calls=%fused_computation.20 | convolution fusion | flops 3225157632 | bytes 16777216 | tf_op jit(solution)/shard_map/dot_general | solution.py:69
  223.4 11.8 %multiply_convert_fusion = bf16[1536,4096]{1,0:T(8,128)(2,1)} fusion(bf16[512,1536]{0,1:T(8,128)(2,1)S(1)} %bitcast.76, bf16[512,4096]{1,0:T(8,128)(2,1)} %bitcast.9), kind=kOutput, calls=%fused_computation.8 | convolution fusion | flops 6455033856 | bytes 18350080 | tf_op jit(solution)/shard_map/weight_grads/rf,rd->fd/dot_general | solution.py:91
  235.3 4.6 %all-to-all-start.2 = ((bf16[8,64,4096]{2,1,0:T(8,128)(2,1)}), bf16[8,64,4096]{2,1,0:T(8,128)(2,1)}, u32[]{:S(2)}, u32[]{:S(2)}) async-start(bf16[8,64,4096]{2,1,0:T(8,128)(2,1)} %bitcast.17), calls=%async_computation.3 | async-start | bytes 8388608 | tf_op jit(solution)/shard_map/all_to_all | solution.py:61
  240.2 9.4 %multiply_convert_fusion.1 = bf16[768,4096]{1,0:T(8,128)(2,1)} fusion(bf16[512,4096]{1,0:T(8,128)(2,1)} %bitcast.6, bf16[512,768]{1,0:T(8,128)(2,1)} %get-tuple-element.66), kind=kOutput, calls=%fused_computation.9 | convolution fusion | flops 3227516928 | bytes 11272192 | tf_op jit(solution)/shard_map/weight_grads/rf,rd->fd/dot_general | solution.py:81
  249.8 5.6 %fusion.19 = f32[512,4096]{1,0:T(8,128)S(1)} fusion(bf16[512,768]{1,0:T(8,128)(2,1)S(1)} %get-tuple-element.76, bf16[1,768,4096]{2,1,0:T(8,128)(2,1)} %param.12), kind=kOutput, calls=%fused_computation.68 | convolution fusion | flops 3221225472 | bytes 15466496 | tf_op jit(solution)/shard_map/dot_general | solution.py:75
  255.4 6.8 %add_convert_fusion = bf16[512,4096]{1,0:T(8,128)(2,1)S(1)} fusion(f32[512,4096]{1,0:T(8,128)S(1)} %fusion.19, bf16[512,768]{1,0:T(8,128)(2,1)S(1)} %copy-done.4, bf16[1,768,4096]{2,1,0:T(8,128)(2,1)} %param.13), kind=kOutput, calls=%fused_computation.10 | convolution fusion | flops 3225419776 | bytes 19660800 | tf_op jit(solution)/shard_map/dot_general | solution.py:76
  262.2 2.1 constant_dynamic-slice_fusion
  264.3 3.4 collective-permute-start.6
  268.2 1.7 collective-permute-start.2
  270.8 63.6 %all-to-all-done.2 = bf16[8,64,4096]{2,1,0:T(8,128)(2,1)} async-done(((bf16[8,64,4096]{2,1,0:T(8,128)(2,1)}), bf16[8,64,4096]{2,1,0:T(8,128)(2,1)}, u32[]{:S(2)}, u32[]{:S(2)}) %all-to-all-start.2) | async-done | bytes 4194336 | tf_op jit(solution)/shard_map/all_to_all | solution.py:61
  334.4 3.5 fusion.8
  337.9 2.0 fusion.4
  340.5 16.5 %collective-permute-done = bf16[64,4096]{1,0:T(8,128)(2,1)} collective-permute-done((bf16[64,4096]{1,0:T(8,128)(2,1)}, bf16[64,4096]{1,0:T(8,128)(2,1)}, u32[]{:S(2)}, u32[]{:S(2)}) %collective-permute-start) | collective-permute-done | bytes 524320 | tf_op jit(solution)/shard_map/ppermute | solution.py:104
  357.0 16.2 %collective-permute-start.1 = (bf16[64,4096]{1,0:T(8,128)(2,1)}, bf16[64,4096]{1,0:T(8,128)(2,1)S(1)}, u32[]{:S(2)}, u32[]{:S(2)}) collective-permute-start(bf16[64,4096]{1,0:T(8,128)(2,1)} %get-tuple-element.83), channel_id=1, source_target_pairs={{0,2},{1,3},{2,4},{3,5},{4,6},{5,7},{6,0},{7,1},{8,10},{9,11},{10,... | collective-permute-start | bytes 1572872 | tf_op jit(solution)/shard_map/ppermute | solution.py:104
  373.2 2.0 constant_dynamic-update-slice_fusion.6
  375.1 3.9 fusion.25
  379.0 8.8 %collective-permute-done.1 = bf16[64,4096]{1,0:T(8,128)(2,1)S(1)} collective-permute-done((bf16[64,4096]{1,0:T(8,128)(2,1)}, bf16[64,4096]{1,0:T(8,128)(2,1)S(1)}, u32[]{:S(2)}, u32[]{:S(2)}) %collective-permute-start.1) | collective-permute-done | bytes 524320 | tf_op jit(solution)/shard_map/ppermute | solution.py:104
  387.9 22.5 %collective-permute-start.3 = (bf16[64,4096]{1,0:T(8,128)(2,1)S(1)}, bf16[64,4096]{1,0:T(8,128)(2,1)S(1)}, u32[]{:S(2)}, u32[]{:S(2)}) collective-permute-start(bf16[64,4096]{1,0:T(8,128)(2,1)S(1)} %copy-done.5), channel_id=1, source_target_pairs={{0,4},{1,5},{2,6},{3,7},{4,0},{5,1},{6,2},{7,3},{8,12},{9,13},{10,... | collective-permute-start | bytes 1572872 | tf_op jit(solution)/shard_map/ppermute | solution.py:104
  412.1 11.6 %collective-permute-done.3 = bf16[64,4096]{1,0:T(8,128)(2,1)S(1)} collective-permute-done((bf16[64,4096]{1,0:T(8,128)(2,1)S(1)}, bf16[64,4096]{1,0:T(8,128)(2,1)S(1)}, u32[]{:S(2)}, u32[]{:S(2)}) %collective-permute-start.3) | collective-permute-done | bytes 524320 | tf_op jit(solution)/shard_map/ppermute | solution.py:104
  425.4 0.9 constant_dynamic-update-slice_fusion.1
  427.1 4.0 convolution_convert_fusion.1
  (62 shorter events, 11.0 us)
Async XLA Ops:
  7.2 3.2 copy-start
  13.6 6.5 %copy-start.7 = (f32[128,2]{0,1:T(2,128)S(1)}, f32[128,2]{0,1:T(2,128)}, u32[]{:S(2)}) copy-start(f32[128,2]{0,1:T(2,128)} %param.11) | copy-start | bytes 3076
  13.6 6.6 %copy-start.2 = (bf16[128,4096]{1,0:T(8,128)(2,1)S(1)}, bf16[128,4096]{1,0:T(8,128)(2,1)}, u32[]{:S(2)}) copy-start(bf16[128,4096]{1,0:T(8,128)(2,1)} %param.15) | copy-start | bytes 3145732
  13.6 100.6 %all-to-all-start = ((bf16[8,64,4096]{2,1,0:T(8,128)(2,1)}), bf16[8,64,4096]{2,1,0:T(8,128)(2,1)}, u32[]{:S(2)}, u32[]{:S(2)}) async-start(bf16[8,64,4096]{2,1,0:T(8,128)(2,1)} %bitcast.71), calls=%async_computation | async-start | bytes 8388608 | tf_op jit(solution)/shard_map/all_to_all | solution.py:39
  114.2 4.8 %copy-start.6 = (s32[128,2]{0,1:T(2,128)S(1)}, s32[128,2]{0,1:T(2,128)}, u32[]{:S(2)}) copy-start(s32[128,2]{0,1:T(2,128)} %param.10) | copy-start | bytes 3076
  114.2 98.7 %all-to-all-start.1 = ((bf16[8,64,4096]{2,1,0:T(8,128)(2,1)}), bf16[8,64,4096]{2,1,0:T(8,128)(2,1)}, u32[]{:S(2)}, u32[]{:S(2)}) async-start(bf16[8,64,4096]{2,1,0:T(8,128)(2,1)} %bitcast.70), calls=%async_computation.1 | async-start | bytes 8388608 | tf_op jit(solution)/shard_map/all_to_all | solution.py:41
  118.9 256.2 %reduce-scatter.3.cloned.1.call-start = ((), (), s32[]{:S(2)}) async-start(), calls=%async_computation.5 | async-start | bytes 15728640 | tf_op jit(solution)/shard_map/reduce_scatter | solution.py:94
  120.3 8.8 %copy-start.9 = (bf16[768,4096]{1,0:T(8,128)(2,1)S(1)}, bf16[768,4096]{1,0:T(8,128)(2,1)}, u32[]{:S(2)}) copy-start(bf16[768,4096]{1,0:T(8,128)(2,1)} %get-tuple-element.29) | copy-start | bytes 18874372 | tf_op jit(solution)/shard_map/conditional
  120.3 17.0 %slice-start.2 = ((s8[6291456]{0:T(1024)(128)(4,1)}), s8[4194304]{0:T(1024)(128)(4,1)S(1)}, s32[]{:S(2)}) async-start(s8[6291456]{0:T(1024)(128)(4,1)} %bitcast.86), calls=%async_computation.9 | async-start | bytes 8388608 | tf_op jit(solution)/shard_map/conditional
  129.1 8.2 %slice-start.3 = ((s8[6291456]{0:T(1024)(128)(4,1)}), s8[2097152]{0:T(1024)(128)(4,1)S(1)}, s32[]{:S(2)}) async-start(s8[6291456]{0:T(1024)(128)(4,1)} %bitcast.86), calls=%async_computation.10 | async-start | bytes 4194304 | tf_op jit(solution)/shard_map/conditional
  221.9 0.9 copy-start.3
  235.3 99.1 %all-to-all-start.2 = ((bf16[8,64,4096]{2,1,0:T(8,128)(2,1)}), bf16[8,64,4096]{2,1,0:T(8,128)(2,1)}, u32[]{:S(2)}, u32[]{:S(2)}) async-start(bf16[8,64,4096]{2,1,0:T(8,128)(2,1)} %bitcast.17), calls=%async_computation.3 | async-start | bytes 8388608 | tf_op jit(solution)/shard_map/all_to_all | solution.py:61
  239.9 191.1 %reduce-scatter.5.cloned.1.call-start = ((), (), s32[]{:S(2)}) async-start(), calls=%async_computation.6 | async-start | bytes 7864320 | tf_op jit(solution)/shard_map/reduce_scatter | solution.py:93
  249.8 5.6 %copy-start.4 = (bf16[512,768]{1,0:T(8,128)(2,1)S(1)}, bf16[512,768]{1,0:T(8,128)(2,1)}, u32[]{:S(2)}) copy-start(bf16[512,768]{1,0:T(8,128)(2,1)} %copy-done.3) | copy-start | bytes 2359300
  264.3 161.9 %collective-permute-start.6 = (bf16[64,4096]{1,0:T(8,128)(2,1)}, bf16[64,4096]{1,0:T(8,128)(2,1)S(1)}, u32[]{:S(2)}, u32[]{:S(2)}) collective-permute-start(bf16[64,4096]{1,0:T(8,128)(2,1)} %get-tuple-element.78), channel_id=1, source_target_pairs={{0,7},{1,0},{2,1},{3,2},{4,3},{5,4},{6,5},{7,6},{8,15},{9,8},{10,9... | collective-permute-start | bytes 1572872 | tf_op jit(solution)/shard_map/ppermute | solution.py:104
  267.7 157.7 %collective-permute-start.5 = (bf16[64,4096]{1,0:T(8,128)(2,1)}, bf16[64,4096]{1,0:T(8,128)(2,1)S(1)}, u32[]{:S(2)}, u32[]{:S(2)}) collective-permute-start(bf16[64,4096]{1,0:T(8,128)(2,1)} %get-tuple-element.79), channel_id=1, source_target_pairs={{0,6},{1,7},{2,0},{3,1},{4,2},{5,3},{6,4},{7,5},{8,14},{9,15},{10,... | collective-permute-start | bytes 1572872 | tf_op jit(solution)/shard_map/ppermute | solution.py:104
  268.2 156.3 %collective-permute-start.4 = (bf16[64,4096]{1,0:T(8,128)(2,1)}, bf16[64,4096]{1,0:T(8,128)(2,1)S(1)}, u32[]{:S(2)}, u32[]{:S(2)}) collective-permute-start(bf16[64,4096]{1,0:T(8,128)(2,1)} %get-tuple-element.80), channel_id=1, source_target_pairs={{0,5},{1,6},{2,7},{3,0},{4,1},{5,2},{6,3},{7,4},{8,13},{9,14},{10,... | collective-permute-start | bytes 1572872 | tf_op jit(solution)/shard_map/ppermute | solution.py:104
  268.2 143.0 %collective-permute-start.2 = (bf16[64,4096]{1,0:T(8,128)(2,1)}, bf16[64,4096]{1,0:T(8,128)(2,1)S(1)}, u32[]{:S(2)}, u32[]{:S(2)}) collective-permute-start(bf16[64,4096]{1,0:T(8,128)(2,1)} %get-tuple-element.82), channel_id=1, source_target_pairs={{0,3},{1,4},{2,5},{3,6},{4,7},{5,0},{6,1},{7,2},{8,11},{9,12},{10,... | collective-permute-start | bytes 1572872 | tf_op jit(solution)/shard_map/ppermute | solution.py:104
  270.0 87.0 %collective-permute-start = (bf16[64,4096]{1,0:T(8,128)(2,1)}, bf16[64,4096]{1,0:T(8,128)(2,1)}, u32[]{:S(2)}, u32[]{:S(2)}) collective-permute-start(bf16[64,4096]{1,0:T(8,128)(2,1)} %get-tuple-element.84), channel_id=1, source_target_pairs={{0,1},{1,2},{2,3},{3,4},{4,5},{5,6},{6,7},{7,0},{8,9},{9,10},{10,1... | collective-permute-start | bytes 1572872 | tf_op jit(solution)/shard_map/ppermute | solution.py:104
  339.9 48.0 %copy-start.5 = (bf16[64,4096]{1,0:T(8,128)(2,1)S(1)}, bf16[64,4096]{1,0:T(8,128)(2,1)}, u32[]{:S(2)}) copy-start(bf16[64,4096]{1,0:T(8,128)(2,1)} %get-tuple-element.57) | copy-start | bytes 1572868
  357.0 30.9 %collective-permute-start.1 = (bf16[64,4096]{1,0:T(8,128)(2,1)}, bf16[64,4096]{1,0:T(8,128)(2,1)S(1)}, u32[]{:S(2)}, u32[]{:S(2)}) collective-permute-start(bf16[64,4096]{1,0:T(8,128)(2,1)} %get-tuple-element.83), channel_id=1, source_target_pairs={{0,2},{1,3},{2,4},{3,5},{4,6},{5,7},{6,0},{7,1},{8,10},{9,11},{10,... | collective-permute-start | bytes 1572872 | tf_op jit(solution)/shard_map/ppermute | solution.py:104
  387.9 35.8 %collective-permute-start.3 = (bf16[64,4096]{1,0:T(8,128)(2,1)S(1)}, bf16[64,4096]{1,0:T(8,128)(2,1)S(1)}, u32[]{:S(2)}, u32[]{:S(2)}) collective-permute-start(bf16[64,4096]{1,0:T(8,128)(2,1)S(1)} %copy-done.5), channel_id=1, source_target_pairs={{0,4},{1,5},{2,6},{3,7},{4,0},{5,1},{6,2},{7,3},{8,12},{9,13},{10,... | collective-permute-start | bytes 1572872 | tf_op jit(solution)/shard_map/ppermute | solution.py:104
  423.7 7.4 %copy-start.1 = (bf16[128,4096]{1,0:T(8,128)(2,1)S(1)}, bf16[128,4096]{1,0:T(8,128)(2,1)}, u32[]{:S(2)}) copy-start(bf16[128,4096]{1,0:T(8,128)(2,1)} %param.9) | copy-start | bytes 3145732
Sparse Core Ops, SparseCore 0:
  235.4 119.6 reduce-scatter.2
  358.7 70.1 reduce-scatter.4

commit v11 on v10

--- a/solution.py
+++ b/solution.py
@@ -123,12 +123,10 @@
             (back_grads, gate_share, up_share, mixed, grad_combine)
         )
         shift_target = ((me - expert_ids) % experts) * capacity + target % capacity
-        token_onehot = jnp.any(
-            shift_target[:, :, None] == slot_iota[None, None, :], axis=1
-        ).astype(jnp.bfloat16)
-        grad_tokens = jnp.dot(
-            token_onehot, back_grads.reshape(slots, model_width), preferred_element_type=jnp.float32
-        ).astype(jnp.bfloat16)
+        grad_tokens = back_grads[shift_target[:, 0]].astype(jnp.float32)
+        for k in range(1, top_count):
+            grad_tokens = grad_tokens + back_grads[shift_target[:, k]].astype(jnp.float32)
+        grad_tokens = grad_tokens.astype(jnp.bfloat16)
     return (mixed, grad_tokens, grad_combine, gate_share[None], up_share[None], down_share[None])
 
 

time: 439 us -> 454 us (1.034); the launches traced: 438 us -> 445 us
  local copies, waits for them, and re-layouts: 16.4 us -> 26.4 us
    gather x0 -> x2, local copies, waits for them, and re-layouts: none -> 10.1 us  [the longest x1 5.03 us: per_device(): back_grads[shift_target[:, k]].astype(jnp.float32)]
  transfers between devices with their start and end apart: 12 -> 12, of which waited for: 6 -> 6; matrix products, arithmetic and copies ran while one was open for 16% -> 18% of each run, Pallas kernels for 0% -> 0%
where the time goes in v11:
time: 454 us; the launch traced here: 445 us
  waiting for transfers between devices  260 us (57%)
  matrix products  75.6 us (17%)
  starting transfers between devices  61.4 us (14%)
  local copies, waits for them, and re-layouts  26.4 us (6%)
  between operations  15.3 us (3%)
  other arithmetic  5.67 us (1%)
    all_to_all x1, waiting for transfers between devices, per_device(): lax.all_to_all(send_rows, 'expert', split_axis=0, concat_axis=0, tiled=True)  90.7 us
    all_to_all x1, waiting for transfers between devices, per_device(): lax.all_to_all(send_grads, 'expert', split_axis=0, concat_axis=0, tiled=T...  69 us
    all_to_all x1, waiting for transfers between devices, per_device(): lax.all_to_all(expert_out.reshape(experts, capacity, model_width), 'exper...  63.5 us
    ppermute x7, starting transfers between devices, per_device(): lax.ppermute(chunk, 'expert', [(j, (j + shift) % experts) for j in range(...  45.4 us
    ppermute x7, waiting for transfers between devices, per_device(): lax.ppermute(chunk, 'expert', [(j, (j + shift) % experts) for j in range(...  37 us
    dot_general x1, matrix products, per_device(): jnp.einsum('rf,rd->fd', gate_up_pre, in_rows, preferred_element_type=jnp....  11.8 us
    dot_general x1, matrix products, per_device(): jnp.einsum('rf,rd->fd', activated, out_grads, preferred_element_type=jnp....  9.4 us
  transfers between devices with their start and end apart: 12, of which 6 were waited for; matrix products, arithmetic and copies ran while one was open for 18% of the time, Pallas kernels for 0%

profile of v11, /device:TPU:0, one launch (start us, length us, event | category | flops | bytes accessed | tf_op | source)
XLA Modules:
  0.0 445.3 jit_solution(6209922817945926218)
XLA Ops:
  10.3 3.3 convolution_convert_fusion
  13.6 6.5 %all-to-all-start = ((bf16[8,64,4096]{2,1,0:T(8,128)(2,1)}), bf16[8,64,4096]{2,1,0:T(8,128)(2,1)}, u32[]{:S(2)}, u32[]{:S(2)}) async-start(bf16[8,64,4096]{2,1,0:T(8,128)(2,1)} %bitcast.73), calls=%async_computation | async-start | bytes 8388608 | tf_op jit(solution)/shard_map/all_to_all | solution.py:39
  20.3 3.3 multiply_convert_fusion.2
  23.5 90.7 %all-to-all-done = bf16[8,64,4096]{2,1,0:T(8,128)(2,1)} async-done(((bf16[8,64,4096]{2,1,0:T(8,128)(2,1)}), bf16[8,64,4096]{2,1,0:T(8,128)(2,1)}, u32[]{:S(2)}, u32[]{:S(2)}) %all-to-all-start) | async-done | bytes 4194336 | tf_op jit(solution)/shard_map/all_to_all | solution.py:39
  114.2 4.7 %all-to-all-start.1 = ((bf16[8,64,4096]{2,1,0:T(8,128)(2,1)}), bf16[8,64,4096]{2,1,0:T(8,128)(2,1)}, u32[]{:S(2)}, u32[]{:S(2)}) async-start(bf16[8,64,4096]{2,1,0:T(8,128)(2,1)} %bitcast.72), calls=%async_computation.1 | async-start | bytes 8388608 | tf_op jit(solution)/shard_map/all_to_all | solution.py:41
  120.1 23.8 %conditional.2 = (f32[512,768]{1,0:T(8,128)}, f32[512,768]{1,0:T(8,128)}, f32[512,768]{1,0:T(8,128)}, bf16[512,768]{1,0:T(8,128)(2,1)}, bf16[512,4096]{1,0:T(8,128)(2,1)}) conditional(s32[]{:T(128)} %bitcast.8, (bf16[512,4096]{1,0:T(8,128)(2,1)}, bf16[768,4096]{1,0:T(8,128)(2,1)}, bf16[768,4096]{1,0:T(8,128)(2,1)}, ...), branch_computations={%region_5.6_spmd, %region_6.7_spmd} | conditional | flops 9666035712 | bytes 83361904
  120.7 8.8 %fusion.29 = f32[512,768]{1,0:T(8,128)} fusion(bf16[512,4096]{1,0:T(8,128)(2,1)} %get-tuple-element.27, bf16[768,4096]{1,0:T(8,128)(2,1)} %get-tuple-element.28), kind=kOutput, calls=%fused_computation.83 | convolution fusion | flops 3221225472 | bytes 12058624 | tf_op jit(solution)/shard_map/cond/branch_1_fun/dot_general | solution.py:48
  129.5 8.2 %multiply_multiply_fusion.1 = (bf16[512,768]{1,0:T(8,128)(2,1)}, f32[512,768]{1,0:T(8,128)}, f32[512,768]{1,0:T(8,128)}) fusion(f32[512,768]{1,0:T(8,128)} %fusion.29, bf16[512,4096]{1,0:T(8,128)(2,1)} %get-tuple-element.27, bf16[768,4096]{1,0:T(8,128)(2,1)S(1)} %copy-done.8), kind=kOutput, calls=%fused_computation.6 | convolution fusion | flops 3223584768 | bytes 15990784 | tf_op jit(solution)/shard_map/cond/branch_1_fun/dot_general | solution.py:49
  137.7 6.1 %fusion.30 = bf16[512,4096]{1,0:T(8,128)(2,1)} fusion(bf16[512,768]{1,0:T(8,128)(2,1)} %get-tuple-element.105, bf16[768,4096]{1,0:T(8,128)(2,1)S(1)} %bitcast.89), kind=kOutput, calls=%fused_computation.84 | convolution fusion | flops 3221225472 | bytes 11272192 | tf_op jit(solution)/shard_map/cond/branch_1_fun/dot_general | solution.py:52
  143.9 69.0 %all-to-all-done.1 = bf16[8,64,4096]{2,1,0:T(8,128)(2,1)} async-done(((bf16[8,64,4096]{2,1,0:T(8,128)(2,1)}), bf16[8,64,4096]{2,1,0:T(8,128)(2,1)}, u32[]{:S(2)}, u32[]{:S(2)}) %all-to-all-start.1) | async-done | bytes 4194336 | tf_op jit(solution)/shard_map/all_to_all | solution.py:41
  212.9 8.9 %multiply_convert_fusion.3 = (bf16[512,768]{1,0:T(8,128)(2,1)S(1)}, bf16[512,768]{1,0:T(8,128)(2,1)S(1)}) fusion(f32[512,768]{1,0:T(8,128)} %get-tuple-element.55, f32[512,768]{1,0:T(8,128)} %get-tuple-element.56, f32[512,768]{1,0:T(8,128)} %get-tuple-element.54, bf16[512,4096]{1,0:T(8,128)(2,1)} %bitcast.6, bf16[1,768,4096]{2,1,0:T(8,128)(2,1)} %param.14), kind=kOutput, calls=%fused_computation.22 | convolution fusion | flops 3225157632 | bytes 16777216 | tf_op jit(solution)/shard_map/dot_general | solution.py:69
  223.3 11.8 %multiply_convert_fusion = bf16[1536,4096]{1,0:T(8,128)(2,1)} fusion(bf16[512,1536]{0,1:T(8,128)(2,1)S(1)} %bitcast.78, bf16[512,4096]{1,0:T(8,128)(2,1)} %bitcast.9), kind=kOutput, calls=%fused_computation.10 | convolution fusion | flops 6455033856 | bytes 18350080 | tf_op jit(solution)/shard_map/weight_grads/rf,rd->fd/dot_general | solution.py:91
  235.2 4.6 %all-to-all-start.2 = ((bf16[8,64,4096]{2,1,0:T(8,128)(2,1)}), bf16[8,64,4096]{2,1,0:T(8,128)(2,1)}, u32[]{:S(2)}, u32[]{:S(2)}) async-start(bf16[8,64,4096]{2,1,0:T(8,128)(2,1)} %bitcast.17), calls=%async_computation.3 | async-start | bytes 8388608 | tf_op jit(solution)/shard_map/all_to_all | solution.py:61
  240.0 9.4 %multiply_convert_fusion.1 = bf16[768,4096]{1,0:T(8,128)(2,1)} fusion(bf16[512,4096]{1,0:T(8,128)(2,1)} %bitcast.6, bf16[512,768]{1,0:T(8,128)(2,1)} %get-tuple-element.66), kind=kOutput, calls=%fused_computation.11 | convolution fusion | flops 3227516928 | bytes 11272192 | tf_op jit(solution)/shard_map/weight_grads/rf,rd->fd/dot_general | solution.py:81
  249.6 5.6 %fusion.20 = f32[512,4096]{1,0:T(8,128)S(1)} fusion(bf16[512,768]{1,0:T(8,128)(2,1)S(1)} %get-tuple-element.76, bf16[1,768,4096]{2,1,0:T(8,128)(2,1)} %param.12), kind=kOutput, calls=%fused_computation.74 | convolution fusion | flops 3221225472 | bytes 15466496 | tf_op jit(solution)/shard_map/dot_general | solution.py:75
  255.2 6.8 %add_convert_fusion = bf16[512,4096]{1,0:T(8,128)(2,1)S(1)} fusion(f32[512,4096]{1,0:T(8,128)S(1)} %fusion.20, bf16[512,768]{1,0:T(8,128)(2,1)S(1)} %copy-done.4, bf16[1,768,4096]{2,1,0:T(8,128)(2,1)} %param.13), kind=kOutput, calls=%fused_computation.12 | convolution fusion | flops 3225419776 | bytes 19660800 | tf_op jit(solution)/shard_map/dot_general | solution.py:76
  262.0 2.1 constant_dynamic-slice_fusion
  264.1 3.5 collective-permute-start.6
  268.2 1.7 collective-permute-start.2
  270.7 63.5 %all-to-all-done.2 = bf16[8,64,4096]{2,1,0:T(8,128)(2,1)} async-done(((bf16[8,64,4096]{2,1,0:T(8,128)(2,1)}), bf16[8,64,4096]{2,1,0:T(8,128)(2,1)}, u32[]{:S(2)}, u32[]{:S(2)}) %all-to-all-start.2) | async-done | bytes 4194336 | tf_op jit(solution)/shard_map/all_to_all | solution.py:61
  334.2 3.5 fusion.8
  337.7 2.0 fusion.4
  340.3 16.5 %collective-permute-done = bf16[64,4096]{1,0:T(8,128)(2,1)} collective-permute-done((bf16[64,4096]{1,0:T(8,128)(2,1)}, bf16[64,4096]{1,0:T(8,128)(2,1)}, u32[]{:S(2)}, u32[]{:S(2)}) %collective-permute-start) | collective-permute-done | bytes 524320 | tf_op jit(solution)/shard_map/ppermute | solution.py:104
  356.8 16.4 %collective-permute-start.1 = (bf16[64,4096]{1,0:T(8,128)(2,1)}, bf16[64,4096]{1,0:T(8,128)(2,1)S(1)}, u32[]{:S(2)}, u32[]{:S(2)}) collective-permute-start(bf16[64,4096]{1,0:T(8,128)(2,1)} %get-tuple-element.83), channel_id=1, source_target_pairs={{0,2},{1,3},{2,4},{3,5},{4,6},{5,7},{6,0},{7,1},{8,10},{9,11},{10,... | collective-permute-start | bytes 1572872 | tf_op jit(solution)/shard_map/ppermute | solution.py:104
  373.3 1.9 constant_dynamic-update-slice_fusion.6
  375.2 3.9 fusion.26
  379.1 8.9 %collective-permute-done.1 = bf16[64,4096]{1,0:T(8,128)(2,1)S(1)} collective-permute-done((bf16[64,4096]{1,0:T(8,128)(2,1)}, bf16[64,4096]{1,0:T(8,128)(2,1)S(1)}, u32[]{:S(2)}, u32[]{:S(2)}) %collective-permute-start.1) | collective-permute-done | bytes 524320 | tf_op jit(solution)/shard_map/ppermute | solution.py:104
  388.0 22.3 %collective-permute-start.3 = (bf16[64,4096]{1,0:T(8,128)(2,1)}, bf16[64,4096]{1,0:T(8,128)(2,1)S(1)}, u32[]{:S(2)}, u32[]{:S(2)}) collective-permute-start(bf16[64,4096]{1,0:T(8,128)(2,1)} %get-tuple-element.57), channel_id=1, source_target_pairs={{0,4},{1,5},{2,6},{3,7},{4,0},{5,1},{6,2},{7,3},{8,12},{9,13},{10,... | collective-permute-start | bytes 1572872 | tf_op jit(solution)/shard_map/ppermute | solution.py:104
  411.9 11.6 %collective-permute-done.3 = bf16[64,4096]{1,0:T(8,128)(2,1)S(1)} collective-permute-done((bf16[64,4096]{1,0:T(8,128)(2,1)}, bf16[64,4096]{1,0:T(8,128)(2,1)S(1)}, u32[]{:S(2)}, u32[]{:S(2)}) %collective-permute-start.3) | collective-permute-done | bytes 524320 | tf_op jit(solution)/shard_map/ppermute | solution.py:104
  426.9 5.0 %gather_fusion.1 = bf16[128,4096]{1,0:T(8,128)(2,1)S(1)} fusion(bf16[512,4096]{1,0:T(8,128)(2,1)} %constant_dynamic-update-slice_fusion, s32[1024]{0:T(1024)S(1)} %get-tuple-element.95), kind=kCustom, calls=%fused_computation.1 | custom fusion | bytes 2097664 | tf_op jit(solution)/shard_map/combine_rows/gather | solution.py:128
  432.0 5.0 %gather_fusion = bf16[128,4096]{1,0:T(8,128)(2,1)S(1)} fusion(bf16[512,4096]{1,0:T(8,128)(2,1)} %constant_dynamic-update-slice_fusion, s32[1024]{0:T(1024)S(1)} %get-tuple-element.96), kind=kCustom, calls=%fused_computation | custom fusion | bytes 2097664 | tf_op jit(solution)/shard_map/combine_rows/gather | solution.py:126
  437.0 1.2 add_convert_fusion.1
  (63 shorter events, 12.6 us)
Async XLA Ops:
  7.2 3.2 copy-start
  13.6 6.5 %copy-start.6 = (f32[128,2]{0,1:T(2,128)S(1)}, f32[128,2]{0,1:T(2,128)}, u32[]{:S(2)}) copy-start(f32[128,2]{0,1:T(2,128)} %param.11) | copy-start | bytes 3076
  13.6 6.6 %copy-start.2 = (bf16[128,4096]{1,0:T(8,128)(2,1)S(1)}, bf16[128,4096]{1,0:T(8,128)(2,1)}, u32[]{:S(2)}) copy-start(bf16[128,4096]{1,0:T(8,128)(2,1)} %param.15) | copy-start | bytes 3145732
  13.6 100.6 %all-to-all-start = ((bf16[8,64,4096]{2,1,0:T(8,128)(2,1)}), bf16[8,64,4096]{2,1,0:T(8,128)(2,1)}, u32[]{:S(2)}, u32[]{:S(2)}) async-start(bf16[8,64,4096]{2,1,0:T(8,128)(2,1)} %bitcast.73), calls=%async_computation | async-start | bytes 8388608 | tf_op jit(solution)/shard_map/all_to_all | solution.py:39
  114.2 4.8 %copy-start.5 = (s32[128,2]{0,1:T(2,128)S(1)}, s32[128,2]{0,1:T(2,128)}, u32[]{:S(2)}) copy-start(s32[128,2]{0,1:T(2,128)} %param.10) | copy-start | bytes 3076
  114.2 98.7 %all-to-all-start.1 = ((bf16[8,64,4096]{2,1,0:T(8,128)(2,1)}), bf16[8,64,4096]{2,1,0:T(8,128)(2,1)}, u32[]{:S(2)}, u32[]{:S(2)}) async-start(bf16[8,64,4096]{2,1,0:T(8,128)(2,1)} %bitcast.72), calls=%async_computation.1 | async-start | bytes 8388608 | tf_op jit(solution)/shard_map/all_to_all | solution.py:41
  118.9 256.3 %reduce-scatter.3.cloned.1.call-start = ((), (), s32[]{:S(2)}) async-start(), calls=%async_computation.5 | async-start | bytes 15728640 | tf_op jit(solution)/shard_map/reduce_scatter | solution.py:94
  120.7 8.8 %copy-start.8 = (bf16[768,4096]{1,0:T(8,128)(2,1)S(1)}, bf16[768,4096]{1,0:T(8,128)(2,1)}, u32[]{:S(2)}) copy-start(bf16[768,4096]{1,0:T(8,128)(2,1)} %get-tuple-element.29) | copy-start | bytes 18874372 | tf_op jit(solution)/shard_map/conditional
  120.7 17.0 %slice-start.2 = ((s8[6291456]{0:T(1024)(128)(4,1)}), s8[4194304]{0:T(1024)(128)(4,1)S(1)}, s32[]{:S(2)}) async-start(s8[6291456]{0:T(1024)(128)(4,1)} %bitcast.88), calls=%async_computation.9 | async-start | bytes 8388608 | tf_op jit(solution)/shard_map/conditional
  129.5 8.2 %slice-start.3 = ((s8[6291456]{0:T(1024)(128)(4,1)}), s8[2097152]{0:T(1024)(128)(4,1)S(1)}, s32[]{:S(2)}) async-start(s8[6291456]{0:T(1024)(128)(4,1)} %bitcast.88), calls=%async_computation.10 | async-start | bytes 4194304 | tf_op jit(solution)/shard_map/conditional
  221.9 0.9 copy-start.3
  235.2 99.0 %all-to-all-start.2 = ((bf16[8,64,4096]{2,1,0:T(8,128)(2,1)}), bf16[8,64,4096]{2,1,0:T(8,128)(2,1)}, u32[]{:S(2)}, u32[]{:S(2)}) async-start(bf16[8,64,4096]{2,1,0:T(8,128)(2,1)} %bitcast.17), calls=%async_computation.3 | async-start | bytes 8388608 | tf_op jit(solution)/shard_map/all_to_all | solution.py:61
  239.8 198.5 %reduce-scatter.5.cloned.1.call-start = ((), (), s32[]{:S(2)}) async-start(), calls=%async_computation.6 | async-start | bytes 7864320 | tf_op jit(solution)/shard_map/reduce_scatter | solution.py:93
  249.6 5.6 %copy-start.4 = (bf16[512,768]{1,0:T(8,128)(2,1)S(1)}, bf16[512,768]{1,0:T(8,128)(2,1)}, u32[]{:S(2)}) copy-start(bf16[512,768]{1,0:T(8,128)(2,1)} %copy-done.3) | copy-start | bytes 2359300
  264.1 162.0 %collective-permute-start.6 = (bf16[64,4096]{1,0:T(8,128)(2,1)}, bf16[64,4096]{1,0:T(8,128)(2,1)S(1)}, u32[]{:S(2)}, u32[]{:S(2)}) collective-permute-start(bf16[64,4096]{1,0:T(8,128)(2,1)} %get-tuple-element.78), channel_id=1, source_target_pairs={{0,7},{1,0},{2,1},{3,2},{4,3},{5,4},{6,5},{7,6},{8,15},{9,8},{10,9... | collective-permute-start | bytes 1572872 | tf_op jit(solution)/shard_map/ppermute | solution.py:104
  267.6 157.6 %collective-permute-start.5 = (bf16[64,4096]{1,0:T(8,128)(2,1)}, bf16[64,4096]{1,0:T(8,128)(2,1)S(1)}, u32[]{:S(2)}, u32[]{:S(2)}) collective-permute-start(bf16[64,4096]{1,0:T(8,128)(2,1)} %get-tuple-element.79), channel_id=1, source_target_pairs={{0,6},{1,7},{2,0},{3,1},{4,2},{5,3},{6,4},{7,5},{8,14},{9,15},{10,... | collective-permute-start | bytes 1572872 | tf_op jit(solution)/shard_map/ppermute | solution.py:104
  268.2 156.2 %collective-permute-start.4 = (bf16[64,4096]{1,0:T(8,128)(2,1)}, bf16[64,4096]{1,0:T(8,128)(2,1)S(1)}, u32[]{:S(2)}, u32[]{:S(2)}) collective-permute-start(bf16[64,4096]{1,0:T(8,128)(2,1)} %get-tuple-element.80), channel_id=1, source_target_pairs={{0,5},{1,6},{2,7},{3,0},{4,1},{5,2},{6,3},{7,4},{8,13},{9,14},{10,... | collective-permute-start | bytes 1572872 | tf_op jit(solution)/shard_map/ppermute | solution.py:104
  268.2 142.9 %collective-permute-start.2 = (bf16[64,4096]{1,0:T(8,128)(2,1)}, bf16[64,4096]{1,0:T(8,128)(2,1)S(1)}, u32[]{:S(2)}, u32[]{:S(2)}) collective-permute-start(bf16[64,4096]{1,0:T(8,128)(2,1)} %get-tuple-element.82), channel_id=1, source_target_pairs={{0,3},{1,4},{2,5},{3,6},{4,7},{5,0},{6,1},{7,2},{8,11},{9,12},{10,... | collective-permute-start | bytes 1572872 | tf_op jit(solution)/shard_map/ppermute | solution.py:104
  269.9 86.9 %collective-permute-start = (bf16[64,4096]{1,0:T(8,128)(2,1)}, bf16[64,4096]{1,0:T(8,128)(2,1)}, u32[]{:S(2)}, u32[]{:S(2)}) collective-permute-start(bf16[64,4096]{1,0:T(8,128)(2,1)} %get-tuple-element.84), channel_id=1, source_target_pairs={{0,1},{1,2},{2,3},{3,4},{4,5},{5,6},{6,7},{7,0},{8,9},{9,10},{10,1... | collective-permute-start | bytes 1572872 | tf_op jit(solution)/shard_map/ppermute | solution.py:104
  356.8 31.1 %collective-permute-start.1 = (bf16[64,4096]{1,0:T(8,128)(2,1)}, bf16[64,4096]{1,0:T(8,128)(2,1)S(1)}, u32[]{:S(2)}, u32[]{:S(2)}) collective-permute-start(bf16[64,4096]{1,0:T(8,128)(2,1)} %get-tuple-element.83), channel_id=1, source_target_pairs={{0,2},{1,3},{2,4},{3,5},{4,6},{5,7},{6,0},{7,1},{8,10},{9,11},{10,... | collective-permute-start | bytes 1572872 | tf_op jit(solution)/shard_map/ppermute | solution.py:104
  388.0 35.6 %collective-permute-start.3 = (bf16[64,4096]{1,0:T(8,128)(2,1)}, bf16[64,4096]{1,0:T(8,128)(2,1)S(1)}, u32[]{:S(2)}, u32[]{:S(2)}) collective-permute-start(bf16[64,4096]{1,0:T(8,128)(2,1)} %get-tuple-element.57), channel_id=1, source_target_pairs={{0,4},{1,5},{2,6},{3,7},{4,0},{5,1},{6,2},{7,3},{8,12},{9,13},{10,... | collective-permute-start | bytes 1572872 | tf_op jit(solution)/shard_map/ppermute | solution.py:104
  432.0 6.3 %copy-start.1 = (bf16[128,4096]{1,0:T(8,128)(2,1)S(1)}, bf16[128,4096]{1,0:T(8,128)(2,1)}, u32[]{:S(2)}) copy-start(bf16[128,4096]{1,0:T(8,128)(2,1)} %param.9) | copy-start | bytes 3145732
Sparse Core Ops, SparseCore 0:
  235.3 119.5 reduce-scatter.2
  358.5 70.1 reduce-scatter.4

commit v12 on v10

--- a/solution.py
+++ b/solution.py
@@ -8,9 +8,11 @@
     tok_count, top_count = expert_ids.shape
     pair_total = tok_count * top_count
     flat_ids = expert_ids.reshape(pair_total)
-    onehot = (flat_ids[:, None] == jnp.arange(experts, dtype=jnp.int32)[None, :]).astype(jnp.int32)
-    earlier = jnp.cumsum(onehot, axis=0) - onehot
-    position = jnp.sum(earlier * onehot, axis=1)
+    onehot = flat_ids[:, None] == jnp.arange(experts, dtype=jnp.int32)[None, :]
+    pair_iota = jnp.arange(pair_total, dtype=jnp.int32)
+    before = (pair_iota[None, :] < pair_iota[:, None]).astype(jnp.bfloat16)
+    earlier = jnp.dot(before, onehot.astype(jnp.bfloat16), preferred_element_type=jnp.float32)
+    position = jnp.sum(jnp.where(onehot, earlier, 0.0), axis=1).astype(jnp.int32)
     return (flat_ids * capacity + position).reshape(tok_count, top_count)
 
 

time: 439 us -> 438 us (level)
  no operation moved by 1% of the time
where the time goes in v12:
time: 438 us; the launch traced here: 437 us
  waiting for transfers between devices  261 us (60%)
  matrix products  80.1 us (18%)
  starting transfers between devices  61.2 us (14%)
  local copies, waits for them, and re-layouts  16 us (4%)
  between operations  15 us (3%)
    all_to_all x1, waiting for transfers between devices, per_device(): lax.all_to_all(send_rows, 'expert', split_axis=0, concat_axis=0, tiled=True)  90.7 us
    all_to_all x1, waiting for transfers between devices, per_device(): lax.all_to_all(send_grads, 'expert', split_axis=0, concat_axis=0, tiled=T...  69.3 us
    all_to_all x1, waiting for transfers between devices, per_device(): lax.all_to_all(expert_out.reshape(experts, capacity, model_width), 'exper...  63.6 us
    ppermute x7, starting transfers between devices, per_device(): lax.ppermute(chunk, 'expert', [(j, (j + shift) % experts) for j in range(...  45.2 us
    ppermute x7, waiting for transfers between devices, per_device(): lax.ppermute(chunk, 'expert', [(j, (j + shift) % experts) for j in range(...  37 us
    dot_general x1, matrix products, per_device(): jnp.einsum('rf,rd->fd', gate_up_pre, in_rows, preferred_element_type=jnp....  11.8 us
    dot_general x1, matrix products, per_device(): jnp.einsum('rf,rd->fd', activated, out_grads, preferred_element_type=jnp....  9.39 us
    dot_general x1, matrix products, per_device(): grad_act = jnp.dot(out_grads, w_down.T, preferred_element_type=jnp.float32)  9.04 us
  transfers between devices with their start and end apart: 12, of which 6 were waited for; matrix products, arithmetic and copies ran while one was open for 16% of the time, Pallas kernels for 0%

profile of v12, /device:TPU:0, one launch (start us, length us, event | category | flops | bytes accessed | tf_op | source)
XLA Modules:
  0.0 437.0 jit_solution(4742299365381697743)
XLA Ops:
  7.2 0.9 copy.56
  9.5 3.3 convolution_convert_fusion
  12.8 6.5 %all-to-all-start = ((bf16[8,64,4096]{2,1,0:T(8,128)(2,1)}), bf16[8,64,4096]{2,1,0:T(8,128)(2,1)}, u32[]{:S(2)}, u32[]{:S(2)}) async-start(bf16[8,64,4096]{2,1,0:T(8,128)(2,1)} %bitcast.63), calls=%async_computation | async-start | bytes 8388608 | tf_op jit(solution)/shard_map/all_to_all | solution.py:41
  19.4 3.2 multiply_convert_fusion.2
  22.6 90.7 %all-to-all-done = bf16[8,64,4096]{2,1,0:T(8,128)(2,1)} async-done(((bf16[8,64,4096]{2,1,0:T(8,128)(2,1)}), bf16[8,64,4096]{2,1,0:T(8,128)(2,1)}, u32[]{:S(2)}, u32[]{:S(2)}) %all-to-all-start) | async-done | bytes 4194336 | tf_op jit(solution)/shard_map/all_to_all | solution.py:41
  113.3 4.7 %all-to-all-start.1 = ((bf16[8,64,4096]{2,1,0:T(8,128)(2,1)}), bf16[8,64,4096]{2,1,0:T(8,128)(2,1)}, u32[]{:S(2)}, u32[]{:S(2)}) async-start(bf16[8,64,4096]{2,1,0:T(8,128)(2,1)} %bitcast.62), calls=%async_computation.1 | async-start | bytes 8388608 | tf_op jit(solution)/shard_map/all_to_all | solution.py:43
  119.3 23.5 %conditional.2 = (f32[512,768]{1,0:T(8,128)}, f32[512,768]{1,0:T(8,128)}, f32[512,768]{1,0:T(8,128)}, bf16[512,768]{1,0:T(8,128)(2,1)}, bf16[512,4096]{1,0:T(8,128)(2,1)}) conditional(s32[]{:T(128)} %bitcast.6, (bf16[512,4096]{1,0:T(8,128)(2,1)}, bf16[768,4096]{1,0:T(8,128)(2,1)}, bf16[768,4096]{1,0:T(8,128)(2,1)}, ...), branch_computations={%region_3.4_spmd, %region_4.5_spmd} | conditional | flops 9666035712 | bytes 83361904
  119.5 8.8 %fusion.27 = f32[512,768]{1,0:T(8,128)} fusion(bf16[512,4096]{1,0:T(8,128)(2,1)} %get-tuple-element.27, bf16[768,4096]{1,0:T(8,128)(2,1)} %get-tuple-element.28), kind=kOutput, calls=%fused_computation.75 | convolution fusion | flops 3221225472 | bytes 12058624 | tf_op jit(solution)/shard_map/cond/branch_1_fun/dot_general | solution.py:50
  128.3 8.2 %multiply_multiply_fusion.1 = (bf16[512,768]{1,0:T(8,128)(2,1)}, f32[512,768]{1,0:T(8,128)}, f32[512,768]{1,0:T(8,128)}) fusion(f32[512,768]{1,0:T(8,128)} %fusion.27, bf16[512,4096]{1,0:T(8,128)(2,1)} %get-tuple-element.27, bf16[768,4096]{1,0:T(8,128)(2,1)S(1)} %copy-done.9), kind=kOutput, calls=%fused_computation.4 | convolution fusion | flops 3223584768 | bytes 15990784 | tf_op jit(solution)/shard_map/cond/branch_1_fun/dot_general | solution.py:51
  136.5 6.2 %fusion.28 = bf16[512,4096]{1,0:T(8,128)(2,1)} fusion(bf16[512,768]{1,0:T(8,128)(2,1)} %get-tuple-element.101, bf16[768,4096]{1,0:T(8,128)(2,1)S(1)} %bitcast.79), kind=kOutput, calls=%fused_computation.76 | convolution fusion | flops 3221225472 | bytes 11272192 | tf_op jit(solution)/shard_map/cond/branch_1_fun/dot_general | solution.py:54
  142.7 69.3 %all-to-all-done.1 = bf16[8,64,4096]{2,1,0:T(8,128)(2,1)} async-done(((bf16[8,64,4096]{2,1,0:T(8,128)(2,1)}), bf16[8,64,4096]{2,1,0:T(8,128)(2,1)}, u32[]{:S(2)}, u32[]{:S(2)}) %all-to-all-start.1) | async-done | bytes 4194336 | tf_op jit(solution)/shard_map/all_to_all | solution.py:43
  212.0 9.0 %multiply_convert_fusion.3 = (bf16[512,768]{1,0:T(8,128)(2,1)S(1)}, bf16[512,768]{1,0:T(8,128)(2,1)S(1)}) fusion(f32[512,768]{1,0:T(8,128)} %get-tuple-element.55, f32[512,768]{1,0:T(8,128)} %get-tuple-element.56, f32[512,768]{1,0:T(8,128)} %get-tuple-element.54, bf16[512,4096]{1,0:T(8,128)(2,1)} %bitcast.4, bf16[1,768,4096]{2,1,0:T(8,128)(2,1)} %param.14), kind=kOutput, calls=%fused_computation.20 | convolution fusion | flops 3225157632 | bytes 16777216 | tf_op jit(solution)/shard_map/dot_general | solution.py:71
  222.6 11.8 %multiply_convert_fusion = bf16[1536,4096]{1,0:T(8,128)(2,1)} fusion(bf16[512,1536]{0,1:T(8,128)(2,1)S(1)} %bitcast.68, bf16[512,4096]{1,0:T(8,128)(2,1)} %bitcast.7), kind=kOutput, calls=%fused_computation.8 | convolution fusion | flops 6455033856 | bytes 18350080 | tf_op jit(solution)/shard_map/weight_grads/rf,rd->fd/dot_general | solution.py:93
  234.4 4.6 %all-to-all-start.2 = ((bf16[8,64,4096]{2,1,0:T(8,128)(2,1)}), bf16[8,64,4096]{2,1,0:T(8,128)(2,1)}, u32[]{:S(2)}, u32[]{:S(2)}) async-start(bf16[8,64,4096]{2,1,0:T(8,128)(2,1)} %bitcast.15), calls=%async_computation.3 | async-start | bytes 8388608 | tf_op jit(solution)/shard_map/all_to_all | solution.py:63
  239.3 9.4 %multiply_convert_fusion.1 = bf16[768,4096]{1,0:T(8,128)(2,1)} fusion(bf16[512,4096]{1,0:T(8,128)(2,1)} %bitcast.4, bf16[512,768]{1,0:T(8,128)(2,1)} %get-tuple-element.66), kind=kOutput, calls=%fused_computation.9 | convolution fusion | flops 3227516928 | bytes 11272192 | tf_op jit(solution)/shard_map/weight_grads/rf,rd->fd/dot_general | solution.py:83
  248.9 5.6 %fusion.18 = f32[512,4096]{1,0:T(8,128)S(1)} fusion(bf16[512,768]{1,0:T(8,128)(2,1)S(1)} %get-tuple-element.76, bf16[1,768,4096]{2,1,0:T(8,128)(2,1)} %param.12), kind=kOutput, calls=%fused_computation.66 | convolution fusion | flops 3221225472 | bytes 15466496 | tf_op jit(solution)/shard_map/dot_general | solution.py:77
  254.5 6.8 %add_convert_fusion = bf16[512,4096]{1,0:T(8,128)(2,1)S(1)} fusion(f32[512,4096]{1,0:T(8,128)S(1)} %fusion.18, bf16[512,768]{1,0:T(8,128)(2,1)S(1)} %copy-done.4, bf16[1,768,4096]{2,1,0:T(8,128)(2,1)} %param.13), kind=kOutput, calls=%fused_computation.10 | convolution fusion | flops 3225419776 | bytes 19660800 | tf_op jit(solution)/shard_map/dot_general | solution.py:78
  261.3 2.1 constant_dynamic-slice_fusion
  263.4 3.4 collective-permute-start.6
  267.3 1.7 collective-permute-start.2
  269.9 63.6 %all-to-all-done.2 = bf16[8,64,4096]{2,1,0:T(8,128)(2,1)} async-done(((bf16[8,64,4096]{2,1,0:T(8,128)(2,1)}), bf16[8,64,4096]{2,1,0:T(8,128)(2,1)}, u32[]{:S(2)}, u32[]{:S(2)}) %all-to-all-start.2) | async-done | bytes 4194336 | tf_op jit(solution)/shard_map/all_to_all | solution.py:63
  333.5 3.5 fusion.9
  337.0 2.0 fusion.4
  339.6 16.5 %collective-permute-done = bf16[64,4096]{1,0:T(8,128)(2,1)} collective-permute-done((bf16[64,4096]{1,0:T(8,128)(2,1)}, bf16[64,4096]{1,0:T(8,128)(2,1)}, u32[]{:S(2)}, u32[]{:S(2)}) %collective-permute-start) | collective-permute-done | bytes 524320 | tf_op jit(solution)/shard_map/ppermute | solution.py:106
  356.1 16.2 %collective-permute-start.1 = (bf16[64,4096]{1,0:T(8,128)(2,1)}, bf16[64,4096]{1,0:T(8,128)(2,1)S(1)}, u32[]{:S(2)}, u32[]{:S(2)}) collective-permute-start(bf16[64,4096]{1,0:T(8,128)(2,1)} %get-tuple-element.83), channel_id=1, source_target_pairs={{0,2},{1,3},{2,4},{3,5},{4,6},{5,7},{6,0},{7,1},{8,10},{9,11},{10,... | collective-permute-start | bytes 1572872 | tf_op jit(solution)/shard_map/ppermute | solution.py:106
  372.3 1.9 constant_dynamic-update-slice_fusion.6
  374.2 3.9 fusion.24
  378.1 8.8 %collective-permute-done.1 = bf16[64,4096]{1,0:T(8,128)(2,1)S(1)} collective-permute-done((bf16[64,4096]{1,0:T(8,128)(2,1)}, bf16[64,4096]{1,0:T(8,128)(2,1)S(1)}, u32[]{:S(2)}, u32[]{:S(2)}) %collective-permute-start.1) | collective-permute-done | bytes 524320 | tf_op jit(solution)/shard_map/ppermute | solution.py:106
  387.0 22.5 %collective-permute-start.3 = (bf16[64,4096]{1,0:T(8,128)(2,1)S(1)}, bf16[64,4096]{1,0:T(8,128)(2,1)S(1)}, u32[]{:S(2)}, u32[]{:S(2)}) collective-permute-start(bf16[64,4096]{1,0:T(8,128)(2,1)S(1)} %copy-done.5), channel_id=1, source_target_pairs={{0,4},{1,5},{2,6},{3,7},{4,0},{5,1},{6,2},{7,3},{8,12},{9,13},{10,... | collective-permute-start | bytes 1572872 | tf_op jit(solution)/shard_map/ppermute | solution.py:106
  411.2 11.6 %collective-permute-done.3 = bf16[64,4096]{1,0:T(8,128)(2,1)S(1)} collective-permute-done((bf16[64,4096]{1,0:T(8,128)(2,1)S(1)}, bf16[64,4096]{1,0:T(8,128)(2,1)S(1)}, u32[]{:S(2)}, u32[]{:S(2)}) %collective-permute-start.3) | collective-permute-done | bytes 524320 | tf_op jit(solution)/shard_map/ppermute | solution.py:106
  425.3 0.9 constant_dynamic-update-slice_fusion
  426.2 4.0 convolution_convert_fusion.1
  (57 shorter events, 10.1 us)
Async XLA Ops:
  7.2 2.3 copy-start
  12.8 6.5 %copy-start.7 = (f32[128,2]{0,1:T(2,128)S(1)}, f32[128,2]{0,1:T(2,128)}, u32[]{:S(2)}) copy-start(f32[128,2]{0,1:T(2,128)} %param.11) | copy-start | bytes 3076
  12.8 6.6 %copy-start.2 = (bf16[128,4096]{1,0:T(8,128)(2,1)S(1)}, bf16[128,4096]{1,0:T(8,128)(2,1)}, u32[]{:S(2)}) copy-start(bf16[128,4096]{1,0:T(8,128)(2,1)} %param.15) | copy-start | bytes 3145732
  12.8 100.6 %all-to-all-start = ((bf16[8,64,4096]{2,1,0:T(8,128)(2,1)}), bf16[8,64,4096]{2,1,0:T(8,128)(2,1)}, u32[]{:S(2)}, u32[]{:S(2)}) async-start(bf16[8,64,4096]{2,1,0:T(8,128)(2,1)} %bitcast.63), calls=%async_computation | async-start | bytes 8388608 | tf_op jit(solution)/shard_map/all_to_all | solution.py:41
  113.3 4.7 %copy-start.6 = (s32[128,2]{0,1:T(2,128)S(1)}, s32[128,2]{0,1:T(2,128)}, u32[]{:S(2)}) copy-start(s32[128,2]{0,1:T(2,128)} %param.10) | copy-start | bytes 3076
  113.3 98.7 %all-to-all-start.1 = ((bf16[8,64,4096]{2,1,0:T(8,128)(2,1)}), bf16[8,64,4096]{2,1,0:T(8,128)(2,1)}, u32[]{:S(2)}, u32[]{:S(2)}) async-start(bf16[8,64,4096]{2,1,0:T(8,128)(2,1)} %bitcast.62), calls=%async_computation.1 | async-start | bytes 8388608 | tf_op jit(solution)/shard_map/all_to_all | solution.py:43
  118.0 256.2 %reduce-scatter.3.cloned.1.call-start = ((), (), s32[]{:S(2)}) async-start(), calls=%async_computation.5 | async-start | bytes 15728640 | tf_op jit(solution)/shard_map/reduce_scatter | solution.py:96
  119.5 8.8 %copy-start.9 = (bf16[768,4096]{1,0:T(8,128)(2,1)S(1)}, bf16[768,4096]{1,0:T(8,128)(2,1)}, u32[]{:S(2)}) copy-start(bf16[768,4096]{1,0:T(8,128)(2,1)} %get-tuple-element.29) | copy-start | bytes 18874372 | tf_op jit(solution)/shard_map/conditional
  119.5 17.0 %slice-start.2 = ((s8[6291456]{0:T(1024)(128)(4,1)}), s8[4194304]{0:T(1024)(128)(4,1)S(1)}, s32[]{:S(2)}) async-start(s8[6291456]{0:T(1024)(128)(4,1)} %bitcast.78), calls=%async_computation.9 | async-start | bytes 8388608 | tf_op jit(solution)/shard_map/conditional
  128.3 8.2 %slice-start.3 = ((s8[6291456]{0:T(1024)(128)(4,1)}), s8[2097152]{0:T(1024)(128)(4,1)S(1)}, s32[]{:S(2)}) async-start(s8[6291456]{0:T(1024)(128)(4,1)} %bitcast.78), calls=%async_computation.10 | async-start | bytes 4194304 | tf_op jit(solution)/shard_map/conditional
  221.1 0.9 copy-start.3
  234.4 99.1 %all-to-all-start.2 = ((bf16[8,64,4096]{2,1,0:T(8,128)(2,1)}), bf16[8,64,4096]{2,1,0:T(8,128)(2,1)}, u32[]{:S(2)}, u32[]{:S(2)}) async-start(bf16[8,64,4096]{2,1,0:T(8,128)(2,1)} %bitcast.15), calls=%async_computation.3 | async-start | bytes 8388608 | tf_op jit(solution)/shard_map/all_to_all | solution.py:63
  239.0 191.2 %reduce-scatter.5.cloned.1.call-start = ((), (), s32[]{:S(2)}) async-start(), calls=%async_computation.6 | async-start | bytes 7864320 | tf_op jit(solution)/shard_map/reduce_scatter | solution.py:95
  248.9 5.6 %copy-start.4 = (bf16[512,768]{1,0:T(8,128)(2,1)S(1)}, bf16[512,768]{1,0:T(8,128)(2,1)}, u32[]{:S(2)}) copy-start(bf16[512,768]{1,0:T(8,128)(2,1)} %copy-done.3) | copy-start | bytes 2359300
  263.4 161.9 %collective-permute-start.6 = (bf16[64,4096]{1,0:T(8,128)(2,1)}, bf16[64,4096]{1,0:T(8,128)(2,1)S(1)}, u32[]{:S(2)}, u32[]{:S(2)}) collective-permute-start(bf16[64,4096]{1,0:T(8,128)(2,1)} %get-tuple-element.78), channel_id=1, source_target_pairs={{0,7},{1,0},{2,1},{3,2},{4,3},{5,4},{6,5},{7,6},{8,15},{9,8},{10,9... | collective-permute-start | bytes 1572872 | tf_op jit(solution)/shard_map/ppermute | solution.py:106
  266.8 157.7 %collective-permute-start.5 = (bf16[64,4096]{1,0:T(8,128)(2,1)}, bf16[64,4096]{1,0:T(8,128)(2,1)S(1)}, u32[]{:S(2)}, u32[]{:S(2)}) collective-permute-start(bf16[64,4096]{1,0:T(8,128)(2,1)} %get-tuple-element.79), channel_id=1, source_target_pairs={{0,6},{1,7},{2,0},{3,1},{4,2},{5,3},{6,4},{7,5},{8,14},{9,15},{10,... | collective-permute-start | bytes 1572872 | tf_op jit(solution)/shard_map/ppermute | solution.py:106
  267.3 156.3 %collective-permute-start.4 = (bf16[64,4096]{1,0:T(8,128)(2,1)}, bf16[64,4096]{1,0:T(8,128)(2,1)S(1)}, u32[]{:S(2)}, u32[]{:S(2)}) collective-permute-start(bf16[64,4096]{1,0:T(8,128)(2,1)} %get-tuple-element.80), channel_id=1, source_target_pairs={{0,5},{1,6},{2,7},{3,0},{4,1},{5,2},{6,3},{7,4},{8,13},{9,14},{10,... | collective-permute-start | bytes 1572872 | tf_op jit(solution)/shard_map/ppermute | solution.py:106
  267.3 143.0 %collective-permute-start.2 = (bf16[64,4096]{1,0:T(8,128)(2,1)}, bf16[64,4096]{1,0:T(8,128)(2,1)S(1)}, u32[]{:S(2)}, u32[]{:S(2)}) collective-permute-start(bf16[64,4096]{1,0:T(8,128)(2,1)} %get-tuple-element.82), channel_id=1, source_target_pairs={{0,3},{1,4},{2,5},{3,6},{4,7},{5,0},{6,1},{7,2},{8,11},{9,12},{10,... | collective-permute-start | bytes 1572872 | tf_op jit(solution)/shard_map/ppermute | solution.py:106
  269.1 87.0 %collective-permute-start = (bf16[64,4096]{1,0:T(8,128)(2,1)}, bf16[64,4096]{1,0:T(8,128)(2,1)}, u32[]{:S(2)}, u32[]{:S(2)}) collective-permute-start(bf16[64,4096]{1,0:T(8,128)(2,1)} %get-tuple-element.84), channel_id=1, source_target_pairs={{0,1},{1,2},{2,3},{3,4},{4,5},{5,6},{6,7},{7,0},{8,9},{9,10},{10,1... | collective-permute-start | bytes 1572872 | tf_op jit(solution)/shard_map/ppermute | solution.py:106
  339.0 48.0 %copy-start.5 = (bf16[64,4096]{1,0:T(8,128)(2,1)S(1)}, bf16[64,4096]{1,0:T(8,128)(2,1)}, u32[]{:S(2)}) copy-start(bf16[64,4096]{1,0:T(8,128)(2,1)} %get-tuple-element.57) | copy-start | bytes 1572868
  356.1 30.9 %collective-permute-start.1 = (bf16[64,4096]{1,0:T(8,128)(2,1)}, bf16[64,4096]{1,0:T(8,128)(2,1)S(1)}, u32[]{:S(2)}, u32[]{:S(2)}) collective-permute-start(bf16[64,4096]{1,0:T(8,128)(2,1)} %get-tuple-element.83), channel_id=1, source_target_pairs={{0,2},{1,3},{2,4},{3,5},{4,6},{5,7},{6,0},{7,1},{8,10},{9,11},{10,... | collective-permute-start | bytes 1572872 | tf_op jit(solution)/shard_map/ppermute | solution.py:106
  387.0 35.8 %collective-permute-start.3 = (bf16[64,4096]{1,0:T(8,128)(2,1)S(1)}, bf16[64,4096]{1,0:T(8,128)(2,1)S(1)}, u32[]{:S(2)}, u32[]{:S(2)}) collective-permute-start(bf16[64,4096]{1,0:T(8,128)(2,1)S(1)} %copy-done.5), channel_id=1, source_target_pairs={{0,4},{1,5},{2,6},{3,7},{4,0},{5,1},{6,2},{7,3},{8,12},{9,13},{10,... | collective-permute-start | bytes 1572872 | tf_op jit(solution)/shard_map/ppermute | solution.py:106
  422.8 7.4 %copy-start.1 = (bf16[128,4096]{1,0:T(8,128)(2,1)S(1)}, bf16[128,4096]{1,0:T(8,128)(2,1)}, u32[]{:S(2)}) copy-start(bf16[128,4096]{1,0:T(8,128)(2,1)} %param.9) | copy-start | bytes 3145732
Sparse Core Ops, SparseCore 0:
  234.5 119.6 reduce-scatter.2
  357.8 70.2 reduce-scatter.4

commit v13 on v12

--- a/solution.py
+++ b/solution.py
@@ -26,7 +26,9 @@
     target = slot_targets(expert_ids, experts, capacity)
     slot_iota = jnp.arange(slots, dtype=jnp.int32)
     hit = target.T[:, :, None] == slot_iota[None, None, :]
-    send_onehot = jnp.any(hit, axis=0).T.astype(jnp.bfloat16)
+    send_onehot = jnp.any(
+        slot_iota[:, None, None] == target[None, :, :], axis=2
+    ).astype(jnp.bfloat16)
     weight_pair = jnp.sum(
         jnp.where(hit, combine.T[:, :, None], jnp.zeros((), jnp.float32)), axis=(0, 1)
     )

time: 438 us -> 438 us (level)
  no operation moved by 1% of the time
where the time goes in v13:
time: 438 us; the launch traced here: 437 us
  waiting for transfers between devices  261 us (60%)
  matrix products  80 us (18%)
  starting transfers between devices  61.2 us (14%)
  local copies, waits for them, and re-layouts  16 us (4%)
  between operations  15 us (3%)
    all_to_all x1, waiting for transfers between devices, per_device(): lax.all_to_all(send_rows, 'expert', split_axis=0, concat_axis=0, tiled=True)  90.8 us
    all_to_all x1, waiting for transfers between devices, per_device(): lax.all_to_all(send_grads, 'expert', split_axis=0, concat_axis=0, tiled=T...  69.3 us
    all_to_all x1, waiting for transfers between devices, per_device(): lax.all_to_all(expert_out.reshape(experts, capacity, model_width), 'exper...  63.6 us
    ppermute x7, starting transfers between devices, per_device(): lax.ppermute(chunk, 'expert', [(j, (j + shift) % experts) for j in range(...  45.2 us
    ppermute x7, waiting for transfers between devices, per_device(): lax.ppermute(chunk, 'expert', [(j, (j + shift) % experts) for j in range(...  37 us
    dot_general x1, matrix products, per_device(): jnp.einsum('rf,rd->fd', gate_up_pre, in_rows, preferred_element_type=jnp....  11.8 us
    dot_general x1, matrix products, per_device(): jnp.einsum('rf,rd->fd', activated, out_grads, preferred_element_type=jnp....  9.38 us
    dot_general x1, matrix products, per_device(): grad_act = jnp.dot(out_grads, w_down.T, preferred_element_type=jnp.float32)  9.05 us
  transfers between devices with their start and end apart: 12, of which 6 were waited for; matrix products, arithmetic and copies ran while one was open for 16% of the time, Pallas kernels for 0%

profile of v13, /device:TPU:0, one launch (start us, length us, event | category | flops | bytes accessed | tf_op | source)
XLA Modules:
  0.0 436.9 jit_solution(16438851046727026995)
XLA Ops:
  7.2 0.9 copy.58
  9.4 3.2 convolution_convert_fusion
  12.6 6.5 %all-to-all-start = ((bf16[8,64,4096]{2,1,0:T(8,128)(2,1)}), bf16[8,64,4096]{2,1,0:T(8,128)(2,1)}, u32[]{:S(2)}, u32[]{:S(2)}) async-start(bf16[8,64,4096]{2,1,0:T(8,128)(2,1)} %bitcast.61), calls=%async_computation | async-start | bytes 8388608 | tf_op jit(solution)/shard_map/all_to_all | solution.py:43
  19.3 3.2 multiply_convert_fusion.2
  22.5 90.8 %all-to-all-done = bf16[8,64,4096]{2,1,0:T(8,128)(2,1)} async-done(((bf16[8,64,4096]{2,1,0:T(8,128)(2,1)}), bf16[8,64,4096]{2,1,0:T(8,128)(2,1)}, u32[]{:S(2)}, u32[]{:S(2)}) %all-to-all-start) | async-done | bytes 4194336 | tf_op jit(solution)/shard_map/all_to_all | solution.py:43
  113.2 4.7 %all-to-all-start.1 = ((bf16[8,64,4096]{2,1,0:T(8,128)(2,1)}), bf16[8,64,4096]{2,1,0:T(8,128)(2,1)}, u32[]{:S(2)}, u32[]{:S(2)}) async-start(bf16[8,64,4096]{2,1,0:T(8,128)(2,1)} %bitcast.60), calls=%async_computation.1 | async-start | bytes 8388608 | tf_op jit(solution)/shard_map/all_to_all | solution.py:45
  119.1 23.5 %conditional.2 = (f32[512,768]{1,0:T(8,128)}, f32[512,768]{1,0:T(8,128)}, f32[512,768]{1,0:T(8,128)}, bf16[512,768]{1,0:T(8,128)(2,1)}, bf16[512,4096]{1,0:T(8,128)(2,1)}) conditional(s32[]{:T(128)} %bitcast.6, (bf16[512,4096]{1,0:T(8,128)(2,1)}, bf16[768,4096]{1,0:T(8,128)(2,1)}, bf16[768,4096]{1,0:T(8,128)(2,1)}, ...), branch_computations={%region_3.4_spmd, %region_4.5_spmd} | conditional | flops 9666035712 | bytes 83361904
  119.4 8.8 %fusion.25 = f32[512,768]{1,0:T(8,128)} fusion(bf16[512,4096]{1,0:T(8,128)(2,1)} %get-tuple-element.27, bf16[768,4096]{1,0:T(8,128)(2,1)} %get-tuple-element.28), kind=kOutput, calls=%fused_computation.74 | convolution fusion | flops 3221225472 | bytes 12058624 | tf_op jit(solution)/shard_map/cond/branch_1_fun/dot_general | solution.py:52
  128.2 8.2 %multiply_multiply_fusion.1 = (bf16[512,768]{1,0:T(8,128)(2,1)}, f32[512,768]{1,0:T(8,128)}, f32[512,768]{1,0:T(8,128)}) fusion(f32[512,768]{1,0:T(8,128)} %fusion.25, bf16[512,4096]{1,0:T(8,128)(2,1)} %get-tuple-element.27, bf16[768,4096]{1,0:T(8,128)(2,1)S(1)} %copy-done.9), kind=kOutput, calls=%fused_computation.4 | convolution fusion | flops 3223584768 | bytes 15990784 | tf_op jit(solution)/shard_map/cond/branch_1_fun/dot_general | solution.py:53
  136.4 6.2 %fusion.26 = bf16[512,4096]{1,0:T(8,128)(2,1)} fusion(bf16[512,768]{1,0:T(8,128)(2,1)} %get-tuple-element.100, bf16[768,4096]{1,0:T(8,128)(2,1)S(1)} %bitcast.79), kind=kOutput, calls=%fused_computation.75 | convolution fusion | flops 3221225472 | bytes 11272192 | tf_op jit(solution)/shard_map/cond/branch_1_fun/dot_general | solution.py:56
  142.6 69.3 %all-to-all-done.1 = bf16[8,64,4096]{2,1,0:T(8,128)(2,1)} async-done(((bf16[8,64,4096]{2,1,0:T(8,128)(2,1)}), bf16[8,64,4096]{2,1,0:T(8,128)(2,1)}, u32[]{:S(2)}, u32[]{:S(2)}) %all-to-all-start.1) | async-done | bytes 4194336 | tf_op jit(solution)/shard_map/all_to_all | solution.py:45
  211.9 9.0 %multiply_convert_fusion.3 = (bf16[512,768]{1,0:T(8,128)(2,1)S(1)}, bf16[512,768]{1,0:T(8,128)(2,1)S(1)}) fusion(f32[512,768]{1,0:T(8,128)} %get-tuple-element.55, f32[512,768]{1,0:T(8,128)} %get-tuple-element.56, f32[512,768]{1,0:T(8,128)} %get-tuple-element.54, bf16[512,4096]{1,0:T(8,128)(2,1)} %bitcast.4, bf16[1,768,4096]{2,1,0:T(8,128)(2,1)} %param.14), kind=kOutput, calls=%fused_computation.20 | convolution fusion | flops 3225157632 | bytes 16777216 | tf_op jit(solution)/shard_map/dot_general | solution.py:73
  222.5 11.8 %multiply_convert_fusion = bf16[1536,4096]{1,0:T(8,128)(2,1)} fusion(bf16[512,1536]{0,1:T(8,128)(2,1)S(1)} %bitcast.66, bf16[512,4096]{1,0:T(8,128)(2,1)} %bitcast.7), kind=kOutput, calls=%fused_computation.8 | convolution fusion | flops 6455033856 | bytes 18350080 | tf_op jit(solution)/shard_map/weight_grads/rf,rd->fd/dot_general | solution.py:95
  234.3 4.6 %all-to-all-start.2 = ((bf16[8,64,4096]{2,1,0:T(8,128)(2,1)}), bf16[8,64,4096]{2,1,0:T(8,128)(2,1)}, u32[]{:S(2)}, u32[]{:S(2)}) async-start(bf16[8,64,4096]{2,1,0:T(8,128)(2,1)} %bitcast.15), calls=%async_computation.3 | async-start | bytes 8388608 | tf_op jit(solution)/shard_map/all_to_all | solution.py:65
  239.1 9.4 %multiply_convert_fusion.1 = bf16[768,4096]{1,0:T(8,128)(2,1)} fusion(bf16[512,4096]{1,0:T(8,128)(2,1)} %bitcast.4, bf16[512,768]{1,0:T(8,128)(2,1)} %get-tuple-element.66), kind=kOutput, calls=%fused_computation.9 | convolution fusion | flops 3227516928 | bytes 11272192 | tf_op jit(solution)/shard_map/weight_grads/rf,rd->fd/dot_general | solution.py:85
  248.8 5.6 %fusion.18 = f32[512,4096]{1,0:T(8,128)S(1)} fusion(bf16[512,768]{1,0:T(8,128)(2,1)S(1)} %get-tuple-element.78, bf16[1,768,4096]{2,1,0:T(8,128)(2,1)} %param.12), kind=kOutput, calls=%fused_computation.67 | convolution fusion | flops 3221225472 | bytes 15466496 | tf_op jit(solution)/shard_map/dot_general | solution.py:79
  254.4 6.8 %add_convert_fusion = bf16[512,4096]{1,0:T(8,128)(2,1)S(1)} fusion(f32[512,4096]{1,0:T(8,128)S(1)} %fusion.18, bf16[512,768]{1,0:T(8,128)(2,1)S(1)} %copy-done.4, bf16[1,768,4096]{2,1,0:T(8,128)(2,1)} %param.13), kind=kOutput, calls=%fused_computation.10 | convolution fusion | flops 3225419776 | bytes 19660800 | tf_op jit(solution)/shard_map/dot_general | solution.py:80
  261.2 2.1 constant_dynamic-slice_fusion
  263.3 3.4 collective-permute-start.6
  267.2 1.7 collective-permute-start.2
  269.8 63.6 %all-to-all-done.2 = bf16[8,64,4096]{2,1,0:T(8,128)(2,1)} async-done(((bf16[8,64,4096]{2,1,0:T(8,128)(2,1)}), bf16[8,64,4096]{2,1,0:T(8,128)(2,1)}, u32[]{:S(2)}, u32[]{:S(2)}) %all-to-all-start.2) | async-done | bytes 4194336 | tf_op jit(solution)/shard_map/all_to_all | solution.py:65
  333.4 3.5 fusion.9
  336.9 2.0 fusion.4
  339.5 16.5 %collective-permute-done = bf16[64,4096]{1,0:T(8,128)(2,1)} collective-permute-done((bf16[64,4096]{1,0:T(8,128)(2,1)}, bf16[64,4096]{1,0:T(8,128)(2,1)}, u32[]{:S(2)}, u32[]{:S(2)}) %collective-permute-start) | collective-permute-done | bytes 524320 | tf_op jit(solution)/shard_map/ppermute | solution.py:108
  356.0 16.2 %collective-permute-start.1 = (bf16[64,4096]{1,0:T(8,128)(2,1)}, bf16[64,4096]{1,0:T(8,128)(2,1)S(1)}, u32[]{:S(2)}, u32[]{:S(2)}) collective-permute-start(bf16[64,4096]{1,0:T(8,128)(2,1)} %get-tuple-element.85), channel_id=1, source_target_pairs={{0,2},{1,3},{2,4},{3,5},{4,6},{5,7},{6,0},{7,1},{8,10},{9,11},{10,... | collective-permute-start | bytes 1572872 | tf_op jit(solution)/shard_map/ppermute | solution.py:108
  372.2 1.9 constant_dynamic-update-slice_fusion.6
  374.1 3.9 fusion.22
  378.0 8.8 %collective-permute-done.1 = bf16[64,4096]{1,0:T(8,128)(2,1)S(1)} collective-permute-done((bf16[64,4096]{1,0:T(8,128)(2,1)}, bf16[64,4096]{1,0:T(8,128)(2,1)S(1)}, u32[]{:S(2)}, u32[]{:S(2)}) %collective-permute-start.1) | collective-permute-done | bytes 524320 | tf_op jit(solution)/shard_map/ppermute | solution.py:108
  386.8 22.5 %collective-permute-start.3 = (bf16[64,4096]{1,0:T(8,128)(2,1)S(1)}, bf16[64,4096]{1,0:T(8,128)(2,1)S(1)}, u32[]{:S(2)}, u32[]{:S(2)}) collective-permute-start(bf16[64,4096]{1,0:T(8,128)(2,1)S(1)} %copy-done.5), channel_id=1, source_target_pairs={{0,4},{1,5},{2,6},{3,7},{4,0},{5,1},{6,2},{7,3},{8,12},{9,13},{10,... | collective-permute-start | bytes 1572872 | tf_op jit(solution)/shard_map/ppermute | solution.py:108
  411.0 11.6 %collective-permute-done.3 = bf16[64,4096]{1,0:T(8,128)(2,1)S(1)} collective-permute-done((bf16[64,4096]{1,0:T(8,128)(2,1)S(1)}, bf16[64,4096]{1,0:T(8,128)(2,1)S(1)}, u32[]{:S(2)}, u32[]{:S(2)}) %collective-permute-start.3) | collective-permute-done | bytes 524320 | tf_op jit(solution)/shard_map/ppermute | solution.py:108
  425.2 0.9 constant_dynamic-update-slice_fusion
  426.1 4.0 convolution_convert_fusion.1
  (57 shorter events, 10.1 us)
Async XLA Ops:
  7.2 2.2 copy-start
  12.6 6.5 %copy-start.7 = (f32[128,2]{0,1:T(2,128)S(1)}, f32[128,2]{0,1:T(2,128)}, u32[]{:S(2)}) copy-start(f32[128,2]{0,1:T(2,128)} %param.11) | copy-start | bytes 3076
  12.6 6.6 %copy-start.2 = (bf16[128,4096]{1,0:T(8,128)(2,1)S(1)}, bf16[128,4096]{1,0:T(8,128)(2,1)}, u32[]{:S(2)}) copy-start(bf16[128,4096]{1,0:T(8,128)(2,1)} %param.15) | copy-start | bytes 3145732
  12.6 100.6 %all-to-all-start = ((bf16[8,64,4096]{2,1,0:T(8,128)(2,1)}), bf16[8,64,4096]{2,1,0:T(8,128)(2,1)}, u32[]{:S(2)}, u32[]{:S(2)}) async-start(bf16[8,64,4096]{2,1,0:T(8,128)(2,1)} %bitcast.61), calls=%async_computation | async-start | bytes 8388608 | tf_op jit(solution)/shard_map/all_to_all | solution.py:43
  113.2 4.7 %copy-start.6 = (s32[128,2]{0,1:T(2,128)S(1)}, s32[128,2]{0,1:T(2,128)}, u32[]{:S(2)}) copy-start(s32[128,2]{0,1:T(2,128)} %param.10) | copy-start | bytes 3076
  113.2 98.7 %all-to-all-start.1 = ((bf16[8,64,4096]{2,1,0:T(8,128)(2,1)}), bf16[8,64,4096]{2,1,0:T(8,128)(2,1)}, u32[]{:S(2)}, u32[]{:S(2)}) async-start(bf16[8,64,4096]{2,1,0:T(8,128)(2,1)} %bitcast.60), calls=%async_computation.1 | async-start | bytes 8388608 | tf_op jit(solution)/shard_map/all_to_all | solution.py:45
  117.9 256.2 %reduce-scatter.3.cloned.1.call-start = ((), (), s32[]{:S(2)}) async-start(), calls=%async_computation.5 | async-start | bytes 15728640 | tf_op jit(solution)/shard_map/reduce_scatter | solution.py:98
  119.3 8.8 %copy-start.9 = (bf16[768,4096]{1,0:T(8,128)(2,1)S(1)}, bf16[768,4096]{1,0:T(8,128)(2,1)}, u32[]{:S(2)}) copy-start(bf16[768,4096]{1,0:T(8,128)(2,1)} %get-tuple-element.29) | copy-start | bytes 18874372 | tf_op jit(solution)/shard_map/conditional
  119.3 17.0 %slice-start.2 = ((s8[6291456]{0:T(1024)(128)(4,1)}), s8[4194304]{0:T(1024)(128)(4,1)S(1)}, s32[]{:S(2)}) async-start(s8[6291456]{0:T(1024)(128)(4,1)} %bitcast.78), calls=%async_computation.9 | async-start | bytes 8388608 | tf_op jit(solution)/shard_map/conditional
  128.2 8.2 %slice-start.3 = ((s8[6291456]{0:T(1024)(128)(4,1)}), s8[2097152]{0:T(1024)(128)(4,1)S(1)}, s32[]{:S(2)}) async-start(s8[6291456]{0:T(1024)(128)(4,1)} %bitcast.78), calls=%async_computation.10 | async-start | bytes 4194304 | tf_op jit(solution)/shard_map/conditional
  221.0 0.9 copy-start.3
  234.3 99.1 %all-to-all-start.2 = ((bf16[8,64,4096]{2,1,0:T(8,128)(2,1)}), bf16[8,64,4096]{2,1,0:T(8,128)(2,1)}, u32[]{:S(2)}, u32[]{:S(2)}) async-start(bf16[8,64,4096]{2,1,0:T(8,128)(2,1)} %bitcast.15), calls=%async_computation.3 | async-start | bytes 8388608 | tf_op jit(solution)/shard_map/all_to_all | solution.py:65
  238.9 191.2 %reduce-scatter.5.cloned.1.call-start = ((), (), s32[]{:S(2)}) async-start(), calls=%async_computation.6 | async-start | bytes 7864320 | tf_op jit(solution)/shard_map/reduce_scatter | solution.py:97
  248.8 5.6 %copy-start.4 = (bf16[512,768]{1,0:T(8,128)(2,1)S(1)}, bf16[512,768]{1,0:T(8,128)(2,1)}, u32[]{:S(2)}) copy-start(bf16[512,768]{1,0:T(8,128)(2,1)} %copy-done.3) | copy-start | bytes 2359300
  263.3 161.9 %collective-permute-start.6 = (bf16[64,4096]{1,0:T(8,128)(2,1)}, bf16[64,4096]{1,0:T(8,128)(2,1)S(1)}, u32[]{:S(2)}, u32[]{:S(2)}) collective-permute-start(bf16[64,4096]{1,0:T(8,128)(2,1)} %get-tuple-element.80), channel_id=1, source_target_pairs={{0,7},{1,0},{2,1},{3,2},{4,3},{5,4},{6,5},{7,6},{8,15},{9,8},{10,9... | collective-permute-start | bytes 1572872 | tf_op jit(solution)/shard_map/ppermute | solution.py:108
  266.7 157.7 %collective-permute-start.5 = (bf16[64,4096]{1,0:T(8,128)(2,1)}, bf16[64,4096]{1,0:T(8,128)(2,1)S(1)}, u32[]{:S(2)}, u32[]{:S(2)}) collective-permute-start(bf16[64,4096]{1,0:T(8,128)(2,1)} %get-tuple-element.81), channel_id=1, source_target_pairs={{0,6},{1,7},{2,0},{3,1},{4,2},{5,3},{6,4},{7,5},{8,14},{9,15},{10,... | collective-permute-start | bytes 1572872 | tf_op jit(solution)/shard_map/ppermute | solution.py:108
  267.2 156.3 %collective-permute-start.4 = (bf16[64,4096]{1,0:T(8,128)(2,1)}, bf16[64,4096]{1,0:T(8,128)(2,1)S(1)}, u32[]{:S(2)}, u32[]{:S(2)}) collective-permute-start(bf16[64,4096]{1,0:T(8,128)(2,1)} %get-tuple-element.82), channel_id=1, source_target_pairs={{0,5},{1,6},{2,7},{3,0},{4,1},{5,2},{6,3},{7,4},{8,13},{9,14},{10,... | collective-permute-start | bytes 1572872 | tf_op jit(solution)/shard_map/ppermute | solution.py:108
  267.2 143.0 %collective-permute-start.2 = (bf16[64,4096]{1,0:T(8,128)(2,1)}, bf16[64,4096]{1,0:T(8,128)(2,1)S(1)}, u32[]{:S(2)}, u32[]{:S(2)}) collective-permute-start(bf16[64,4096]{1,0:T(8,128)(2,1)} %get-tuple-element.84), channel_id=1, source_target_pairs={{0,3},{1,4},{2,5},{3,6},{4,7},{5,0},{6,1},{7,2},{8,11},{9,12},{10,... | collective-permute-start | bytes 1572872 | tf_op jit(solution)/shard_map/ppermute | solution.py:108
  269.0 87.0 %collective-permute-start = (bf16[64,4096]{1,0:T(8,128)(2,1)}, bf16[64,4096]{1,0:T(8,128)(2,1)}, u32[]{:S(2)}, u32[]{:S(2)}) collective-permute-start(bf16[64,4096]{1,0:T(8,128)(2,1)} %get-tuple-element.86), channel_id=1, source_target_pairs={{0,1},{1,2},{2,3},{3,4},{4,5},{5,6},{6,7},{7,0},{8,9},{9,10},{10,1... | collective-permute-start | bytes 1572872 | tf_op jit(solution)/shard_map/ppermute | solution.py:108
  338.9 48.0 %copy-start.5 = (bf16[64,4096]{1,0:T(8,128)(2,1)S(1)}, bf16[64,4096]{1,0:T(8,128)(2,1)}, u32[]{:S(2)}) copy-start(bf16[64,4096]{1,0:T(8,128)(2,1)} %get-tuple-element.57) | copy-start | bytes 1572868
  356.0 30.9 %collective-permute-start.1 = (bf16[64,4096]{1,0:T(8,128)(2,1)}, bf16[64,4096]{1,0:T(8,128)(2,1)S(1)}, u32[]{:S(2)}, u32[]{:S(2)}) collective-permute-start(bf16[64,4096]{1,0:T(8,128)(2,1)} %get-tuple-element.85), channel_id=1, source_target_pairs={{0,2},{1,3},{2,4},{3,5},{4,6},{5,7},{6,0},{7,1},{8,10},{9,11},{10,... | collective-permute-start | bytes 1572872 | tf_op jit(solution)/shard_map/ppermute | solution.py:108
  386.8 35.8 %collective-permute-start.3 = (bf16[64,4096]{1,0:T(8,128)(2,1)S(1)}, bf16[64,4096]{1,0:T(8,128)(2,1)S(1)}, u32[]{:S(2)}, u32[]{:S(2)}) collective-permute-start(bf16[64,4096]{1,0:T(8,128)(2,1)S(1)} %copy-done.5), channel_id=1, source_target_pairs={{0,4},{1,5},{2,6},{3,7},{4,0},{5,1},{6,2},{7,3},{8,12},{9,13},{10,... | collective-permute-start | bytes 1572872 | tf_op jit(solution)/shard_map/ppermute | solution.py:108
  422.7 7.4 %copy-start.1 = (bf16[128,4096]{1,0:T(8,128)(2,1)S(1)}, bf16[128,4096]{1,0:T(8,128)(2,1)}, u32[]{:S(2)}) copy-start(bf16[128,4096]{1,0:T(8,128)(2,1)} %param.9) | copy-start | bytes 3145732
Sparse Core Ops, SparseCore 0:
  234.4 119.6 reduce-scatter.2
  357.6 70.1 reduce-scatter.4
